TPU v7x, 512 devices: a whole 4x8x8 slice. The times are simulated.
512 devices in a mesh: dom: 64 (over z, y), feat: 8 (over x, core).
Axes of the slice: x: 4, y: 8, z: 8, core: 2. Of those that a mesh axis runs over, the one named last changes fastest.
Arguments:
- features: bfloat16 [32768, 1024], P('dom', 'feat'), may hold values from -6 to 6
- degree: int32 [32768], P('dom'), may hold values from 4 to 39
- hub_ids: int32 [128], P('dom'), may hold values from 0 to 511
- hub_adjacency: bfloat16 [32768, 128], P('dom'), may hold values from 0 to 1
- local_rows: int32 [512], P('dom'), may hold values from 0 to 3
- local_cols: int32 [512], P('dom'), may hold values from 0 to 3
- local_tiles: bfloat16 [512, 128, 128], P('dom'), may hold values from 0 to 1
- out_dest: int32 [4096, 1], P('dom'), may hold values from 0 to 63; in each aligned block of 64 rows (0 to 63, 64 to 127, ...) at most 2 rows name the same one
- out_src: int32 [4096], P('dom'), may hold values from 0 to 3
- out_tiles: bfloat16 [4096, 128, 128], P('dom'), may hold values from 0 to 1
- recv_target: int32 [64, 64, 2], P('dom'), may hold values from 0 to 3
- w_self: bfloat16 [2, 1024, 1024], P(None, None, 'feat'), may hold values from -0.1875 to 0.1875
- w_neigh: bfloat16 [2, 1024, 1024], P(None, None, 'feat'), may hold values from -0.1875 to 0.1875
- gains: bfloat16 [2, 1024], P(None, 'feat'), may hold values from 0.099609375 to 1.8984375
Outputs:
- embeddings: bfloat16 [32768, 1024], P('dom', 'feat')
Inputs may be any that keep to these rules, and one draw needn't show every extreme that they name: `hub_ids`: hub j is owned by partition j // 2; its entry is its row within that partition's range. `out_dest`: among the 64 tiles of one partition no reader is named more than 2 times; some reader is named exactly 2 times. recv_target[q, s, c] is the row block of q that the c-th tile sent by s to q lands on; entries past the number of tiles s sends to q are unused.
All inputs are finite; a program needn't handle non-finite values.
Results may differ from a plain program's by a relative error of at most 0.0037.
The roundings to bfloat16 on the way count: a program that leaves them out, or rounds other values in their place, can miss the bound.
Values may be sent and summed in bfloat16 or wider, within the bound.
No kernel may reach another device: no remote copies, remote signals or barrier semaphores. Data moves between devices by JAX's collectives and lax.ppermute only.
A program may use at most 64 MiB of HBM per device.

v0:
```python
import jax
import jax.numpy as jnp
from jax import lax
from jax.sharding import PartitionSpec as P

EPSILON = 1e-06


def aggregate(
    inputs,
    degree,
    hub_ids,
    hub_adjacency,
    local_rows,
    local_cols,
    local_tiles,
    out_dest,
    out_src,
    out_tiles,
    recv_target,
):
    vertex_count, col_count = inputs.shape
    tile_side = local_tiles.shape[1]
    block_count = vertex_count // tile_side
    node_count = lax.axis_size("dom")
    capacity = recv_target.shape[2]
    blocks = inputs.reshape(block_count, tile_side, col_count)
    block_ids = jnp.arange(block_count, dtype=jnp.int32)
    partials = jnp.einsum(
        "trs,tsd->trd", out_tiles, blocks[out_src], preferred_element_type=jnp.float32
    ).astype(jnp.bfloat16)
    destination = out_dest[:, 0]
    positions = jnp.arange(destination.shape[0], dtype=jnp.int32)
    matches = (destination[None, :] == destination[:, None]) & (
        positions[None, :] < positions[:, None]
    )
    slot_rank = jnp.sum(matches.astype(jnp.int32), axis=1)
    slots = destination * capacity + slot_rank
    outgoing = (
        jnp.zeros((node_count * capacity, tile_side, col_count), jnp.bfloat16)
        .at[slots]
        .set(partials)
    )
    arrived = lax.all_to_all(
        outgoing.reshape(node_count, capacity, tile_side, col_count),
        "dom",
        split_axis=0,
        concat_axis=0,
        tiled=True,
    )
    targets = recv_target[0].reshape(-1)
    landing = (targets[None, :] == block_ids[:, None]).astype(jnp.bfloat16)
    from_peers = jnp.einsum(
        "bk,krd->brd",
        landing,
        arrived.reshape(node_count * capacity, tile_side, col_count),
        preferred_element_type=jnp.float32,
    )
    local_products = jnp.einsum(
        "trs,tsd->trd", local_tiles, blocks[local_cols], preferred_element_type=jnp.float32
    )
    onehot = (local_rows[None, :] == block_ids[:, None]).astype(jnp.float32)
    from_local = jnp.einsum("bt,trd->brd", onehot, local_products, precision=lax.Precision.HIGHEST)
    hub_local = inputs[hub_ids]
    from_hubs = jnp.dot(
        hub_adjacency,
        lax.all_gather(hub_local, "dom", axis=0, tiled=True),
        preferred_element_type=jnp.float32,
    )
    summed = (from_peers + from_local).reshape(vertex_count, col_count) + from_hubs
    return (summed / degree.astype(jnp.float32)[:, None]).astype(jnp.bfloat16)


def per_device(
    features,
    degree,
    hub_ids,
    hub_adjacency,
    local_rows,
    local_cols,
    local_tiles,
    out_dest,
    out_src,
    out_tiles,
    recv_target,
    w_self,
    w_neigh,
    gains,
):
    width = w_self.shape[1]
    current = features
    for layer_idx in range(w_self.shape[0]):
        neighbours = aggregate(
            current,
            degree,
            hub_ids,
            hub_adjacency,
            local_rows,
            local_cols,
            local_tiles,
            out_dest,
            out_src,
            out_tiles,
            recv_target,
        )
        self_weight = w_self[layer_idx]
        neigh_weight = w_neigh[layer_idx]
        gain_row = gains[layer_idx][None, :]
        own_part = lax.all_gather(current, "feat", axis=1, tiled=True)
        neigh_part = lax.all_gather(neighbours, "feat", axis=1, tiled=True)
        running = jnp.dot(own_part, self_weight, preferred_element_type=jnp.float32)
        mixed = running + jnp.dot(neigh_part, neigh_weight, preferred_element_type=jnp.float32)
        rectified = jnp.maximum(mixed, 0.0)
        squares = lax.psum(jnp.sum(rectified * rectified, axis=1), "feat")
        scaled = (
            gain_row.astype(jnp.float32) * rectified * lax.rsqrt(squares[:, None] / width + EPSILON)
        )
        current = scaled.astype(jnp.bfloat16)
    return current


def solution(mesh):
    in_specs = (
        P("dom", "feat"),
        P("dom"),
        P("dom"),
        P("dom", None),
        P("dom"),
        P("dom"),
        P("dom", None, None),
        P("dom", None),
        P("dom"),
        P("dom", None, None),
        P("dom", None, None),
        P(None, None, "feat"),
        P(None, None, "feat"),
        P(None, "feat"),
    )
    out_specs = P("dom", "feat")
    return jax.shard_map(
        per_device, mesh=mesh, in_specs=in_specs, out_specs=out_specs, check_vma=False
    )
```

profile of v0, /device:TPU:1, one launch (start us, length us, event | category | flops | bytes accessed | tf_op | source)
XLA Modules:
  0.0 541.2 jit_solution(90209324262302581)
XLA Ops:
  6.5 0.8 compare_select_fusion.2
  7.4 3.1 gather_fusion
  10.4 4.5 convert_bitcast_fusion.1
  14.9 4.1 copy.54
  19.0 0.2 convert_reduce_fusion
  19.2 3.0 broadcast.51.clone
  22.2 10.0 %scatter_fusion = bf16[128,128,128]{2,1,0:T(8,128)(2,1)} fusion(bf16[128,128,128]{2,1,0:T(8,128)(2,1)} %broadcast.51.clone, s32[64]{0:T(128)S(1)} %fusion.31, bf16[64,128,128]{2,1,0:T(8,128)(2,1)} %copy.54), kind=kCustom, calls=%fused_computation.6 | custom fusion | bytes 6291712 | tf_op jit(solution)/shard_map/scatter | solution.py:42
  32.2 8.5 %copy.55 = bf16[64,2,128,128]{3,1,2,0:T(2,128)(2,1)} copy(bf16[64,2,128,128]{3,2,1,0:T(8,128)(2,1)} %bitcast.98) | data formatting | bytes 8388608 | tf_op jit(solution)/shard_map/reshape | solution.py:45
  40.7 17.5 %all-to-all-start = ((bf16[64,2,128,128]{3,1,2,0:T(2,128)(2,1)}), bf16[64,2,128,128]{3,1,2,0:T(2,128)(2,1)}, u32[]{:S(2)}, u32[]{:S(2)}) async-start(bf16[64,2,128,128]{3,1,2,0:T(2,128)(2,1)} %copy.55), calls=%async_computation | async-start | bytes 8388608 | tf_op jit(solution)/shard_map/all_to_all | solution.py:44
  58.2 0.0 copy-start.11
  58.3 0.0 copy-start.14
  58.3 0.0 copy-start.8
  58.3 0.0 copy-start.10
  58.3 0.0 all-gather.9.cloned.1.call-start
  58.3 0.7 all-gather.9.cloned.1.call-update
  59.0 0.0 all-gather.11.cloned.1.call-start
  59.1 0.6 gather_fusion.1
  59.7 0.3 convolution_bitcast_fusion.1
  60.1 0.2 copy.58
  60.3 0.1 copy.52
  60.4 0.1 eq.22
  60.6 0.6 gather_fusion.2
  61.2 148.9 %all-gather.2 = bf16[64,2,128]{2,1,0:T(2,128)(2,1)S(1)} all-gather(bf16[1,2,128]{2,1,0:T(2,128)(2,1)S(1)} %bitcast.106), channel_id=2, replica_groups=mesh['dom'=64,'feat'=8] {'dom'}, dimensions={0}, use_global_device_ids=true | all-gather | bytes 33280 | tf_op jit(solution)/shard_map/all_gather | solution.py:67
  210.1 0.4 fusion.23
  210.5 0.0 all-to-all-done
  210.5 6.9 %copy.56 = bf16[64,2,128,128]{3,1,0,2:T(2,128)(2,1)S(1)} copy(bf16[64,2,128,128]{3,1,2,0:T(2,128)(2,1)} %all-to-all-done) | data formatting | bytes 8388608 | tf_op jit(solution)/shard_map/all_to_all | solution.py:44
  217.4 0.7 convolution_add_fusion.1
  218.1 0.1 copy.60
  218.2 1.8 fusion.6
  220.1 0.0 all-gather.11.cloned.1.call-update
  220.1 0.0 all-gather.9.cloned.1.call-done
  220.1 1.7 fusion.12
  221.8 33.2 %all-gather.11.cloned.1.call-done = bf16[512,1024]{0,1:T(8,128)(2,1)} async-done(((bf16[512,128]{0,1:T(8,128)(2,1)}), bf16[512,1024]{0,1:T(8,128)(2,1)}) %all-gather.11.cloned.1.call-update) | async-done | bytes 1048592 | tf_op jit(solution)/shard_map/all_gather | solution.py:110
  255.0 1.8 multiply_reduce_fusion.1
  256.8 12.0 %psum.14 = f32[512]{0:T(512)S(1)} all-reduce(f32[512]{0:T(512)S(1)} %get-tuple-element.7), channel_id=1, replica_groups=mesh['dom'=64,'feat'=8] {'feat'}, use_global_device_ids=true, to_apply=%region_3.0 | all-reduce | flops 512 | bytes 4096 | tf_op jit(solution)/shard_map/psum | solution.py:114
  268.8 0.1 multiply_convert_fusion.1
  269.0 0.0 copy-start.1
  269.0 2.1 gather_fusion.3
  271.2 4.5 convert_bitcast_fusion
  275.7 4.1 copy.62
  279.8 3.0 broadcast.51
  282.8 10.0 %scatter_fusion.1 = bf16[128,128,128]{2,1,0:T(8,128)(2,1)} fusion(bf16[128,128,128]{2,1,0:T(8,128)(2,1)} %broadcast.51, s32[64]{0:T(128)S(1)} %fusion.31, bf16[64,128,128]{2,1,0:T(8,128)(2,1)} %copy.62), kind=kCustom, calls=%fused_computation.7 | custom fusion | bytes 6291712 | tf_op jit(solution)/shard_map/scatter | solution.py:42
  292.7 8.5 %copy.63 = bf16[64,2,128,128]{3,1,2,0:T(2,128)(2,1)} copy(bf16[64,2,128,128]{3,2,1,0:T(8,128)(2,1)} %bitcast.97) | data formatting | bytes 8388608 | tf_op jit(solution)/shard_map/reshape | solution.py:45
  301.2 13.2 %all-to-all-start.1 = ((bf16[64,2,128,128]{3,1,2,0:T(2,128)(2,1)}), bf16[64,2,128,128]{3,1,2,0:T(2,128)(2,1)}, u32[]{:S(2)}, u32[]{:S(2)}) async-start(bf16[64,2,128,128]{3,1,2,0:T(2,128)(2,1)} %copy.63), calls=%async_computation.1 | async-start | bytes 8388608 | tf_op jit(solution)/shard_map/all_to_all | solution.py:44
  314.4 0.0 all-gather.13.cloned.1.call-start
  314.5 0.7 all-gather.13.cloned.1.call-update
  315.2 0.0 all-gather.15.cloned.1.call-start
  315.2 0.6 gather_fusion.4
  315.8 0.6 gather_fusion.5
  316.4 0.3 convolution_bitcast_fusion
  316.7 0.2 copy.66
  317.0 154.6 %all-gather.3 = bf16[64,2,128]{2,1,0:T(2,128)(2,1)S(1)} all-gather(bf16[1,2,128]{2,1,0:T(2,128)(2,1)S(1)} %bitcast.105), channel_id=3, replica_groups=mesh['dom'=64,'feat'=8] {'dom'}, dimensions={0}, use_global_device_ids=true | all-gather | bytes 33280 | tf_op jit(solution)/shard_map/all_gather | solution.py:67
  471.6 0.4 fusion.21
  472.0 6.9 %copy.64 = bf16[64,2,128,128]{3,1,0,2:T(2,128)(2,1)S(1)} copy(bf16[64,2,128,128]{3,1,2,0:T(2,128)(2,1)} %all-to-all-done.1) | data formatting | bytes 8388608 | tf_op jit(solution)/shard_map/all_to_all | solution.py:44
  478.9 0.7 convolution_add_fusion
  479.6 0.1 copy.68
  479.7 1.8 fusion.7
  481.5 0.0 all-gather.15.cloned.1.call-update
  481.5 0.0 all-gather.13.cloned.1.call-done
  481.6 1.7 fusion.9
  483.2 36.8 %all-gather.15.cloned.1.call-done = bf16[512,1024]{0,1:T(8,128)(2,1)} async-done(((bf16[512,128]{0,1:T(8,128)(2,1)}), bf16[512,1024]{0,1:T(8,128)(2,1)}) %all-gather.15.cloned.1.call-update) | async-done | bytes 1048592 | tf_op jit(solution)/shard_map/all_gather | solution.py:110
  520.0 1.8 multiply_reduce_fusion
  521.9 12.0 %psum.15 = f32[512]{0:T(512)S(1)} all-reduce(f32[512]{0:T(512)S(1)} %get-tuple-element.9), channel_id=1, replica_groups=mesh['dom'=64,'feat'=8] {'feat'}, use_global_device_ids=true, to_apply=%region_6.0 | all-reduce | flops 512 | bytes 4096 | tf_op jit(solution)/shard_map/psum | solution.py:114
  533.9 0.8 multiply_convert_fusion
  (38 shorter events, 0.2 us)
Async XLA Ops:
  6.5 3.9 copy-start
  14.9 4.1 copy-start.12
  40.7 18.4 %copy-start.13 = (s32[8]{0:T(128)S(1)}, s32[8]{0:T(128)}, u32[]{:S(2)}) copy-start(s32[8]{0:T(128)} %param.19) | copy-start | bytes 100
  40.7 18.4 %copy-start.3 = (bf16[512,128]{1,0:T(8,128)(2,1)S(1)}, bf16[512,128]{1,0:T(8,128)(2,1)}, u32[]{:S(2)}) copy-start(bf16[512,128]{1,0:T(8,128)(2,1)} %param.14) | copy-start | bytes 393220
  40.7 19.0 %copy-start.4 = (bf16[8,128,128]{2,1,0:T(8,128)(2,1)S(1)}, bf16[8,128,128]{2,1,0:T(8,128)(2,1)}, u32[]{:S(2)}) copy-start(bf16[8,128,128]{2,1,0:T(8,128)(2,1)} %param.20) | copy-start | bytes 786436
  40.7 169.8 %all-to-all-start = ((bf16[64,2,128,128]{3,1,2,0:T(2,128)(2,1)}), bf16[64,2,128,128]{3,1,2,0:T(2,128)(2,1)}, u32[]{:S(2)}, u32[]{:S(2)}) async-start(bf16[64,2,128,128]{3,1,2,0:T(2,128)(2,1)} %copy.55), calls=%async_computation | async-start | bytes 8388608 | tf_op jit(solution)/shard_map/all_to_all | solution.py:44
  58.2 2.1 copy-start.11
  58.3 2.3 copy-start.14
  58.3 2.9 copy-start.8
  58.3 151.8 %copy-start.10 = (s32[8]{0:T(128)S(1)}, s32[8]{0:T(128)}, u32[]{:S(2)}) copy-start(s32[8]{0:T(128)} %param.18) | copy-start | bytes 100
  58.3 161.8 %all-gather.9.cloned.1.call-start = ((), (), s32[]{:S(2)}) async-start(), calls=%async_computation.2 | async-start | bytes 1179648 | tf_op jit(solution)/shard_map/all_gather | solution.py:109
  59.0 196.0 %all-gather.11.cloned.1.call-start = ((), (), s32[]{:S(2)}) async-start(), calls=%async_computation.3 | async-start | bytes 1179648 | tf_op jit(solution)/shard_map/all_gather | solution.py:110
  218.1 2.0 copy-start.9
  218.1 2.1 copy-start.6
  269.0 2.2 copy-start.1
  301.2 14.0 %copy-start.2 = (bf16[512,128]{1,0:T(8,128)(2,1)S(1)}, bf16[512,128]{1,0:T(8,128)(2,1)}, u32[]{:S(2)}) copy-start(bf16[512,128]{1,0:T(8,128)(2,1)} %copy-done.1) | copy-start | bytes 393220
  301.2 15.2 %copy-start.5 = (bf16[8,128,128]{2,1,0:T(8,128)(2,1)S(1)}, bf16[8,128,128]{2,1,0:T(8,128)(2,1)}, u32[]{:S(2)}) copy-start(bf16[8,128,128]{2,1,0:T(8,128)(2,1)} %param.20) | copy-start | bytes 786436
  301.2 170.8 %all-to-all-start.1 = ((bf16[64,2,128,128]{3,1,2,0:T(2,128)(2,1)}), bf16[64,2,128,128]{3,1,2,0:T(2,128)(2,1)}, u32[]{:S(2)}, u32[]{:S(2)}) async-start(bf16[64,2,128,128]{3,1,2,0:T(2,128)(2,1)} %copy.63), calls=%async_computation.1 | async-start | bytes 8388608 | tf_op jit(solution)/shard_map/all_to_all | solution.py:44
  314.4 167.1 %all-gather.13.cloned.1.call-start = ((), (), s32[]{:S(2)}) async-start(), calls=%async_computation.4 | async-start | bytes 1179648 | tf_op jit(solution)/shard_map/all_gather | solution.py:109
  315.2 204.9 %all-gather.15.cloned.1.call-start = ((), (), s32[]{:S(2)}) async-start(), calls=%async_computation.5 | async-start | bytes 1179648 | tf_op jit(solution)/shard_map/all_gather | solution.py:110
  479.6 2.0 copy-start.7
Sparse Core Ops, SparseCore 0:
  61.2 30.0 all-gather.8
  220.2 34.7 all-gather.10
  317.4 28.4 all-gather.12
  481.7 38.3 all-gather.14
where the time goes:
time: 542 us; the launch traced here: 541 us
  blocking collectives  328 us (61%)
  local copies, waits for them, and re-layouts  73.5 us (14%)
  waiting for transfers between devices  71.4 us (13%)
  starting transfers between devices  30.9 us (6%)
  matrix products  22.3 us (4%)
  between operations  13.5 us (2%)
    all_gather x2, blocking collectives, aggregate(): lax.all_gather(hub_local, 'dom', axis=0, tiled=True)  304 us
    all_gather x2, waiting for transfers between devices, per_device(): neigh_part = lax.all_gather(neighbours, 'feat', axis=1, tiled=True)  70 us
    all_to_all x2, starting transfers between devices, aggregate(): lax.all_to_all(outgoing.reshape(node_count, capacity, tile_side, col_coun...  30.7 us
    psum x2, blocking collectives, per_device(): squares = lax.psum(jnp.sum(rectified * rectified, axis=1), 'feat')  24 us
    scatter x2, local copies, waits for them, and re-layouts, aggregate(): outgoing = jnp.zeros((node_count * capacity, tile_side, col_count), jnp.b...  19.9 us
    reshape x2, local copies, waits for them, and re-layouts, aggregate(): outgoing.reshape(node_count, capacity, tile_side, col_count)  17 us
    all_to_all x2, local copies, waits for them, and re-layouts, aggregate(): lax.all_to_all(outgoing.reshape(node_count, capacity, tile_side, col_coun...  13.8 us
  transfers between devices with their start and end apart: 6, of which 2 were waited for; matrix products, arithmetic and copies ran while one was open for 5% of the time, Pallas kernels for 0%

commit v1 on v0

--- a/solution.py
+++ b/solution.py
@@ -4,6 +4,24 @@
 from jax.sharding import PartitionSpec as P
 
 EPSILON = 1e-06
+HUB_PAD = 16
+
+
+def routing(out_dest, recv_target, block_count, node_count):
+    capacity = recv_target.shape[2]
+    destination = out_dest[:, 0]
+    positions = jnp.arange(destination.shape[0], dtype=jnp.int32)
+    matches = (destination[None, :] == destination[:, None]) & (
+        positions[None, :] < positions[:, None]
+    )
+    slot_rank = jnp.sum(matches.astype(jnp.int32), axis=1)
+    slots = destination * capacity + slot_rank
+    slot_ids = jnp.arange(node_count * capacity, dtype=jnp.int32)
+    placing = (slot_ids[:, None] == slots[None, :]).astype(jnp.bfloat16)
+    targets = recv_target[0].reshape(-1)
+    block_ids = jnp.arange(block_count, dtype=jnp.int32)
+    landing = (targets[None, :] == block_ids[:, None]).astype(jnp.bfloat16)
+    return placing, landing
 
 
 def aggregate(
@@ -14,59 +32,49 @@
     local_rows,
     local_cols,
     local_tiles,
-    out_dest,
     out_src,
     out_tiles,
-    recv_target,
+    placing,
+    landing,
 ):
     vertex_count, col_count = inputs.shape
     tile_side = local_tiles.shape[1]
     block_count = vertex_count // tile_side
     node_count = lax.axis_size("dom")
-    capacity = recv_target.shape[2]
+    slot_count = placing.shape[0]
+    capacity = slot_count // node_count
+    hub_count = hub_ids.shape[0]
     blocks = inputs.reshape(block_count, tile_side, col_count)
     block_ids = jnp.arange(block_count, dtype=jnp.int32)
     partials = jnp.einsum(
         "trs,tsd->trd", out_tiles, blocks[out_src], preferred_element_type=jnp.float32
     ).astype(jnp.bfloat16)
-    destination = out_dest[:, 0]
-    positions = jnp.arange(destination.shape[0], dtype=jnp.int32)
-    matches = (destination[None, :] == destination[:, None]) & (
-        positions[None, :] < positions[:, None]
+    outgoing = jnp.einsum(
+        "kt,trd->krd", placing, partials, preferred_element_type=jnp.float32
+    ).astype(jnp.bfloat16)
+    hub_local = inputs[hub_ids]
+    hub_block = jnp.zeros((HUB_PAD, col_count), jnp.bfloat16).at[:hub_count].set(hub_local)
+    payload = jnp.concatenate(
+        [
+            outgoing.reshape(node_count, capacity * tile_side, col_count),
+            jnp.broadcast_to(hub_block[None], (node_count, HUB_PAD, col_count)),
+        ],
+        axis=1,
     )
-    slot_rank = jnp.sum(matches.astype(jnp.int32), axis=1)
-    slots = destination * capacity + slot_rank
-    outgoing = (
-        jnp.zeros((node_count * capacity, tile_side, col_count), jnp.bfloat16)
-        .at[slots]
-        .set(partials)
+    arrived = lax.all_to_all(payload, "dom", split_axis=0, concat_axis=0, tiled=True)
+    tiles_in = arrived[:, : capacity * tile_side, :].reshape(slot_count, tile_side, col_count)
+    hub_rows = arrived[:, capacity * tile_side : capacity * tile_side + hub_count, :].reshape(
+        node_count * hub_count, col_count
     )
-    arrived = lax.all_to_all(
-        outgoing.reshape(node_count, capacity, tile_side, col_count),
-        "dom",
-        split_axis=0,
-        concat_axis=0,
-        tiled=True,
-    )
-    targets = recv_target[0].reshape(-1)
-    landing = (targets[None, :] == block_ids[:, None]).astype(jnp.bfloat16)
     from_peers = jnp.einsum(
-        "bk,krd->brd",
-        landing,
-        arrived.reshape(node_count * capacity, tile_side, col_count),
-        preferred_element_type=jnp.float32,
+        "bk,krd->brd", landing, tiles_in, preferred_element_type=jnp.float32
     )
     local_products = jnp.einsum(
         "trs,tsd->trd", local_tiles, blocks[local_cols], preferred_element_type=jnp.float32
     )
     onehot = (local_rows[None, :] == block_ids[:, None]).astype(jnp.float32)
     from_local = jnp.einsum("bt,trd->brd", onehot, local_products, precision=lax.Precision.HIGHEST)
-    hub_local = inputs[hub_ids]
-    from_hubs = jnp.dot(
-        hub_adjacency,
-        lax.all_gather(hub_local, "dom", axis=0, tiled=True),
-        preferred_element_type=jnp.float32,
-    )
+    from_hubs = jnp.dot(hub_adjacency, hub_rows, preferred_element_type=jnp.float32)
     summed = (from_peers + from_local).reshape(vertex_count, col_count) + from_hubs
     return (summed / degree.astype(jnp.float32)[:, None]).astype(jnp.bfloat16)
 
@@ -88,6 +96,10 @@
     gains,
 ):
     width = w_self.shape[1]
+    tile_side = local_tiles.shape[1]
+    placing, landing = routing(
+        out_dest, recv_target, features.shape[0] // tile_side, lax.axis_size("dom")
+    )
     current = features
     for layer_idx in range(w_self.shape[0]):
         neighbours = aggregate(
@@ -98,10 +110,10 @@
             local_rows,
             local_cols,
             local_tiles,
-            out_dest,
             out_src,
             out_tiles,
-            recv_target,
+            placing,
+            landing,
         )
         self_weight = w_self[layer_idx]
         neigh_weight = w_neigh[layer_idx]

time: 542 us -> 472 us (0.87)
  blocking collectives: 328 us -> 24 us
  waiting for transfers between devices: 71.4 us -> 338 us
  local copies, waits for them, and re-layouts: 73.5 us -> 29.2 us
  matrix products: 22.3 us -> 28.2 us
  other arithmetic: 1.98 us -> 7.49 us
    all_gather x2 -> x0, blocking collectives: 304 us -> none  [aggregate(): lax.all_gather(hub_local, 'dom', axis=0, tiled=True)]
    all_to_all x2, waiting for transfers between devices: 0.01 us -> 213 us  [aggregate(): lax.all_to_all(payload, 'dom', split_axis=0, concat_axis=0, tiled=True)]
    all_gather x2, waiting for transfers between devices: 70 us -> 123 us  [per_device(): neigh_part = lax.all_gather(neighbours, 'feat', axis=1, tiled=True)]
    scatter x2, local copies, waits for them, and re-layouts: 19.9 us -> 0.01 us  [aggregate(): jnp.zeros((HUB_PAD, col_count), jnp.bfloat16).at[:hub_count].set(hub_local)]
    reshape x2 -> x0, local copies, waits for them, and re-layouts: 17 us -> none  [aggregate(): outgoing.reshape(node_count, capacity, tile_side, col_count)]
    all_to_all x2 -> x0, local copies, waits for them, and re-layouts: 13.8 us -> none  [aggregate(): lax.all_to_all(outgoing.reshape(node_count, capacity, tile_side, col_coun...]
    slice x0 -> x4, local copies, waits for them, and re-layouts: none -> 6.77 us  [the longest x2 4.92 us: aggregate(): arrived[:, :capacity * tile_side, :]]
    another operation x2 -> x0, local copies, waits for them, and re-layouts: 6.03 us -> none
  transfers between devices with their start and end apart: 6 -> 6, of which waited for: 2 -> 4; matrix products, arithmetic and copies ran while one was open for 5% -> 4% of each run, Pallas kernels for 0% -> 0%
where the time goes in v1:
time: 472 us; the launch traced here: 471 us
  waiting for transfers between devices  338 us (72%)
  starting transfers between devices  31.1 us (7%)
  local copies, waits for them, and re-layouts  29.2 us (6%)
  matrix products  28.2 us (6%)
  blocking collectives  24 us (5%)
  between operations  13.5 us (3%)
  other arithmetic  7.49 us (2%)
    all_to_all x2, waiting for transfers between devices, aggregate(): lax.all_to_all(payload, 'dom', split_axis=0, concat_axis=0, tiled=True)  213 us
    all_gather x2, waiting for transfers between devices, per_device(): neigh_part = lax.all_gather(neighbours, 'feat', axis=1, tiled=True)  123 us
    all_to_all x2, starting transfers between devices, aggregate(): lax.all_to_all(payload, 'dom', split_axis=0, concat_axis=0, tiled=True)  30.7 us
    psum x2, blocking collectives, per_device(): squares = lax.psum(jnp.sum(rectified * rectified, axis=1), 'feat')  24 us
  transfers between devices with their start and end apart: 6, of which 4 were waited for; matrix products, arithmetic and copies ran while one was open for 4% of the time, Pallas kernels for 0%

profile of v1, /device:TPU:1, one launch (start us, length us, event | category | flops | bytes accessed | tf_op | source)
XLA Modules:
  0.0 471.2 jit_solution(1605894640688960011)
XLA Ops:
  6.5 0.8 compare_select_fusion.1
  7.4 0.7 compare_select_fusion.2
  8.0 1.5 gather_fusion.1
  9.5 3.0 gather_fusion
  12.5 4.6 convert_bitcast_fusion.1
  17.1 4.1 copy.44
  21.2 0.2 convert_reduce_fusion
  21.4 3.0 convolution_convert_fusion.1
  24.4 2.7 copy.45
  27.1 2.4 pad_maximum_fusion
  29.6 0.0 copy-start.9
  29.6 17.5 %all-to-all-start = ((bf16[64,272,128]{2,1,0:T(8,128)(2,1)}), bf16[64,272,128]{2,1,0:T(8,128)(2,1)}, u32[]{:S(2)}, u32[]{:S(2)}) async-start(bf16[64,272,128]{2,1,0:T(8,128)(2,1)} %pad_maximum_fusion), calls=%async_computation | async-start | bytes 8912896 | tf_op jit(solution)/shard_map/all_to_all | solution.py:64
  47.1 0.0 all-gather.5.cloned.1.call-start
  47.2 0.7 all-gather.5.cloned.1.call-update
  47.9 0.2 all-gather.7.cloned.1.call-start
  48.1 0.6 gather_fusion.2
  48.7 0.3 convolution_bitcast_fusion.1
  49.1 0.2 copy.48
  49.3 0.1 copy.42
  49.4 0.1 eq.26
  49.6 0.4 fusion.38
  50.0 110.1 %all-to-all-done = bf16[64,272,128]{2,1,0:T(8,128)(2,1)} async-done(((bf16[64,272,128]{2,1,0:T(8,128)(2,1)}), bf16[64,272,128]{2,1,0:T(8,128)(2,1)}, u32[]{:S(2)}, u32[]{:S(2)}) %all-to-all-start) | async-done | bytes 4456480 | tf_op jit(solution)/shard_map/all_to_all | solution.py:64
  160.1 2.5 slice.84
  162.6 0.0 copy-start.8
  162.6 2.3 fusion.4
  165.0 0.1 copy.50
  165.1 0.9 slice.85
  166.0 0.9 fusion.16
  166.9 0.0 all-gather.7.cloned.1.call-update
  166.9 0.0 all-gather.5.cloned.1.call-done
  167.0 1.7 fusion.22
  168.7 53.7 %all-gather.7.cloned.1.call-done = bf16[512,1024]{0,1:T(8,128)(2,1)} async-done(((bf16[512,128]{0,1:T(8,128)(2,1)}), bf16[512,1024]{0,1:T(8,128)(2,1)}) %all-gather.7.cloned.1.call-update) | async-done | bytes 1048592 | tf_op jit(solution)/shard_map/all_gather | solution.py:122
  222.4 1.8 multiply_reduce_fusion.1
  224.2 12.0 %psum.14 = f32[512]{0:T(512)S(1)} all-reduce(f32[512]{0:T(512)S(1)} %get-tuple-element.31), channel_id=1, replica_groups=mesh['dom'=64,'feat'=8] {'feat'}, use_global_device_ids=true, to_apply=%region_2.0 | all-reduce | flops 512 | bytes 4096 | tf_op jit(solution)/shard_map/psum | solution.py:126
  236.2 0.1 multiply_convert_fusion.1
  236.4 0.0 copy-start.2
  236.4 0.6 gather_fusion.4
  237.0 2.2 gather_fusion.3
  239.1 4.5 convert_bitcast_fusion
  243.6 3.3 copy.52
  246.9 1.4 convolution_convert_fusion
  248.3 2.7 copy.53
  251.0 2.4 pad_maximum_fusion.1
  253.5 13.2 %all-to-all-start.1 = ((bf16[64,272,128]{2,1,0:T(8,128)(2,1)}), bf16[64,272,128]{2,1,0:T(8,128)(2,1)}, u32[]{:S(2)}, u32[]{:S(2)}) async-start(bf16[64,272,128]{2,1,0:T(8,128)(2,1)} %pad_maximum_fusion.1), calls=%async_computation.1 | async-start | bytes 8912896 | tf_op jit(solution)/shard_map/all_to_all | solution.py:64
  266.7 0.0 all-gather.9.cloned.1.call-start
  266.7 0.7 all-gather.9.cloned.1.call-update
  267.4 0.0 all-gather.11.cloned.1.call-start
  267.5 0.6 gather_fusion.5
  268.1 0.3 convolution_bitcast_fusion
  268.4 0.2 copy.56
  268.7 0.4 fusion.36
  269.0 103.2 %all-to-all-done.1 = bf16[64,272,128]{2,1,0:T(8,128)(2,1)} async-done(((bf16[64,272,128]{2,1,0:T(8,128)(2,1)}), bf16[64,272,128]{2,1,0:T(8,128)(2,1)}, u32[]{:S(2)}, u32[]{:S(2)}) %all-to-all-start.1) | async-done | bytes 4456480 | tf_op jit(solution)/shard_map/all_to_all | solution.py:64
  372.2 2.5 slice.86
  374.7 2.4 fusion.7
  377.1 0.1 copy.58
  377.3 0.9 slice.87
  378.2 0.9 fusion.17
  379.1 0.0 all-gather.11.cloned.1.call-update
  379.1 0.0 all-gather.9.cloned.1.call-done
  379.1 1.7 fusion.19
  380.8 69.2 %all-gather.11.cloned.1.call-done = bf16[512,1024]{0,1:T(8,128)(2,1)} async-done(((bf16[512,128]{0,1:T(8,128)(2,1)}), bf16[512,1024]{0,1:T(8,128)(2,1)}) %all-gather.11.cloned.1.call-update) | async-done | bytes 1048592 | tf_op jit(solution)/shard_map/all_gather | solution.py:122
  450.0 1.8 multiply_reduce_fusion
  451.8 12.0 %psum.15 = f32[512]{0:T(512)S(1)} all-reduce(f32[512]{0:T(512)S(1)} %get-tuple-element.33), channel_id=1, replica_groups=mesh['dom'=64,'feat'=8] {'feat'}, use_global_device_ids=true, to_apply=%region_4.0 | all-reduce | flops 512 | bytes 4096 | tf_op jit(solution)/shard_map/psum | solution.py:126
  463.9 0.8 multiply_convert_fusion
  (42 shorter events, 0.2 us)
Async XLA Ops:
  6.5 6.0 %copy-start = (bf16[64,128,128]{2,1,0:T(8,128)(2,1)S(1)}, bf16[64,128,128]{2,1,0:T(8,128)(2,1)}, u32[]{:S(2)}) copy-start(bf16[64,128,128]{2,1,0:T(8,128)(2,1)} %param.27) | copy-start | bytes 6291460
  12.5 8.7 %copy-start.13 = (s32[64,1]{0,1:T(1,128)S(1)}, s32[64,1]{0,1:T(1,128)}, u32[]{:S(2)}) copy-start(s32[64,1]{0,1:T(1,128)} %param.25) | copy-start | bytes 772
  29.6 18.5 %copy-start.14 = (s32[8]{0:T(128)S(1)}, s32[8]{0:T(128)}, u32[]{:S(2)}) copy-start(s32[8]{0:T(128)} %param.23) | copy-start | bytes 100
  29.6 18.6 %copy-start.4 = (bf16[512,128]{1,0:T(8,128)(2,1)S(1)}, bf16[512,128]{1,0:T(8,128)(2,1)}, u32[]{:S(2)}) copy-start(bf16[512,128]{1,0:T(8,128)(2,1)} %param.18) | copy-start | bytes 393220
  29.6 19.2 %copy-start.5 = (bf16[8,128,128]{2,1,0:T(8,128)(2,1)S(1)}, bf16[8,128,128]{2,1,0:T(8,128)(2,1)}, u32[]{:S(2)}) copy-start(bf16[8,128,128]{2,1,0:T(8,128)(2,1)} %param.24) | copy-start | bytes 786436
  29.6 19.8 %copy-start.10 = (s32[1,64,2]{1,2,0:T(2,128)S(1)}, s32[1,64,2]{1,2,0:T(2,128)}, u32[]{:S(2)}) copy-start(s32[1,64,2]{1,2,0:T(2,128)} %param.28) | copy-start | bytes 1540
  29.6 20.0 %copy-start.7 = (s32[512]{0:T(512)S(1)}, s32[512]{0:T(512)}, u32[]{:S(2)}) copy-start(s32[512]{0:T(512)} %param.19) | copy-start | bytes 6148
  29.6 20.0 %copy-start.9 = (s32[8]{0:T(128)S(1)}, s32[8]{0:T(128)}, u32[]{:S(2)}) copy-start(s32[8]{0:T(128)} %param.22) | copy-start | bytes 100
  29.6 130.5 %all-to-all-start = ((bf16[64,272,128]{2,1,0:T(8,128)(2,1)}), bf16[64,272,128]{2,1,0:T(8,128)(2,1)}, u32[]{:S(2)}, u32[]{:S(2)}) async-start(bf16[64,272,128]{2,1,0:T(8,128)(2,1)} %pad_maximum_fusion), calls=%async_computation | async-start | bytes 8912896 | tf_op jit(solution)/shard_map/all_to_all | solution.py:64
  47.1 119.8 %all-gather.5.cloned.1.call-start = ((), (), s32[]{:S(2)}) async-start(), calls=%async_computation.2 | async-start | bytes 1179648 | tf_op jit(solution)/shard_map/all_gather | solution.py:121
  47.9 174.5 %all-gather.7.cloned.1.call-start = ((), (), s32[]{:S(2)}) async-start(), calls=%async_computation.3 | async-start | bytes 1179648 | tf_op jit(solution)/shard_map/all_gather | solution.py:122
  162.6 3.5 copy-start.11
  162.6 4.3 copy-start.8
  236.4 7.3 %copy-start.2 = (bf16[512,128]{1,0:T(8,128)(2,1)}, bf16[512,128]{1,0:T(8,128)(2,1)S(1)}, u32[]{:S(2)}) copy-start(bf16[512,128]{1,0:T(8,128)(2,1)S(1)} %multiply_convert_fusion.1) | copy-start | bytes 393220
  253.5 14.0 %copy-start.3 = (bf16[512,128]{1,0:T(8,128)(2,1)S(1)}, bf16[512,128]{1,0:T(8,128)(2,1)}, u32[]{:S(2)}) copy-start(bf16[512,128]{1,0:T(8,128)(2,1)} %copy-done.2) | copy-start | bytes 393220
  253.5 118.8 %all-to-all-start.1 = ((bf16[64,272,128]{2,1,0:T(8,128)(2,1)}), bf16[64,272,128]{2,1,0:T(8,128)(2,1)}, u32[]{:S(2)}, u32[]{:S(2)}) async-start(bf16[64,272,128]{2,1,0:T(8,128)(2,1)} %pad_maximum_fusion.1), calls=%async_computation.1 | async-start | bytes 8912896 | tf_op jit(solution)/shard_map/all_to_all | solution.py:64
  266.7 112.4 %all-gather.9.cloned.1.call-start = ((), (), s32[]{:S(2)}) async-start(), calls=%async_computation.4 | async-start | bytes 1179648 | tf_op jit(solution)/shard_map/all_gather | solution.py:121
  267.4 182.6 %all-gather.11.cloned.1.call-start = ((), (), s32[]{:S(2)}) async-start(), calls=%async_computation.5 | async-start | bytes 1179648 | tf_op jit(solution)/shard_map/all_gather | solution.py:122
  374.7 3.5 copy-start.12
  374.7 4.4 copy-start.6
  374.7 89.9 %copy-start.1 = (bf16[64,128,128]{2,1,0:T(8,128)(2,1)S(1)}, bf16[64,128,128]{2,1,0:T(8,128)(2,1)}, u32[]{:S(2)}) copy-start(bf16[64,128,128]{2,1,0:T(8,128)(2,1)} %param.27) | copy-start | bytes 6291460
Sparse Core Ops, SparseCore 0:
  50.1 30.0 all-gather.4
  167.0 55.2 all-gather.6
  269.6 28.4 all-gather.8
  379.2 70.7 all-gather.10

commit v2 on v1

--- a/solution.py
+++ b/solution.py
@@ -79,6 +79,32 @@
     return (summed / degree.astype(jnp.float32)[:, None]).astype(jnp.bfloat16)
 
 
+def feat_to_rows(block):
+    feat_count = lax.axis_size("feat")
+    row_count, col_count = block.shape
+    pieces = block.reshape(feat_count, row_count // feat_count, col_count)
+    gathered = lax.all_to_all(pieces, "feat", split_axis=0, concat_axis=0, tiled=True)
+    return gathered.transpose(1, 0, 2).reshape(row_count // feat_count, feat_count * col_count)
+
+
+def rows_to_feat(rows):
+    feat_count = lax.axis_size("feat")
+    row_count, width = rows.shape
+    pieces = rows.reshape(row_count, feat_count, width // feat_count).transpose(1, 0, 2)
+    gathered = lax.all_to_all(pieces, "feat", split_axis=0, concat_axis=0, tiled=True)
+    return gathered.reshape(feat_count * row_count, width // feat_count)
+
+
+def mix(own_rows, neigh_rows, self_weight, neigh_weight, gain):
+    width = self_weight.shape[1]
+    running = jnp.dot(own_rows, self_weight, preferred_element_type=jnp.float32)
+    mixed = running + jnp.dot(neigh_rows, neigh_weight, preferred_element_type=jnp.float32)
+    rectified = jnp.maximum(mixed, 0.0)
+    squares = jnp.sum(rectified * rectified, axis=1, keepdims=True)
+    scaled = gain.astype(jnp.float32)[None, :] * rectified * lax.rsqrt(squares / width + EPSILON)
+    return scaled.astype(jnp.bfloat16)
+
+
 def per_device(
     features,
     degree,
@@ -95,12 +121,15 @@
     w_neigh,
     gains,
 ):
-    width = w_self.shape[1]
     tile_side = local_tiles.shape[1]
     placing, landing = routing(
         out_dest, recv_target, features.shape[0] // tile_side, lax.axis_size("dom")
     )
+    full_self = lax.all_gather(w_self, "feat", axis=2, tiled=True)
+    full_neigh = lax.all_gather(w_neigh, "feat", axis=2, tiled=True)
+    full_gains = lax.all_gather(gains, "feat", axis=1, tiled=True)
     current = features
+    own_rows = feat_to_rows(features)
     for layer_idx in range(w_self.shape[0]):
         neighbours = aggregate(
             current,
@@ -115,19 +144,15 @@
             placing,
             landing,
         )
-        self_weight = w_self[layer_idx]
-        neigh_weight = w_neigh[layer_idx]
-        gain_row = gains[layer_idx][None, :]
-        own_part = lax.all_gather(current, "feat", axis=1, tiled=True)
-        neigh_part = lax.all_gather(neighbours, "feat", axis=1, tiled=True)
-        running = jnp.dot(own_part, self_weight, preferred_element_type=jnp.float32)
-        mixed = running + jnp.dot(neigh_part, neigh_weight, preferred_element_type=jnp.float32)
-        rectified = jnp.maximum(mixed, 0.0)
-        squares = lax.psum(jnp.sum(rectified * rectified, axis=1), "feat")
-        scaled = (
-            gain_row.astype(jnp.float32) * rectified * lax.rsqrt(squares[:, None] / width + EPSILON)
+        neigh_rows = feat_to_rows(neighbours)
+        own_rows = mix(
+            own_rows,
+            neigh_rows,
+            full_self[layer_idx],
+            full_neigh[layer_idx],
+            full_gains[layer_idx],
         )
-        current = scaled.astype(jnp.bfloat16)
+        current = rows_to_feat(own_rows)
     return current
 
 

time: 472 us -> 421 us (0.89)
  the two profiles are of different devices: /device:TPU:1 before, /device:TPU:112 now
where the time goes in v2:
time: 421 us; the launch traced here: 420 us
  waiting for transfers between devices  265 us (63%)
  starting transfers between devices  38.1 us (9%)
  blocking collectives  36 us (9%)
  local copies, waits for them, and re-layouts  31.6 us (8%)
  matrix products  28.4 us (7%)
  between operations  13.8 us (3%)
  other arithmetic  6.6 us (2%)
    all_to_all x2, waiting for transfers between devices, aggregate(): lax.all_to_all(payload, 'dom', split_axis=0, concat_axis=0, tiled=True)  254 us
    all_to_all x2, starting transfers between devices, aggregate(): lax.all_to_all(payload, 'dom', split_axis=0, concat_axis=0, tiled=True)  24.1 us
    all_to_all x2, blocking collectives, rows_to_feat(): lax.all_to_all(pieces, 'feat', split_axis=0, concat_axis=0, tiled=True)  17 us
    all_to_all x2, starting transfers between devices, feat_to_rows(): lax.all_to_all(pieces, 'feat', split_axis=0, concat_axis=0, tiled=True)  13.9 us
    all_gather x1, blocking collectives, per_device(): full_gains = lax.all_gather(gains, 'feat', axis=1, tiled=True)  10.5 us
    all_to_all x2, waiting for transfers between devices, feat_to_rows(): lax.all_to_all(pieces, 'feat', split_axis=0, concat_axis=0, tiled=True)  10.1 us
    dot_general x2, matrix products, aggregate(): jnp.einsum('trs,tsd->trd', out_tiles, blocks[out_src], preferred_element_...  9.08 us
    all_to_all x1, blocking collectives, feat_to_rows(): lax.all_to_all(pieces, 'feat', split_axis=0, concat_axis=0, tiled=True)  8.52 us
  transfers between devices with their start and end apart: 6, of which 4 were waited for; matrix products, arithmetic and copies ran while one was open for 9% of the time, Pallas kernels for 0%

profile of v2, /device:TPU:112, one launch (start us, length us, event | category | flops | bytes accessed | tf_op | source)
XLA Modules:
  0.0 420.0 jit_solution(4387864718230443200)
XLA Ops:
  6.5 0.7 all-gather.5.cloned.1.call-update
  7.3 0.7 compare_select_fusion.1
  7.9 1.5 gather_fusion.1
  9.4 0.7 compare_select_fusion.2
  10.1 3.0 gather_fusion
  13.1 4.6 %convert_bitcast_fusion.1 = bf16[64,128,128]{1,2,0:T(8,128)(2,1)} fusion(bf16[64,128,128]{2,1,0:T(8,128)(2,1)} %gather_fusion, bf16[64,128,128]{2,1,0:T(8,128)(2,1)S(1)} %copy-done), kind=kOutput, calls=%fused_computation.23 | convolution fusion | flops 269484032 | bytes 6291456 | tf_op jit(solution)/shard_map/trs,tsd->trd/dot_general | solution.py:49
  17.7 4.1 copy.81
  21.8 0.2 convert_reduce_fusion
  22.0 3.0 convolution_convert_fusion.1
  24.9 2.7 copy.82
  27.7 2.4 pad_maximum_fusion
  30.2 0.0 copy-start.4
  30.2 15.5 %all-to-all-start.1 = ((bf16[64,272,128]{2,1,0:T(8,128)(2,1)}), bf16[64,272,128]{2,1,0:T(8,128)(2,1)}, u32[]{:S(2)}, u32[]{:S(2)}) async-start(bf16[64,272,128]{2,1,0:T(8,128)(2,1)} %pad_maximum_fusion), calls=%async_computation.1 | async-start | bytes 8912896 | tf_op jit(solution)/shard_map/all_to_all | solution.py:64
  45.7 0.0 all-gather.3.cloned.1.call-start
  45.8 0.7 all-gather.3.cloned.1.call-update
  46.5 1.5 gather_fusion.2
  48.0 0.3 convolution_bitcast_fusion.1
  48.4 0.2 copy.85
  48.6 0.1 copy.79
  48.7 0.1 eq.26
  48.9 10.5 %all_gather.9 = bf16[2,1024]{1,0:T(2,128)(2,1)S(1)} all-gather(bf16[2,128]{1,0:T(2,128)(2,1)S(1)} %copy-done.6), channel_id=1, replica_groups=mesh['dom'=64,'feat'=8] {'feat'}, dimensions={1}, use_global_device_ids=true | all-gather | bytes 4608 | tf_op jit(solution)/shard_map/all_gather | solution.py:130
  59.4 0.4 fusion.41
  59.7 118.7 %all-to-all-done.1 = bf16[64,272,128]{2,1,0:T(8,128)(2,1)} async-done(((bf16[64,272,128]{2,1,0:T(8,128)(2,1)}), bf16[64,272,128]{2,1,0:T(8,128)(2,1)}, u32[]{:S(2)}, u32[]{:S(2)}) %all-to-all-start.1) | async-done | bytes 4456480 | tf_op jit(solution)/shard_map/all_to_all | solution.py:64
  178.4 2.5 slice.87
  180.9 2.3 fusion.12
  183.3 0.1 copy.87
  183.4 0.9 slice.88
  184.4 0.2 fusion.22
  184.6 0.8 copy.88
  185.3 10.6 %all-to-all-start.2 = ((bf16[8,64,128]{2,1,0:T(8,128)(2,1)}), bf16[8,64,128]{2,1,0:T(8,128)(2,1)S(1)}, u32[]{:S(2)}, u32[]{:S(2)}) async-start(bf16[8,64,128]{2,1,0:T(8,128)(2,1)} %bitcast.17), calls=%async_computation.2 | async-start | bytes 262144 | tf_op jit(solution)/shard_map/all_to_all | solution.py:86
  195.9 6.1 %all-to-all-done.2 = bf16[8,64,128]{2,1,0:T(8,128)(2,1)S(1)} async-done(((bf16[8,64,128]{2,1,0:T(8,128)(2,1)}), bf16[8,64,128]{2,1,0:T(8,128)(2,1)S(1)}, u32[]{:S(2)}, u32[]{:S(2)}) %all-to-all-start.2) | async-done | bytes 131104 | tf_op jit(solution)/shard_map/all_to_all | solution.py:86
  202.0 3.4 all-to-all-start
  205.4 0.0 all-gather.5.cloned.1.call-done
  205.4 2.1 fusion.6
  207.5 3.9 all-to-all-done
  211.5 2.2 multiply_reduce_fusion.1
  213.7 0.1 bitcast_bitcast_fusion.1
  213.8 8.5 %all_to_all.35 = bf16[8,64,128]{2,1,0:T(8,128)(2,1)S(1)} all-to-all(bf16[8,64,128]{2,1,0:T(8,128)(2,1)S(1)} %bitcast_bitcast_fusion.1), channel_id=1, replica_groups=mesh['dom'=64,'feat'=8] {'feat'}, dimensions={0} | all-to-all | bytes 262144 | tf_op jit(solution)/shard_map/all_to_all | solution.py:94
  222.3 0.6 gather_fusion.4
  222.9 2.2 gather_fusion.3
  225.0 4.5 %convert_bitcast_fusion = bf16[64,128,128]{1,2,0:T(8,128)(2,1)} fusion(bf16[64,128,128]{2,1,0:T(8,128)(2,1)} %gather_fusion.3, bf16[64,128,128]{2,1,0:T(8,128)(2,1)S(1)} %copy-done), kind=kOutput, calls=%fused_computation.22 | convolution fusion | flops 269484032 | bytes 6291456 | tf_op jit(solution)/shard_map/trs,tsd->trd/dot_general | solution.py:49
  229.5 3.3 copy.92
  232.8 1.4 convolution_convert_fusion
  234.2 2.7 copy.93
  237.0 2.4 pad_maximum_fusion.1
  239.4 8.5 %all-to-all-start.4 = ((bf16[64,272,128]{2,1,0:T(8,128)(2,1)}), bf16[64,272,128]{2,1,0:T(8,128)(2,1)}, u32[]{:S(2)}, u32[]{:S(2)}) async-start(bf16[64,272,128]{2,1,0:T(8,128)(2,1)} %pad_maximum_fusion.1), calls=%async_computation.4 | async-start | bytes 8912896 | tf_op jit(solution)/shard_map/all_to_all | solution.py:64
  247.9 0.6 gather_fusion.5
  248.5 0.3 convolution_bitcast_fusion
  248.9 0.2 copy.96
  249.1 0.4 fusion.39
  249.5 135.3 %all-to-all-done.4 = bf16[64,272,128]{2,1,0:T(8,128)(2,1)} async-done(((bf16[64,272,128]{2,1,0:T(8,128)(2,1)}), bf16[64,272,128]{2,1,0:T(8,128)(2,1)}, u32[]{:S(2)}, u32[]{:S(2)}) %all-to-all-start.4) | async-done | bytes 4456480 | tf_op jit(solution)/shard_map/all_to_all | solution.py:64
  384.8 2.5 slice.91
  387.2 0.0 copy-start.8
  387.2 2.4 fusion.15
  389.6 0.2 copy.97
  389.8 0.9 slice.92
  390.7 0.2 fusion.23
  390.9 0.1 copy.98
  391.0 8.5 %all_to_all.36 = bf16[8,64,128]{2,1,0:T(8,128)(2,1)S(1)} all-to-all(bf16[8,64,128]{2,1,0:T(8,128)(2,1)S(1)} %bitcast.147), channel_id=1, replica_groups=mesh['dom'=64,'feat'=8] {'feat'}, dimensions={0} | all-to-all | bytes 262144 | tf_op jit(solution)/shard_map/all_to_all | solution.py:86
  399.6 2.1 fusion.4
  401.6 2.2 multiply_reduce_fusion
  403.9 0.1 bitcast_bitcast_fusion
  404.0 8.5 %all_to_all.37 = bf16[8,64,128]{2,1,0:T(8,128)(2,1)S(1)} all-to-all(bf16[8,64,128]{2,1,0:T(8,128)(2,1)S(1)} %bitcast_bitcast_fusion), channel_id=1, replica_groups=mesh['dom'=64,'feat'=8] {'feat'}, dimensions={0} | all-to-all | bytes 262144 | tf_op jit(solution)/shard_map/all_to_all | solution.py:94
  412.5 0.7 copy.137
  (36 shorter events, 0.2 us)
Async XLA Ops:
  6.5 6.6 %copy-start = (bf16[64,128,128]{2,1,0:T(8,128)(2,1)S(1)}, bf16[64,128,128]{2,1,0:T(8,128)(2,1)}, u32[]{:S(2)}) copy-start(bf16[64,128,128]{2,1,0:T(8,128)(2,1)} %param.27) | copy-start | bytes 6291460
  6.5 198.9 %all-gather.5.cloned.1.call-start = ((), (), s32[]{:S(2)}) async-start(), calls=%async_computation.8 | async-start | bytes 4718592 | tf_op jit(solution)/shard_map/all_gather | solution.py:129
  13.1 8.7 %copy-start.9 = (s32[64,1]{0,1:T(1,128)S(1)}, s32[64,1]{0,1:T(1,128)}, u32[]{:S(2)}) copy-start(s32[64,1]{0,1:T(1,128)} %param.25) | copy-start | bytes 772
  30.1 16.3 %copy-start.10 = (s32[8]{0:T(128)S(1)}, s32[8]{0:T(128)}, u32[]{:S(2)}) copy-start(s32[8]{0:T(128)} %param.23) | copy-start | bytes 100
  30.1 17.9 %copy-start.2 = (bf16[8,128,128]{2,1,0:T(8,128)(2,1)S(1)}, bf16[8,128,128]{2,1,0:T(8,128)(2,1)}, u32[]{:S(2)}) copy-start(bf16[8,128,128]{2,1,0:T(8,128)(2,1)} %param.24) | copy-start | bytes 786436
  30.1 18.5 %copy-start.5 = (s32[1,64,2]{1,2,0:T(2,128)S(1)}, s32[1,64,2]{1,2,0:T(2,128)}, u32[]{:S(2)}) copy-start(s32[1,64,2]{1,2,0:T(2,128)} %param.28) | copy-start | bytes 1540
  30.1 18.7 %copy-start.3 = (s32[512]{0:T(512)S(1)}, s32[512]{0:T(512)}, u32[]{:S(2)}) copy-start(s32[512]{0:T(512)} %param.19) | copy-start | bytes 6148
  30.2 18.7 %copy-start.6 = (bf16[2,128]{1,0:T(2,128)(2,1)S(1)}, bf16[2,128]{1,0:T(2,128)(2,1)}, u32[]{:S(2)}) copy-start(bf16[2,128]{1,0:T(2,128)(2,1)} %param.31) | copy-start | bytes 1540
  30.2 29.2 %copy-start.4 = (s32[8]{0:T(128)S(1)}, s32[8]{0:T(128)}, u32[]{:S(2)}) copy-start(s32[8]{0:T(128)} %param.22) | copy-start | bytes 100
  30.2 148.3 %all-to-all-start.1 = ((bf16[64,272,128]{2,1,0:T(8,128)(2,1)}), bf16[64,272,128]{2,1,0:T(8,128)(2,1)}, u32[]{:S(2)}, u32[]{:S(2)}) async-start(bf16[64,272,128]{2,1,0:T(8,128)(2,1)} %pad_maximum_fusion), calls=%async_computation.1 | async-start | bytes 8912896 | tf_op jit(solution)/shard_map/all_to_all | solution.py:64
  45.7 165.7 %all-gather.3.cloned.1.call-start = ((), (), s32[]{:S(2)}) async-start(), calls=%async_computation.7 | async-start | bytes 4718592 | tf_op jit(solution)/shard_map/all_gather | solution.py:128
  180.9 3.4 copy-start.7
  185.3 16.7 %all-to-all-start.2 = ((bf16[8,64,128]{2,1,0:T(8,128)(2,1)}), bf16[8,64,128]{2,1,0:T(8,128)(2,1)S(1)}, u32[]{:S(2)}, u32[]{:S(2)}) async-start(bf16[8,64,128]{2,1,0:T(8,128)(2,1)} %bitcast.17), calls=%async_computation.2 | async-start | bytes 262144 | tf_op jit(solution)/shard_map/all_to_all | solution.py:86
  202.0 9.4 %all-to-all-start = ((bf16[8,64,128]{2,1,0:T(8,128)(2,1)}), bf16[8,64,128]{2,1,0:T(8,128)(2,1)S(1)}, u32[]{:S(2)}, u32[]{:S(2)}) async-start(bf16[8,64,128]{2,1,0:T(8,128)(2,1)} %bitcast.2), calls=%async_computation | async-start | bytes 262144 | tf_op jit(solution)/shard_map/all_to_all | solution.py:86
  239.4 145.4 %all-to-all-start.4 = ((bf16[64,272,128]{2,1,0:T(8,128)(2,1)}), bf16[64,272,128]{2,1,0:T(8,128)(2,1)}, u32[]{:S(2)}, u32[]{:S(2)}) async-start(bf16[64,272,128]{2,1,0:T(8,128)(2,1)} %pad_maximum_fusion.1), calls=%async_computation.4 | async-start | bytes 8912896 | tf_op jit(solution)/shard_map/all_to_all | solution.py:64
  387.2 3.5 copy-start.8
  387.2 25.9 %copy-start.1 = (bf16[64,128,128]{2,1,0:T(8,128)(2,1)S(1)}, bf16[64,128,128]{2,1,0:T(8,128)(2,1)}, u32[]{:S(2)}) copy-start(bf16[64,128,128]{2,1,0:T(8,128)(2,1)} %param.27) | copy-start | bytes 6291460
Sparse Core Ops, SparseCore 0:
  9.5 44.8 all-gather.4
  56.4 42.3 all-gather.2

commit v3 on v2

--- a/solution.py
+++ b/solution.py
@@ -1,6 +1,8 @@
 import jax
 import jax.numpy as jnp
 from jax import lax
+from jax.experimental import pallas as pl
+from jax.experimental.pallas import tpu as pltpu
 from jax.sharding import PartitionSpec as P
 
 EPSILON = 1e-06
@@ -16,12 +18,57 @@
     )
     slot_rank = jnp.sum(matches.astype(jnp.int32), axis=1)
     slots = destination * capacity + slot_rank
-    slot_ids = jnp.arange(node_count * capacity, dtype=jnp.int32)
-    placing = (slot_ids[:, None] == slots[None, :]).astype(jnp.bfloat16)
     targets = recv_target[0].reshape(-1)
     block_ids = jnp.arange(block_count, dtype=jnp.int32)
     landing = (targets[None, :] == block_ids[:, None]).astype(jnp.bfloat16)
-    return placing, landing
+    return slots.astype(jnp.int32), landing
+
+
+def payload_kernel(slot_ref, src_ref, tiles_ref, blocks_ref, hub_ref, out_ref):
+    node_count, rows_per_node, _ = out_ref.shape
+    tile_count, tile_side, _ = tiles_ref.shape
+    tail = rows_per_node - HUB_PAD
+    capacity = tail // tile_side
+    out_ref[...] = jnp.zeros(out_ref.shape, out_ref.dtype)
+    hub = hub_ref[...]
+
+    def put_hub(node, carry):
+        out_ref[node, pl.ds(tail, HUB_PAD), :] = hub
+        return carry
+
+    lax.fori_loop(0, node_count, put_hub, 0)
+
+    def put_tile(tile, carry):
+        slot = slot_ref[tile]
+        node = slot // capacity
+        first = pl.multiple_of((slot % capacity) * tile_side, tile_side)
+        product = jnp.dot(
+            tiles_ref[tile], blocks_ref[src_ref[tile]], preferred_element_type=jnp.float32
+        )
+        out_ref[node, pl.ds(first, tile_side), :] = product.astype(out_ref.dtype)
+        return carry
+
+    lax.fori_loop(0, tile_count, put_tile, 0)
+
+
+def build_payload(slots, sources, tiles, blocks, hub_block, node_count, capacity):
+    tile_side = tiles.shape[1]
+    col_count = blocks.shape[2]
+    rows_per_node = capacity * tile_side + HUB_PAD
+    return pl.pallas_call(
+        payload_kernel,
+        out_shape=jax.ShapeDtypeStruct((node_count, rows_per_node, col_count), blocks.dtype),
+        grid_spec=pltpu.PrefetchScalarGridSpec(
+            num_scalar_prefetch=2,
+            grid=(1,),
+            in_specs=[
+                pl.BlockSpec(memory_space=pltpu.VMEM),
+                pl.BlockSpec(memory_space=pltpu.VMEM),
+                pl.BlockSpec(memory_space=pltpu.VMEM),
+            ],
+            out_specs=pl.BlockSpec(memory_space=pltpu.VMEM),
+        ),
+    )(slots, sources, tiles, blocks, hub_block)
 
 
 def aggregate(
@@ -34,33 +81,26 @@
     local_tiles,
     out_src,
     out_tiles,
-    placing,
+    slots,
     landing,
+    anchor,
 ):
     vertex_count, col_count = inputs.shape
     tile_side = local_tiles.shape[1]
     block_count = vertex_count // tile_side
     node_count = lax.axis_size("dom")
-    slot_count = placing.shape[0]
+    slot_count = landing.shape[1]
     capacity = slot_count // node_count
     hub_count = hub_ids.shape[0]
     blocks = inputs.reshape(block_count, tile_side, col_count)
     block_ids = jnp.arange(block_count, dtype=jnp.int32)
-    partials = jnp.einsum(
-        "trs,tsd->trd", out_tiles, blocks[out_src], preferred_element_type=jnp.float32
-    ).astype(jnp.bfloat16)
-    outgoing = jnp.einsum(
-        "kt,trd->krd", placing, partials, preferred_element_type=jnp.float32
-    ).astype(jnp.bfloat16)
     hub_local = inputs[hub_ids]
     hub_block = jnp.zeros((HUB_PAD, col_count), jnp.bfloat16).at[:hub_count].set(hub_local)
-    payload = jnp.concatenate(
-        [
-            outgoing.reshape(node_count, capacity * tile_side, col_count),
-            jnp.broadcast_to(hub_block[None], (node_count, HUB_PAD, col_count)),
-        ],
-        axis=1,
-    )
+    payload = build_payload(
+        slots, out_src.astype(jnp.int32), out_tiles, blocks, hub_block, node_count, capacity
+    )
+    if anchor is not None:
+        payload, anchor = lax.optimization_barrier((payload, anchor))
     arrived = lax.all_to_all(payload, "dom", split_axis=0, concat_axis=0, tiled=True)
     tiles_in = arrived[:, : capacity * tile_side, :].reshape(slot_count, tile_side, col_count)
     hub_rows = arrived[:, capacity * tile_side : capacity * tile_side + hub_count, :].reshape(
@@ -76,7 +116,7 @@
     from_local = jnp.einsum("bt,trd->brd", onehot, local_products, precision=lax.Precision.HIGHEST)
     from_hubs = jnp.dot(hub_adjacency, hub_rows, preferred_element_type=jnp.float32)
     summed = (from_peers + from_local).reshape(vertex_count, col_count) + from_hubs
-    return (summed / degree.astype(jnp.float32)[:, None]).astype(jnp.bfloat16)
+    return (summed / degree.astype(jnp.float32)[:, None]).astype(jnp.bfloat16), anchor
 
 
 def feat_to_rows(block):
@@ -122,7 +162,7 @@
     gains,
 ):
     tile_side = local_tiles.shape[1]
-    placing, landing = routing(
+    slots, landing = routing(
         out_dest, recv_target, features.shape[0] // tile_side, lax.axis_size("dom")
     )
     full_self = lax.all_gather(w_self, "feat", axis=2, tiled=True)
@@ -131,7 +171,7 @@
     current = features
     own_rows = feat_to_rows(features)
     for layer_idx in range(w_self.shape[0]):
-        neighbours = aggregate(
+        neighbours, anchored = aggregate(
             current,
             degree,
             hub_ids,
@@ -141,9 +181,12 @@
             local_tiles,
             out_src,
             out_tiles,
-            placing,
+            slots,
             landing,
+            own_rows if layer_idx == 0 else None,
         )
+        if anchored is not None:
+            own_rows = anchored
         neigh_rows = feat_to_rows(neighbours)
         own_rows = mix(
             own_rows,

time: 421 us -> 424 us (level)
  the two profiles are of different devices: /device:TPU:112 before, /device:TPU:40 now
where the time goes in v3:
time: 424 us; the launch traced here: 423 us
  waiting for transfers between devices  264 us (62%)
  starting transfers between devices  46.1 us (11%)
  blocking collectives  39.6 us (9%)
  Pallas kernels  28.6 us (7%)
  matrix products  15 us (4%)
  local copies, waits for them, and re-layouts  13.8 us (3%)
  between operations  13.8 us (3%)
    all_to_all x2, waiting for transfers between devices, aggregate(): lax.all_to_all(payload, 'dom', split_axis=0, concat_axis=0, tiled=True)  256 us
    pallas_call x2, Pallas kernels, build_payload(): pl.pallas_call(payload_kernel, out_shape=jax.ShapeDtypeStruct((node_count...  28.6 us
    all_to_all x2, starting transfers between devices, aggregate(): lax.all_to_all(payload, 'dom', split_axis=0, concat_axis=0, tiled=True)  23.9 us
    all_to_all x2, starting transfers between devices, feat_to_rows(): lax.all_to_all(pieces, 'feat', split_axis=0, concat_axis=0, tiled=True)  22.1 us
    all_to_all x2, blocking collectives, rows_to_feat(): lax.all_to_all(pieces, 'feat', split_axis=0, concat_axis=0, tiled=True)  17 us
    all_to_all x1, blocking collectives, feat_to_rows(): lax.all_to_all(pieces, 'feat', split_axis=0, concat_axis=0, tiled=True)  11.6 us
    all_gather x1, blocking collectives, per_device(): full_gains = lax.all_gather(gains, 'feat', axis=1, tiled=True)  11 us
  transfers between devices with their start and end apart: 6, of which 3 were waited for; matrix products, arithmetic and copies ran while one was open for 4% of the time, Pallas kernels for 3%

profile of v3, /device:TPU:40, one launch (start us, length us, event | category | flops | bytes accessed | tf_op | source)
XLA Modules:
  0.0 423.4 jit_solution(10904648437019040894)
XLA Ops:
  6.5 0.7 all-gather.5.cloned.1.call-update
  7.3 4.3 %all-to-all-start = ((bf16[8,64,128]{2,1,0:T(8,128)(2,1)}), bf16[8,64,128]{2,1,0:T(8,128)(2,1)S(1)}, u32[]{:S(2)}, u32[]{:S(2)}) async-start(bf16[8,64,128]{2,1,0:T(8,128)(2,1)} %bitcast.122), calls=%async_computation | async-start | bytes 262144 | tf_op jit(solution)/shard_map/all_to_all | solution.py:126
  11.6 0.7 compare_select_fusion.1
  12.2 1.5 gather_fusion
  13.7 0.6 scatter.6.hub_ref
  14.3 0.9 convert_reduce_fusion
  15.2 1.2 multiply_add_fusion.slot_ref
  16.4 14.3 %shard_map.136 = bf16[64,272,128]{2,1,0:T(8,128)(2,1)} custom-call(s32[64]{0:T(128)} %multiply_add_fusion.slot_ref, s32[64]{0:T(128)} %src_ref.3, bf16[64,128,128]{2,1,0:T(8,128)(2,1)} %tiles_ref.3, bf16[4,128,128]{2,1,0:T(8,128)(2,1)} %bitcast.123, bf16[16,128]{1,0:T(8,128)(2,1)} %scatter.6.hub_ref), custom_call_target="tpu_custom_call" | custom-call | tf_op jit(solution)/shard_map/pallas_call | solution.py:58
  30.8 0.0 all-to-all-done
  30.8 0.0 copy-start.9
  30.8 0.0 copy-start.1
  30.8 0.0 copy-start.6
  30.8 0.0 copy-start.4
  30.8 0.0 copy-start.7
  30.8 0.0 copy-start.5
  30.9 16.4 %all-to-all-start.1 = ((bf16[64,272,128]{2,1,0:T(8,128)(2,1)}), bf16[64,272,128]{2,1,0:T(8,128)(2,1)}, u32[]{:S(2)}, u32[]{:S(2)}) async-start(bf16[64,272,128]{2,1,0:T(8,128)(2,1)} %shard_map.136), calls=%async_computation.1 | async-start | bytes 8912896 | tf_op jit(solution)/shard_map/all_to_all | solution.py:104
  47.3 0.0 all-gather.3.cloned.1.call-start
  47.4 0.7 all-gather.3.cloned.1.call-update
  48.1 0.6 gather_fusion.1
  48.7 0.3 convolution_bitcast_fusion.1
  49.0 0.2 copy.55
  49.3 0.1 copy.52
  49.4 0.1 eq.23
  49.6 0.0 copy-done.7
  49.6 11.0 %all_gather.9 = bf16[2,1024]{1,0:T(2,128)(2,1)S(1)} all-gather(bf16[2,128]{1,0:T(2,128)(2,1)S(1)} %copy-done.7), channel_id=1, replica_groups=mesh['dom'=64,'feat'=8] {'feat'}, dimensions={1}, use_global_device_ids=true | all-gather | bytes 4608 | tf_op jit(solution)/shard_map/all_gather | solution.py:170
  60.5 0.4 fusion.34
  60.9 123.5 %all-to-all-done.1 = bf16[64,272,128]{2,1,0:T(8,128)(2,1)} async-done(((bf16[64,272,128]{2,1,0:T(8,128)(2,1)}), bf16[64,272,128]{2,1,0:T(8,128)(2,1)}, u32[]{:S(2)}, u32[]{:S(2)}) %all-to-all-start.1) | async-done | bytes 4456480 | tf_op jit(solution)/shard_map/all_to_all | solution.py:104
  184.4 2.5 slice.83
  186.9 0.0 copy-start.8
  186.9 2.3 fusion.12
  189.3 0.1 copy.57
  189.4 0.9 slice.84
  190.3 0.2 fusion.22
  190.6 0.8 copy.58
  191.3 17.8 %all-to-all-start.2 = ((bf16[8,64,128]{2,1,0:T(8,128)(2,1)}), bf16[8,64,128]{2,1,0:T(8,128)(2,1)S(1)}, u32[]{:S(2)}, u32[]{:S(2)}) async-start(bf16[8,64,128]{2,1,0:T(8,128)(2,1)} %bitcast.14), calls=%async_computation.2 | async-start | bytes 262144 | tf_op jit(solution)/shard_map/all_to_all | solution.py:126
  209.1 0.0 all-gather.5.cloned.1.call-done
  209.1 6.1 %all-to-all-done.2 = bf16[8,64,128]{2,1,0:T(8,128)(2,1)S(1)} async-done(((bf16[8,64,128]{2,1,0:T(8,128)(2,1)}), bf16[8,64,128]{2,1,0:T(8,128)(2,1)S(1)}, u32[]{:S(2)}, u32[]{:S(2)}) %all-to-all-start.2) | async-done | bytes 131104 | tf_op jit(solution)/shard_map/all_to_all | solution.py:126
  215.2 2.1 fusion.6
  217.3 0.0 all-gather.3.cloned.1.call-done
  217.3 2.2 multiply_reduce_fusion.1
  219.5 0.1 bitcast_bitcast_fusion.1
  219.7 8.5 %all_to_all.35 = bf16[8,64,128]{2,1,0:T(8,128)(2,1)S(1)} all-to-all(bf16[8,64,128]{2,1,0:T(8,128)(2,1)S(1)} %bitcast_bitcast_fusion.1), channel_id=1, replica_groups=mesh['dom'=64,'feat'=8] {'feat'}, dimensions={0} | all-to-all | bytes 262144 | tf_op jit(solution)/shard_map/all_to_all | solution.py:134
  228.2 0.6 gather_fusion.2
  228.7 0.6 scatter.9.hub_ref
  229.3 0.0 copy-done.2
  229.3 14.3 %shard_map.137 = bf16[64,272,128]{2,1,0:T(8,128)(2,1)} custom-call(s32[64]{0:T(128)} %multiply_add_fusion.slot_ref, s32[64]{0:T(128)} %src_ref.3, bf16[64,128,128]{2,1,0:T(8,128)(2,1)} %tiles_ref.3, bf16[4,128,128]{2,1,0:T(8,128)(2,1)} %bitcast.126, bf16[16,128]{1,0:T(8,128)(2,1)} %scatter.9.hub_ref), custom_call_target="tpu_custom_call" | custom-call | tf_op jit(solution)/shard_map/pallas_call | solution.py:58
  243.6 7.5 %all-to-all-start.4 = ((bf16[64,272,128]{2,1,0:T(8,128)(2,1)}), bf16[64,272,128]{2,1,0:T(8,128)(2,1)}, u32[]{:S(2)}, u32[]{:S(2)}) async-start(bf16[64,272,128]{2,1,0:T(8,128)(2,1)} %shard_map.137), calls=%async_computation.4 | async-start | bytes 8912896 | tf_op jit(solution)/shard_map/all_to_all | solution.py:104
  251.1 0.6 gather_fusion.3
  251.7 0.3 convolution_bitcast_fusion
  252.1 0.2 copy.63
  252.3 0.4 fusion.32
  252.7 132.5 %all-to-all-done.4 = bf16[64,272,128]{2,1,0:T(8,128)(2,1)} async-done(((bf16[64,272,128]{2,1,0:T(8,128)(2,1)}), bf16[64,272,128]{2,1,0:T(8,128)(2,1)}, u32[]{:S(2)}, u32[]{:S(2)}) %all-to-all-start.4) | async-done | bytes 4456480 | tf_op jit(solution)/shard_map/all_to_all | solution.py:104
  385.2 2.5 slice.87
  387.6 2.3 fusion.15
  390.0 0.2 copy.64
  390.1 0.9 slice.88
  391.1 0.2 fusion.23
  391.3 0.1 copy.65
  391.4 11.6 %all_to_all.36 = bf16[8,64,128]{2,1,0:T(8,128)(2,1)S(1)} all-to-all(bf16[8,64,128]{2,1,0:T(8,128)(2,1)S(1)} %bitcast.129), channel_id=1, replica_groups=mesh['dom'=64,'feat'=8] {'feat'}, dimensions={0} | all-to-all | bytes 262144 | tf_op jit(solution)/shard_map/all_to_all | solution.py:126
  403.0 2.1 fusion.4
  405.0 2.2 multiply_reduce_fusion
  407.3 0.1 bitcast_bitcast_fusion
  407.4 8.5 %all_to_all.37 = bf16[8,64,128]{2,1,0:T(8,128)(2,1)S(1)} all-to-all(bf16[8,64,128]{2,1,0:T(8,128)(2,1)S(1)} %bitcast_bitcast_fusion), channel_id=1, replica_groups=mesh['dom'=64,'feat'=8] {'feat'}, dimensions={0} | all-to-all | bytes 262144 | tf_op jit(solution)/shard_map/all_to_all | solution.py:134
  415.9 0.7 copy.97
  (21 shorter events, 0.1 us)
Async XLA Ops:
  6.5 42.2 %copy-start = (bf16[8,128,128]{2,1,0:T(8,128)(2,1)S(1)}, bf16[8,128,128]{2,1,0:T(8,128)(2,1)}, u32[]{:S(2)}) copy-start(bf16[8,128,128]{2,1,0:T(8,128)(2,1)} %param.24) | copy-start | bytes 786436
  6.5 202.6 %all-gather.5.cloned.1.call-start = ((), (), s32[]{:S(2)}) async-start(), calls=%async_computation.8 | async-start | bytes 4718592 | tf_op jit(solution)/shard_map/all_gather | solution.py:169
  7.3 23.5 %all-to-all-start = ((bf16[8,64,128]{2,1,0:T(8,128)(2,1)}), bf16[8,64,128]{2,1,0:T(8,128)(2,1)S(1)}, u32[]{:S(2)}, u32[]{:S(2)}) async-start(bf16[8,64,128]{2,1,0:T(8,128)(2,1)} %bitcast.122), calls=%async_computation | async-start | bytes 262144 | tf_op jit(solution)/shard_map/all_to_all | solution.py:126
  30.8 17.3 %copy-start.9 = (s32[8]{0:T(128)S(1)}, s32[8]{0:T(128)}, u32[]{:S(2)}) copy-start(s32[8]{0:T(128)} %param.23) | copy-start | bytes 100
  30.8 17.3 %copy-start.1 = (bf16[512,128]{1,0:T(8,128)(2,1)S(1)}, bf16[512,128]{1,0:T(8,128)(2,1)}, u32[]{:S(2)}) copy-start(bf16[512,128]{1,0:T(8,128)(2,1)} %param.18) | copy-start | bytes 393220
  30.8 18.5 %copy-start.6 = (s32[1,64,2]{1,2,0:T(2,128)S(1)}, s32[1,64,2]{1,2,0:T(2,128)}, u32[]{:S(2)}) copy-start(s32[1,64,2]{1,2,0:T(2,128)} %param.28) | copy-start | bytes 1540
  30.8 18.7 %copy-start.4 = (s32[512]{0:T(512)S(1)}, s32[512]{0:T(512)}, u32[]{:S(2)}) copy-start(s32[512]{0:T(512)} %param.19) | copy-start | bytes 6148
  30.8 18.7 %copy-start.7 = (bf16[2,128]{1,0:T(2,128)(2,1)S(1)}, bf16[2,128]{1,0:T(2,128)(2,1)}, u32[]{:S(2)}) copy-start(bf16[2,128]{1,0:T(2,128)(2,1)} %param.31) | copy-start | bytes 1540
  30.8 29.7 %copy-start.5 = (s32[8]{0:T(128)S(1)}, s32[8]{0:T(128)}, u32[]{:S(2)}) copy-start(s32[8]{0:T(128)} %param.22) | copy-start | bytes 100
  30.9 153.6 %all-to-all-start.1 = ((bf16[64,272,128]{2,1,0:T(8,128)(2,1)}), bf16[64,272,128]{2,1,0:T(8,128)(2,1)}, u32[]{:S(2)}, u32[]{:S(2)}) async-start(bf16[64,272,128]{2,1,0:T(8,128)(2,1)} %shard_map.136), calls=%async_computation.1 | async-start | bytes 8912896 | tf_op jit(solution)/shard_map/all_to_all | solution.py:104
  47.3 170.0 %all-gather.3.cloned.1.call-start = ((), (), s32[]{:S(2)}) async-start(), calls=%async_computation.7 | async-start | bytes 4718592 | tf_op jit(solution)/shard_map/all_gather | solution.py:168
  186.9 3.4 copy-start.8
  191.3 23.9 %all-to-all-start.2 = ((bf16[8,64,128]{2,1,0:T(8,128)(2,1)}), bf16[8,64,128]{2,1,0:T(8,128)(2,1)S(1)}, u32[]{:S(2)}, u32[]{:S(2)}) async-start(bf16[8,64,128]{2,1,0:T(8,128)(2,1)} %bitcast.14), calls=%async_computation.2 | async-start | bytes 262144 | tf_op jit(solution)/shard_map/all_to_all | solution.py:126
  228.2 1.2 copy-start.2
  243.6 7.5 %copy-start.3 = (bf16[8,64,128]{2,1,0:T(8,128)(2,1)S(1)}, bf16[8,64,128]{2,1,0:T(8,128)(2,1)}, u32[]{:S(2)}) copy-start(bf16[8,64,128]{2,1,0:T(8,128)(2,1)} %copy-done.2) | copy-start | bytes 393220
  243.6 141.6 %all-to-all-start.4 = ((bf16[64,272,128]{2,1,0:T(8,128)(2,1)}), bf16[64,272,128]{2,1,0:T(8,128)(2,1)}, u32[]{:S(2)}, u32[]{:S(2)}) async-start(bf16[64,272,128]{2,1,0:T(8,128)(2,1)} %shard_map.137), calls=%async_computation.4 | async-start | bytes 8912896 | tf_op jit(solution)/shard_map/all_to_all | solution.py:104
Sparse Core Ops, SparseCore 0:
  9.5 46.0 all-gather.4
  57.7 42.4 all-gather.2

commit v4 on v3

--- a/solution.py
+++ b/solution.py
@@ -36,7 +36,7 @@
         out_ref[node, pl.ds(tail, HUB_PAD), :] = hub
         return carry
 
-    lax.fori_loop(0, node_count, put_hub, 0)
+    lax.fori_loop(0, node_count, put_hub, 0, unroll=8)
 
     def put_tile(tile, carry):
         slot = slot_ref[tile]
@@ -48,7 +48,7 @@
         out_ref[node, pl.ds(first, tile_side), :] = product.astype(out_ref.dtype)
         return carry
 
-    lax.fori_loop(0, tile_count, put_tile, 0)
+    lax.fori_loop(0, tile_count, put_tile, 0, unroll=8)
 
 
 def build_payload(slots, sources, tiles, blocks, hub_block, node_count, capacity):

time: 424 us -> 409 us (0.965)
  Pallas kernels: 28.6 us -> 13.7 us
  starting transfers between devices: 46.1 us -> 35 us
  waiting for transfers between devices: 264 us -> 275 us
    pallas_call x2, Pallas kernels: 28.6 us -> 13.7 us  [build_payload(): pl.pallas_call(payload_kernel, out_shape=jax.ShapeDtypeStruct((node_count...]
    all_to_all x2, waiting for transfers between devices: 256 us -> 267 us  [aggregate(): lax.all_to_all(payload, 'dom', split_axis=0, concat_axis=0, tiled=True)]
    all_to_all x2, starting transfers between devices: 22.1 us -> 11.1 us  [feat_to_rows(): lax.all_to_all(pieces, 'feat', split_axis=0, concat_axis=0, tiled=True)]
  transfers between devices with their start and end apart: 6 -> 6, of which waited for: 3 -> 3; matrix products, arithmetic and copies ran while one was open for 4% -> 4% of each run, Pallas kernels for 3% -> 2%
where the time goes in v4:
time: 409 us; the launch traced here: 408 us
  waiting for transfers between devices  275 us (67%)
  blocking collectives  38.9 us (10%)
  starting transfers between devices  35 us (9%)
  matrix products  15 us (4%)
  local copies, waits for them, and re-layouts  13.8 us (3%)
  between operations  13.8 us (3%)
  Pallas kernels  13.7 us (3%)
    all_to_all x2, waiting for transfers between devices, aggregate(): lax.all_to_all(payload, 'dom', split_axis=0, concat_axis=0, tiled=True)  267 us
    all_to_all x2, starting transfers between devices, aggregate(): lax.all_to_all(payload, 'dom', split_axis=0, concat_axis=0, tiled=True)  23.9 us
    all_to_all x2, blocking collectives, rows_to_feat(): lax.all_to_all(pieces, 'feat', split_axis=0, concat_axis=0, tiled=True)  17 us
    pallas_call x2, Pallas kernels, build_payload(): pl.pallas_call(payload_kernel, out_shape=jax.ShapeDtypeStruct((node_count...  13.7 us
    all_to_all x2, starting transfers between devices, feat_to_rows(): lax.all_to_all(pieces, 'feat', split_axis=0, concat_axis=0, tiled=True)  11.1 us
    all_gather x1, blocking collectives, per_device(): full_gains = lax.all_gather(gains, 'feat', axis=1, tiled=True)  11 us
    all_to_all x1, blocking collectives, feat_to_rows(): lax.all_to_all(pieces, 'feat', split_axis=0, concat_axis=0, tiled=True)  10.9 us
  transfers between devices with their start and end apart: 6, of which 3 were waited for; matrix products, arithmetic and copies ran while one was open for 4% of the time, Pallas kernels for 2%

profile of v4, /device:TPU:40, one launch (start us, length us, event | category | flops | bytes accessed | tf_op | source)
XLA Modules:
  0.0 407.9 jit_solution(11234685779089201046)
XLA Ops:
  6.5 0.7 all-gather.5.cloned.1.call-update
  7.3 4.3 %all-to-all-start = ((bf16[8,64,128]{2,1,0:T(8,128)(2,1)}), bf16[8,64,128]{2,1,0:T(8,128)(2,1)S(1)}, u32[]{:S(2)}, u32[]{:S(2)}) async-start(bf16[8,64,128]{2,1,0:T(8,128)(2,1)} %bitcast.122), calls=%async_computation | async-start | bytes 262144 | tf_op jit(solution)/shard_map/all_to_all | solution.py:126
  11.6 0.7 compare_select_fusion.1
  12.2 1.5 gather_fusion
  13.7 0.6 scatter.6.hub_ref
  14.3 0.9 convert_reduce_fusion
  15.2 1.2 multiply_add_fusion.slot_ref
  16.4 6.9 %shard_map.136 = bf16[64,272,128]{2,1,0:T(8,128)(2,1)} custom-call(s32[64]{0:T(128)} %multiply_add_fusion.slot_ref, s32[64]{0:T(128)} %src_ref.3, bf16[64,128,128]{2,1,0:T(8,128)(2,1)} %tiles_ref.3, bf16[4,128,128]{2,1,0:T(8,128)(2,1)} %bitcast.123, bf16[16,128]{1,0:T(8,128)(2,1)} %scatter.6.hub_ref), custom_call_target="tpu_custom_call" | custom-call | tf_op jit(solution)/shard_map/pallas_call | solution.py:58
  23.3 0.0 all-to-all-done
  23.3 0.0 copy-start.9
  23.3 0.0 copy-start.1
  23.3 0.0 copy-start.6
  23.4 0.0 copy-start.4
  23.4 0.0 copy-start.7
  23.4 0.0 copy-start.5
  23.4 16.4 %all-to-all-start.1 = ((bf16[64,272,128]{2,1,0:T(8,128)(2,1)}), bf16[64,272,128]{2,1,0:T(8,128)(2,1)}, u32[]{:S(2)}, u32[]{:S(2)}) async-start(bf16[64,272,128]{2,1,0:T(8,128)(2,1)} %shard_map.136), calls=%async_computation.1 | async-start | bytes 8912896 | tf_op jit(solution)/shard_map/all_to_all | solution.py:104
  39.8 0.0 all-gather.3.cloned.1.call-start
  39.9 0.7 all-gather.3.cloned.1.call-update
  40.6 0.6 gather_fusion.1
  41.3 0.0 copy-done
  41.3 0.3 convolution_bitcast_fusion.1
  41.6 0.2 copy.55
  41.8 0.0 copy-done.6
  41.8 0.1 copy.52
  41.9 0.1 eq.23
  42.1 11.0 %all_gather.9 = bf16[2,1024]{1,0:T(2,128)(2,1)S(1)} all-gather(bf16[2,128]{1,0:T(2,128)(2,1)S(1)} %copy-done.7), channel_id=1, replica_groups=mesh['dom'=64,'feat'=8] {'feat'}, dimensions={1}, use_global_device_ids=true | all-gather | bytes 4608 | tf_op jit(solution)/shard_map/all_gather | solution.py:170
  53.1 0.4 fusion.34
  53.5 134.2 %all-to-all-done.1 = bf16[64,272,128]{2,1,0:T(8,128)(2,1)} async-done(((bf16[64,272,128]{2,1,0:T(8,128)(2,1)}), bf16[64,272,128]{2,1,0:T(8,128)(2,1)}, u32[]{:S(2)}, u32[]{:S(2)}) %all-to-all-start.1) | async-done | bytes 4456480 | tf_op jit(solution)/shard_map/all_to_all | solution.py:104
  187.7 2.5 slice.83
  190.2 0.0 copy-start.8
  190.2 2.3 fusion.12
  192.5 0.1 copy.57
  192.7 0.9 slice.84
  193.6 0.2 fusion.22
  193.8 0.8 copy.58
  194.6 6.8 %all-to-all-start.2 = ((bf16[8,64,128]{2,1,0:T(8,128)(2,1)}), bf16[8,64,128]{2,1,0:T(8,128)(2,1)S(1)}, u32[]{:S(2)}, u32[]{:S(2)}) async-start(bf16[8,64,128]{2,1,0:T(8,128)(2,1)} %bitcast.14), calls=%async_computation.2 | async-start | bytes 262144 | tf_op jit(solution)/shard_map/all_to_all | solution.py:126
  201.4 0.0 all-gather.5.cloned.1.call-done
  201.4 6.1 %all-to-all-done.2 = bf16[8,64,128]{2,1,0:T(8,128)(2,1)S(1)} async-done(((bf16[8,64,128]{2,1,0:T(8,128)(2,1)}), bf16[8,64,128]{2,1,0:T(8,128)(2,1)S(1)}, u32[]{:S(2)}, u32[]{:S(2)}) %all-to-all-start.2) | async-done | bytes 131104 | tf_op jit(solution)/shard_map/all_to_all | solution.py:126
  207.5 2.1 fusion.6
  209.6 0.0 all-gather.3.cloned.1.call-done
  209.6 2.2 multiply_reduce_fusion.1
  211.8 0.1 bitcast_bitcast_fusion.1
  211.9 8.5 %all_to_all.35 = bf16[8,64,128]{2,1,0:T(8,128)(2,1)S(1)} all-to-all(bf16[8,64,128]{2,1,0:T(8,128)(2,1)S(1)} %bitcast_bitcast_fusion.1), channel_id=1, replica_groups=mesh['dom'=64,'feat'=8] {'feat'}, dimensions={0} | all-to-all | bytes 262144 | tf_op jit(solution)/shard_map/all_to_all | solution.py:134
  220.4 0.6 gather_fusion.2
  221.0 0.6 scatter.9.hub_ref
  221.6 6.8 %shard_map.137 = bf16[64,272,128]{2,1,0:T(8,128)(2,1)} custom-call(s32[64]{0:T(128)} %multiply_add_fusion.slot_ref, s32[64]{0:T(128)} %src_ref.3, bf16[64,128,128]{2,1,0:T(8,128)(2,1)} %tiles_ref.3, bf16[4,128,128]{2,1,0:T(8,128)(2,1)} %bitcast.126, bf16[16,128]{1,0:T(8,128)(2,1)} %scatter.9.hub_ref), custom_call_target="tpu_custom_call" | custom-call | tf_op jit(solution)/shard_map/pallas_call | solution.py:58
  228.4 7.5 %all-to-all-start.4 = ((bf16[64,272,128]{2,1,0:T(8,128)(2,1)}), bf16[64,272,128]{2,1,0:T(8,128)(2,1)}, u32[]{:S(2)}, u32[]{:S(2)}) async-start(bf16[64,272,128]{2,1,0:T(8,128)(2,1)} %shard_map.137), calls=%async_computation.4 | async-start | bytes 8912896 | tf_op jit(solution)/shard_map/all_to_all | solution.py:104
  235.9 0.6 gather_fusion.3
  236.5 0.3 convolution_bitcast_fusion
  236.8 0.2 copy.63
  237.1 0.4 fusion.32
  237.4 132.9 %all-to-all-done.4 = bf16[64,272,128]{2,1,0:T(8,128)(2,1)} async-done(((bf16[64,272,128]{2,1,0:T(8,128)(2,1)}), bf16[64,272,128]{2,1,0:T(8,128)(2,1)}, u32[]{:S(2)}, u32[]{:S(2)}) %all-to-all-start.4) | async-done | bytes 4456480 | tf_op jit(solution)/shard_map/all_to_all | solution.py:104
  370.3 2.5 slice.87
  372.8 2.3 fusion.15
  375.1 0.2 copy.64
  375.3 0.9 slice.88
  376.2 0.2 fusion.23
  376.5 0.1 copy.65
  376.6 10.9 %all_to_all.36 = bf16[8,64,128]{2,1,0:T(8,128)(2,1)S(1)} all-to-all(bf16[8,64,128]{2,1,0:T(8,128)(2,1)S(1)} %bitcast.129), channel_id=1, replica_groups=mesh['dom'=64,'feat'=8] {'feat'}, dimensions={0} | all-to-all | bytes 262144 | tf_op jit(solution)/shard_map/all_to_all | solution.py:126
  387.4 2.1 fusion.4
  389.5 2.2 multiply_reduce_fusion
  391.8 0.1 bitcast_bitcast_fusion
  391.9 8.5 %all_to_all.37 = bf16[8,64,128]{2,1,0:T(8,128)(2,1)S(1)} all-to-all(bf16[8,64,128]{2,1,0:T(8,128)(2,1)S(1)} %bitcast_bitcast_fusion), channel_id=1, replica_groups=mesh['dom'=64,'feat'=8] {'feat'}, dimensions={0} | all-to-all | bytes 262144 | tf_op jit(solution)/shard_map/all_to_all | solution.py:134
  400.4 0.7 copy.97
  (21 shorter events, 0.1 us)
Async XLA Ops:
  6.5 34.7 %copy-start = (bf16[8,128,128]{2,1,0:T(8,128)(2,1)S(1)}, bf16[8,128,128]{2,1,0:T(8,128)(2,1)}, u32[]{:S(2)}) copy-start(bf16[8,128,128]{2,1,0:T(8,128)(2,1)} %param.24) | copy-start | bytes 786436
  6.5 194.8 %all-gather.5.cloned.1.call-start = ((), (), s32[]{:S(2)}) async-start(), calls=%async_computation.8 | async-start | bytes 4718592 | tf_op jit(solution)/shard_map/all_gather | solution.py:169
  7.3 16.0 %all-to-all-start = ((bf16[8,64,128]{2,1,0:T(8,128)(2,1)}), bf16[8,64,128]{2,1,0:T(8,128)(2,1)S(1)}, u32[]{:S(2)}, u32[]{:S(2)}) async-start(bf16[8,64,128]{2,1,0:T(8,128)(2,1)} %bitcast.122), calls=%async_computation | async-start | bytes 262144 | tf_op jit(solution)/shard_map/all_to_all | solution.py:126
  23.3 17.3 %copy-start.9 = (s32[8]{0:T(128)S(1)}, s32[8]{0:T(128)}, u32[]{:S(2)}) copy-start(s32[8]{0:T(128)} %param.23) | copy-start | bytes 100
  23.3 17.3 %copy-start.1 = (bf16[512,128]{1,0:T(8,128)(2,1)S(1)}, bf16[512,128]{1,0:T(8,128)(2,1)}, u32[]{:S(2)}) copy-start(bf16[512,128]{1,0:T(8,128)(2,1)} %param.18) | copy-start | bytes 393220
  23.3 18.5 %copy-start.6 = (s32[1,64,2]{1,2,0:T(2,128)S(1)}, s32[1,64,2]{1,2,0:T(2,128)}, u32[]{:S(2)}) copy-start(s32[1,64,2]{1,2,0:T(2,128)} %param.28) | copy-start | bytes 1540
  23.4 18.7 %copy-start.4 = (s32[512]{0:T(512)S(1)}, s32[512]{0:T(512)}, u32[]{:S(2)}) copy-start(s32[512]{0:T(512)} %param.19) | copy-start | bytes 6148
  23.4 18.7 %copy-start.7 = (bf16[2,128]{1,0:T(2,128)(2,1)S(1)}, bf16[2,128]{1,0:T(2,128)(2,1)}, u32[]{:S(2)}) copy-start(bf16[2,128]{1,0:T(2,128)(2,1)} %param.31) | copy-start | bytes 1540
  23.4 29.7 %copy-start.5 = (s32[8]{0:T(128)S(1)}, s32[8]{0:T(128)}, u32[]{:S(2)}) copy-start(s32[8]{0:T(128)} %param.22) | copy-start | bytes 100
  23.4 164.3 %all-to-all-start.1 = ((bf16[64,272,128]{2,1,0:T(8,128)(2,1)}), bf16[64,272,128]{2,1,0:T(8,128)(2,1)}, u32[]{:S(2)}, u32[]{:S(2)}) async-start(bf16[64,272,128]{2,1,0:T(8,128)(2,1)} %shard_map.136), calls=%async_computation.1 | async-start | bytes 8912896 | tf_op jit(solution)/shard_map/all_to_all | solution.py:104
  39.8 169.7 %all-gather.3.cloned.1.call-start = ((), (), s32[]{:S(2)}) async-start(), calls=%async_computation.7 | async-start | bytes 4718592 | tf_op jit(solution)/shard_map/all_gather | solution.py:168
  190.2 3.4 copy-start.8
  194.6 12.9 %all-to-all-start.2 = ((bf16[8,64,128]{2,1,0:T(8,128)(2,1)}), bf16[8,64,128]{2,1,0:T(8,128)(2,1)S(1)}, u32[]{:S(2)}, u32[]{:S(2)}) async-start(bf16[8,64,128]{2,1,0:T(8,128)(2,1)} %bitcast.14), calls=%async_computation.2 | async-start | bytes 262144 | tf_op jit(solution)/shard_map/all_to_all | solution.py:126
  220.4 1.2 copy-start.2
  228.4 7.5 %copy-start.3 = (bf16[8,64,128]{2,1,0:T(8,128)(2,1)S(1)}, bf16[8,64,128]{2,1,0:T(8,128)(2,1)}, u32[]{:S(2)}) copy-start(bf16[8,64,128]{2,1,0:T(8,128)(2,1)} %copy-done.2) | copy-start | bytes 393220
  228.4 141.9 %all-to-all-start.4 = ((bf16[64,272,128]{2,1,0:T(8,128)(2,1)}), bf16[64,272,128]{2,1,0:T(8,128)(2,1)}, u32[]{:S(2)}, u32[]{:S(2)}) async-start(bf16[64,272,128]{2,1,0:T(8,128)(2,1)} %shard_map.137), calls=%async_computation.4 | async-start | bytes 8912896 | tf_op jit(solution)/shard_map/all_to_all | solution.py:104
Sparse Core Ops, SparseCore 0:
  9.5 45.5 all-gather.4
  57.2 42.4 all-gather.2

commit v5 on v4

--- a/solution.py
+++ b/solution.py
@@ -145,6 +145,23 @@
     return scaled.astype(jnp.bfloat16)
 
 
+def gather_weights(w_self, w_neigh, gains):
+    feat_count = lax.axis_size("feat")
+    layer_count, depth, slice_width = w_self.shape
+    gain_rows = jnp.zeros((layer_count, HUB_PAD, slice_width), gains.dtype).at[:, 0, :].set(gains)
+    stacked = jnp.concatenate([w_self, w_neigh, gain_rows], axis=1)
+    own = lax.axis_index("feat")
+    pieces = [stacked]
+    for shift in range(1, feat_count):
+        pairs = [(source, (source + shift) % feat_count) for source in range(feat_count)]
+        pieces.append(lax.ppermute(stacked, "feat", pairs))
+    received = jnp.stack(pieces)
+    order = (own - jnp.arange(feat_count, dtype=jnp.int32)) % feat_count
+    ordered = jnp.take(received, jnp.argsort(order), axis=0)
+    full = ordered.transpose(1, 2, 0, 3).reshape(layer_count, stacked.shape[1], feat_count * slice_width)
+    return full[:, :depth], full[:, depth : 2 * depth], full[:, 2 * depth]
+
+
 def per_device(
     features,
     degree,
@@ -165,9 +182,7 @@
     slots, landing = routing(
         out_dest, recv_target, features.shape[0] // tile_side, lax.axis_size("dom")
     )
-    full_self = lax.all_gather(w_self, "feat", axis=2, tiled=True)
-    full_neigh = lax.all_gather(w_neigh, "feat", axis=2, tiled=True)
-    full_gains = lax.all_gather(gains, "feat", axis=1, tiled=True)
+    full_self, full_neigh, full_gains = gather_weights(w_self, w_neigh, gains)
     current = features
     own_rows = feat_to_rows(features)
     for layer_idx in range(w_self.shape[0]):

time: 409 us -> 397 us (0.971)
  waiting for transfers between devices: 275 us -> 214 us
  starting transfers between devices: 35 us -> 70.3 us
  local copies, waits for them, and re-layouts: 13.8 us -> 35.2 us
  other arithmetic: 3.01 us -> 19.8 us
  between operations: 13.8 us -> 0.44 us
  blocking collectives: 38.9 us -> 25.6 us
    all_to_all x2, waiting for transfers between devices: 267 us -> 167 us  [aggregate(): lax.all_to_all(payload, 'dom', split_axis=0, concat_axis=0, tiled=True)]
    ppermute x0 -> x7, waiting for transfers between devices: none -> 41.7 us  [gather_weights(): pieces.append(lax.ppermute(stacked, 'feat', pairs))]
    ppermute x0 -> x7, starting transfers between devices: none -> 37.4 us  [gather_weights(): pieces.append(lax.ppermute(stacked, 'feat', pairs))]
    unnamed x22 -> x39, local copies, waits for them, and re-layouts: 0.81 us -> 13 us
    all_gather x1 -> x0, blocking collectives: 11 us -> none  [per_device(): full_gains = lax.all_gather(gains, 'feat', axis=1, tiled=True)]
    reshape x0 -> x1, other arithmetic: none -> 8.99 us  [gather_weights(): ordered.transpose(1, 2, 0, 3)]
    gather x0 -> x1, local copies, waits for them, and re-layouts: none -> 8.11 us  [gather_weights(): ordered = jnp.take(received, jnp.argsort(order), axis=0)]
  transfers between devices with their start and end apart: 6 -> 11, of which waited for: 3 -> 8; matrix products, arithmetic and copies ran while one was open for 4% -> 12% of each run, Pallas kernels for 2% -> 2%
where the time goes in v5:
time: 397 us; the launch traced here: 395 us
  waiting for transfers between devices  214 us (54%)
  starting transfers between devices  70.3 us (18%)
  local copies, waits for them, and re-layouts  35.2 us (9%)
  blocking collectives  25.6 us (6%)
  other arithmetic  19.8 us (5%)
  matrix products  15.7 us (4%)
  Pallas kernels  13.7 us (3%)
    all_to_all x2, waiting for transfers between devices, aggregate(): lax.all_to_all(payload, 'dom', split_axis=0, concat_axis=0, tiled=True)  167 us
    ppermute x7, waiting for transfers between devices, gather_weights(): pieces.append(lax.ppermute(stacked, 'feat', pairs))  41.7 us
    ppermute x7, starting transfers between devices, gather_weights(): pieces.append(lax.ppermute(stacked, 'feat', pairs))  37.4 us
    all_to_all x2, starting transfers between devices, aggregate(): lax.all_to_all(payload, 'dom', split_axis=0, concat_axis=0, tiled=True)  23.9 us
    all_to_all x2, blocking collectives, rows_to_feat(): lax.all_to_all(pieces, 'feat', split_axis=0, concat_axis=0, tiled=True)  17 us
    pallas_call x2, Pallas kernels, build_payload(): pl.pallas_call(payload_kernel, out_shape=jax.ShapeDtypeStruct((node_count...  13.7 us
    unnamed x39, local copies, waits for them, and re-layouts  13 us
    all_to_all x2, starting transfers between devices, feat_to_rows(): lax.all_to_all(pieces, 'feat', split_axis=0, concat_axis=0, tiled=True)  9.02 us
  transfers between devices with their start and end apart: 11, of which 8 were waited for; matrix products, arithmetic and copies ran while one was open for 12% of the time, Pallas kernels for 2%

profile of v5, /device:TPU:40, one launch (start us, length us, event | category | flops | bytes accessed | tf_op | source)
XLA Modules:
  0.0 395.2 jit_solution(5487254771459106741)
XLA Ops:
  0.0 4.4 %all-to-all-start = ((bf16[8,64,128]{2,1,0:T(8,128)(2,1)}), bf16[8,64,128]{2,1,0:T(8,128)(2,1)S(1)}, u32[]{:S(2)}, u32[]{:S(2)}) async-start(bf16[8,64,128]{2,1,0:T(8,128)(2,1)} %bitcast.145), calls=%async_computation | async-start | bytes 262144 | tf_op jit(solution)/shard_map/all_to_all | solution.py:126
  4.4 0.7 compare_select_fusion
  5.1 0.7 compare_select_fusion.1
  5.8 1.5 gather_fusion.1
  7.2 0.9 convert_reduce_fusion
  8.1 0.6 scatter.11.hub_ref
  8.8 1.2 multiply_add_fusion.slot_ref
  9.9 6.9 %shard_map.136 = bf16[64,272,128]{2,1,0:T(8,128)(2,1)} custom-call(s32[64]{0:T(128)} %multiply_add_fusion.slot_ref, s32[64]{0:T(128)} %src_ref.3, bf16[64,128,128]{2,1,0:T(8,128)(2,1)} %tiles_ref.3, bf16[4,128,128]{2,1,0:T(8,128)(2,1)} %bitcast.146, bf16[16,128]{1,0:T(8,128)(2,1)} %scatter.11.hub_ref), custom_call_target="tpu_custom_call" | custom-call | tf_op jit(solution)/shard_map/pallas_call | solution.py:58
  16.9 16.4 %all-to-all-start.1 = ((bf16[64,272,128]{2,1,0:T(8,128)(2,1)}), bf16[64,272,128]{2,1,0:T(8,128)(2,1)}, u32[]{:S(2)}, u32[]{:S(2)}) async-start(bf16[64,272,128]{2,1,0:T(8,128)(2,1)} %shard_map.136), calls=%async_computation.1 | async-start | bytes 8912896 | tf_op jit(solution)/shard_map/all_to_all | solution.py:104
  33.4 1.1 fusion.25
  34.5 3.9 collective-permute-start.1
  38.4 4.0 %collective-permute-start.2 = (bf16[2,2064,128]{2,1,0:T(8,128)(2,1)}, bf16[2,2064,128]{2,1,0:T(8,128)(2,1)}, u32[]{:S(2)}, u32[]{:S(2)}) collective-permute-start(bf16[2,2064,128]{2,1,0:T(8,128)(2,1)} %fusion.25), channel_id=1, source_target_pairs={{0,3},{1,4},{2,5},{3,6},{4,7},{5,0},{6,1},{7,2},{8,11},{9,12},{10,... | collective-permute-start | bytes 3170312 | tf_op jit(solution)/shard_map/ppermute | solution.py:157
  42.4 4.0 %collective-permute-start.3 = (bf16[2,2064,128]{2,1,0:T(8,128)(2,1)}, bf16[2,2064,128]{2,1,0:T(8,128)(2,1)}, u32[]{:S(2)}, u32[]{:S(2)}) collective-permute-start(bf16[2,2064,128]{2,1,0:T(8,128)(2,1)} %fusion.25), channel_id=1, source_target_pairs={{0,4},{1,5},{2,6},{3,7},{4,0},{5,1},{6,2},{7,3},{8,12},{9,13},{10,... | collective-permute-start | bytes 3170312 | tf_op jit(solution)/shard_map/ppermute | solution.py:157
  46.4 3.4 collective-permute-start.4
  49.8 0.6 gather_fusion.2
  50.5 1.0 sort.17
  52.1 0.5 compare_select_fusion.2
  52.9 0.8 copy.59
  53.8 0.7 convert_element_type.47
  54.5 0.7 compare_and_fusion
  55.1 1.7 bitcast_dynamic-update-slice_fusion.7
  56.9 0.6 pad_clamp_fusion.2
  57.5 1.0 fusion.36
  58.5 0.6 collective-permute-done
  59.1 3.9 collective-permute-start.5
  63.1 2.3 bitcast_dynamic-update-slice_fusion.6
  65.4 18.2 %collective-permute-start.6 = (bf16[2,2064,128]{2,1,0:T(8,128)(2,1)}, bf16[2,2064,128]{2,1,0:T(8,128)(2,1)S(1)}, u32[]{:S(2)}, u32[]{:S(2)}) collective-permute-start(bf16[2,2064,128]{2,1,0:T(8,128)(2,1)} %fusion.25), channel_id=1, source_target_pairs={{0,7},{1,0},{2,1},{3,2},{4,3},{5,4},{6,5},{7,6},{8,15},{9,8},{10,9... | collective-permute-start | bytes 3170312 | tf_op jit(solution)/shard_map/ppermute | solution.py:157
  83.5 2.3 bitcast_dynamic-update-slice_fusion.5
  85.8 20.1 %collective-permute-done.2 = bf16[2,2064,128]{2,1,0:T(8,128)(2,1)} collective-permute-done((bf16[2,2064,128]{2,1,0:T(8,128)(2,1)}, bf16[2,2064,128]{2,1,0:T(8,128)(2,1)}, u32[]{:S(2)}, u32[]{:S(2)}) %collective-permute-start.2) | collective-permute-done | bytes 1056800 | tf_op jit(solution)/shard_map/ppermute | solution.py:157
  105.9 2.3 bitcast_dynamic-update-slice_fusion.4
  108.2 2.8 collective-permute-done.3
  110.9 2.3 bitcast_dynamic-update-slice_fusion.3
  113.2 14.7 %collective-permute-done.4 = bf16[2,2064,128]{2,1,0:T(8,128)(2,1)S(1)} collective-permute-done((bf16[2,2064,128]{2,1,0:T(8,128)(2,1)}, bf16[2,2064,128]{2,1,0:T(8,128)(2,1)S(1)}, u32[]{:S(2)}, u32[]{:S(2)}) %collective-permute-start.4) | collective-permute-done | bytes 1056800 | tf_op jit(solution)/shard_map/ppermute | solution.py:157
  127.9 1.1 bitcast_dynamic-update-slice_fusion.2
  129.0 1.0 bitcast_dynamic-update-slice_fusion.1
  130.1 3.5 collective-permute-done.6
  133.5 1.1 bitcast_dynamic-update-slice_fusion
  134.7 8.1 %gather_fusion = bf16[8,2,2064,128]{3,2,1,0:T(8,128)(2,1)} fusion(bf16[8,2,2064,128]{3,2,1,0:T(8,128)(2,1)} %bitcast_dynamic-update-slice_fusion, s32[1024]{0:T(1024)S(1)} %pad_clamp_fusion.2), kind=kCustom, calls=%fused_computation | custom fusion | bytes 16908320 | tf_op jit(solution)/shard_map/jit(_take)/gather | solution.py:160
  142.8 9.0 %copy_bitcast_fusion = bf16[2,2064,1024]{2,1,0:T(8,128)(2,1)} fusion(bf16[8,2,2064,128]{3,2,1,0:T(8,128)(2,1)} %gather_fusion, pred[8]{0:T(512)(128)(4,1)S(1)} %compare_and_fusion), kind=kLoop, calls=%fused_computation.5 | loop fusion | flops 4227072 | bytes 16908296 | tf_op jit(solution)/shard_map/reshape | solution.py:161
  151.8 31.6 %all-to-all-done.1 = bf16[64,272,128]{2,1,0:T(8,128)(2,1)} async-done(((bf16[64,272,128]{2,1,0:T(8,128)(2,1)}), bf16[64,272,128]{2,1,0:T(8,128)(2,1)}, u32[]{:S(2)}, u32[]{:S(2)}) %all-to-all-start.1) | async-done | bytes 4456480 | tf_op jit(solution)/shard_map/all_to_all | solution.py:104
  183.3 2.5 slice.115
  185.8 2.3 fusion.13
  188.3 0.9 slice.116
  189.5 0.8 copy.65
  190.2 4.6 %all-to-all-start.2 = ((bf16[8,64,128]{2,1,0:T(8,128)(2,1)}), bf16[8,64,128]{2,1,0:T(8,128)(2,1)S(1)}, u32[]{:S(2)}, u32[]{:S(2)}) async-start(bf16[8,64,128]{2,1,0:T(8,128)(2,1)} %bitcast.24), calls=%async_computation.2 | async-start | bytes 262144 | tf_op jit(solution)/shard_map/all_to_all | solution.py:126
  194.8 0.7 slice_convert_fusion.1
  195.6 5.4 %all-to-all-done.2 = bf16[8,64,128]{2,1,0:T(8,128)(2,1)S(1)} async-done(((bf16[8,64,128]{2,1,0:T(8,128)(2,1)}), bf16[8,64,128]{2,1,0:T(8,128)(2,1)S(1)}, u32[]{:S(2)}, u32[]{:S(2)}) %all-to-all-start.2) | async-done | bytes 131104 | tf_op jit(solution)/shard_map/all_to_all | solution.py:126
  201.0 2.1 fusion.7
  203.0 2.2 multiply_reduce_fusion.1
  205.4 8.5 %all_to_all.35 = bf16[8,64,128]{2,1,0:T(8,128)(2,1)S(1)} all-to-all(bf16[8,64,128]{2,1,0:T(8,128)(2,1)S(1)} %bitcast_bitcast_fusion.1), channel_id=1, replica_groups=mesh['dom'=64,'feat'=8] {'feat'}, dimensions={0} | all-to-all | bytes 262144 | tf_op jit(solution)/shard_map/all_to_all | solution.py:134
  213.9 0.6 gather_fusion.3
  214.4 0.6 scatter.14.hub_ref
  215.0 6.9 %shard_map.137 = bf16[64,272,128]{2,1,0:T(8,128)(2,1)} custom-call(s32[64]{0:T(128)} %multiply_add_fusion.slot_ref, s32[64]{0:T(128)} %src_ref.3, bf16[64,128,128]{2,1,0:T(8,128)(2,1)} %tiles_ref.3, bf16[4,128,128]{2,1,0:T(8,128)(2,1)} %bitcast.149, bf16[16,128]{1,0:T(8,128)(2,1)} %scatter.14.hub_ref), custom_call_target="tpu_custom_call" | custom-call | tf_op jit(solution)/shard_map/pallas_call | solution.py:58
  221.9 7.5 %all-to-all-start.4 = ((bf16[64,272,128]{2,1,0:T(8,128)(2,1)}), bf16[64,272,128]{2,1,0:T(8,128)(2,1)}, u32[]{:S(2)}, u32[]{:S(2)}) async-start(bf16[64,272,128]{2,1,0:T(8,128)(2,1)} %shard_map.137), calls=%async_computation.4 | async-start | bytes 8912896 | tf_op jit(solution)/shard_map/all_to_all | solution.py:104
  229.4 0.6 gather_fusion.4
  231.0 135.8 %all-to-all-done.4 = bf16[64,272,128]{2,1,0:T(8,128)(2,1)} async-done(((bf16[64,272,128]{2,1,0:T(8,128)(2,1)}), bf16[64,272,128]{2,1,0:T(8,128)(2,1)}, u32[]{:S(2)}, u32[]{:S(2)}) %all-to-all-start.4) | async-done | bytes 4456480 | tf_op jit(solution)/shard_map/all_to_all | solution.py:104
  366.8 2.5 slice.119
  369.3 2.3 fusion.16
  371.8 0.9 slice.120
  373.1 8.5 %all_to_all.36 = bf16[8,64,128]{2,1,0:T(8,128)(2,1)S(1)} all-to-all(bf16[8,64,128]{2,1,0:T(8,128)(2,1)S(1)} %bitcast.152), channel_id=1, replica_groups=mesh['dom'=64,'feat'=8] {'feat'}, dimensions={0} | all-to-all | bytes 262144 | tf_op jit(solution)/shard_map/all_to_all | solution.py:126
  381.6 2.1 fusion.5
  383.7 2.2 multiply_reduce_fusion
  386.0 8.5 %all_to_all.37 = bf16[8,64,128]{2,1,0:T(8,128)(2,1)S(1)} all-to-all(bf16[8,64,128]{2,1,0:T(8,128)(2,1)S(1)} %bitcast_bitcast_fusion), channel_id=1, replica_groups=mesh['dom'=64,'feat'=8] {'feat'}, dimensions={0} | all-to-all | bytes 262144 | tf_op jit(solution)/shard_map/all_to_all | solution.py:134
  394.5 0.7 copy.114
  (55 shorter events, 3.0 us)
Async XLA Ops:
  0.0 51.5 %copy-start = (bf16[8,128,128]{2,1,0:T(8,128)(2,1)S(1)}, bf16[8,128,128]{2,1,0:T(8,128)(2,1)}, u32[]{:S(2)}) copy-start(bf16[8,128,128]{2,1,0:T(8,128)(2,1)} %param.26) | copy-start | bytes 786436
  0.0 16.8 %all-to-all-start = ((bf16[8,64,128]{2,1,0:T(8,128)(2,1)}), bf16[8,64,128]{2,1,0:T(8,128)(2,1)S(1)}, u32[]{:S(2)}, u32[]{:S(2)}) async-start(bf16[8,64,128]{2,1,0:T(8,128)(2,1)} %bitcast.145), calls=%async_computation | async-start | bytes 262144 | tf_op jit(solution)/shard_map/all_to_all | solution.py:126
  16.8 16.5 %copy-start.13 = (bf16[2,128]{1,0:T(2,128)(2,1)S(1)}, bf16[2,128]{1,0:T(2,128)(2,1)}, u32[]{:S(2)}) copy-start(bf16[2,128]{1,0:T(2,128)(2,1)} %param.33) | copy-start | bytes 1540
  16.8 16.5 %copy-start.4 = (bf16[2,1024,128]{2,1,0:T(8,128)(2,1)S(1)}, bf16[2,1024,128]{2,1,0:T(8,128)(2,1)}, u32[]{:S(2)}) copy-start(bf16[2,1024,128]{2,1,0:T(8,128)(2,1)} %param.32) | copy-start | bytes 1572868
  16.8 16.5 %copy-start.5 = (bf16[2,1024,128]{2,1,0:T(8,128)(2,1)S(1)}, bf16[2,1024,128]{2,1,0:T(8,128)(2,1)}, u32[]{:S(2)}) copy-start(bf16[2,1024,128]{2,1,0:T(8,128)(2,1)} %param.31) | copy-start | bytes 1572868
  16.8 33.0 %copy-start.1 = (bf16[512,128]{1,0:T(8,128)(2,1)S(1)}, bf16[512,128]{1,0:T(8,128)(2,1)}, u32[]{:S(2)}) copy-start(bf16[512,128]{1,0:T(8,128)(2,1)} %param.20) | copy-start | bytes 393220
  16.9 166.5 %all-to-all-start.1 = ((bf16[64,272,128]{2,1,0:T(8,128)(2,1)}), bf16[64,272,128]{2,1,0:T(8,128)(2,1)}, u32[]{:S(2)}, u32[]{:S(2)}) async-start(bf16[64,272,128]{2,1,0:T(8,128)(2,1)} %shard_map.136), calls=%async_computation.1 | async-start | bytes 8912896 | tf_op jit(solution)/shard_map/all_to_all | solution.py:104
  33.3 16.5 %copy-start.8 = (bf16[2,1,128]{2,1,0:T(2,128)(2,1)}, bf16[2,1,128]{2,1,0:T(2,128)(2,1)S(1)}, u32[]{:S(2)}) copy-start(bf16[2,1,128]{2,1,0:T(2,128)(2,1)S(1)} %copy.77) | copy-start | bytes 1540
  34.5 24.6 %collective-permute-start = (bf16[2,2064,128]{2,1,0:T(8,128)(2,1)}, bf16[2,2064,128]{2,1,0:T(8,128)(2,1)}, u32[]{:S(2)}, u32[]{:S(2)}) collective-permute-start(bf16[2,2064,128]{2,1,0:T(8,128)(2,1)} %fusion.25), channel_id=1, source_target_pairs={{0,1},{1,2},{2,3},{3,4},{4,5},{5,6},{6,7},{7,0},{8,9},{9,10},{10,1... | collective-permute-start | bytes 3170312 | tf_op jit(solution)/shard_map/ppermute | solution.py:157
  34.5 30.9 %collective-permute-start.1 = (bf16[2,2064,128]{2,1,0:T(8,128)(2,1)}, bf16[2,2064,128]{2,1,0:T(8,128)(2,1)}, u32[]{:S(2)}, u32[]{:S(2)}) collective-permute-start(bf16[2,2064,128]{2,1,0:T(8,128)(2,1)} %fusion.25), channel_id=1, source_target_pairs={{0,2},{1,3},{2,4},{3,5},{4,6},{5,7},{6,0},{7,1},{8,10},{9,11},{10,... | collective-permute-start | bytes 3170312 | tf_op jit(solution)/shard_map/ppermute | solution.py:157
  38.4 67.5 %collective-permute-start.2 = (bf16[2,2064,128]{2,1,0:T(8,128)(2,1)}, bf16[2,2064,128]{2,1,0:T(8,128)(2,1)}, u32[]{:S(2)}, u32[]{:S(2)}) collective-permute-start(bf16[2,2064,128]{2,1,0:T(8,128)(2,1)} %fusion.25), channel_id=1, source_target_pairs={{0,3},{1,4},{2,5},{3,6},{4,7},{5,0},{6,1},{7,2},{8,11},{9,12},{10,... | collective-permute-start | bytes 3170312 | tf_op jit(solution)/shard_map/ppermute | solution.py:157
  42.4 68.5 %collective-permute-start.3 = (bf16[2,2064,128]{2,1,0:T(8,128)(2,1)}, bf16[2,2064,128]{2,1,0:T(8,128)(2,1)}, u32[]{:S(2)}, u32[]{:S(2)}) collective-permute-start(bf16[2,2064,128]{2,1,0:T(8,128)(2,1)} %fusion.25), channel_id=1, source_target_pairs={{0,4},{1,5},{2,6},{3,7},{4,0},{5,1},{6,2},{7,3},{8,12},{9,13},{10,... | collective-permute-start | bytes 3170312 | tf_op jit(solution)/shard_map/ppermute | solution.py:157
  46.4 81.5 %collective-permute-start.4 = (bf16[2,2064,128]{2,1,0:T(8,128)(2,1)}, bf16[2,2064,128]{2,1,0:T(8,128)(2,1)S(1)}, u32[]{:S(2)}, u32[]{:S(2)}) collective-permute-start(bf16[2,2064,128]{2,1,0:T(8,128)(2,1)} %fusion.25), channel_id=1, source_target_pairs={{0,5},{1,6},{2,7},{3,0},{4,1},{5,2},{6,3},{7,4},{8,13},{9,14},{10,... | collective-permute-start | bytes 3170312 | tf_op jit(solution)/shard_map/ppermute | solution.py:157
  51.5 0.6 copy-start.14
  53.8 132.0 %copy-start.6 = (s32[128]{0:T(128)}, s32[128]{0:T(128)S(1)}, u32[]{:S(2)}) copy-start(s32[128]{0:T(128)S(1)} %eq.25) | copy-start | bytes 1540
  54.5 134.8 %copy-start.9 = (f32[512]{0:T(512)}, f32[512]{0:T(512)S(1)}, u32[]{:S(2)}) copy-start(f32[512]{0:T(512)S(1)} %convert_element_type.47) | copy-start | bytes 6148
  59.1 69.9 %collective-permute-start.5 = (bf16[2,2064,128]{2,1,0:T(8,128)(2,1)}, bf16[2,2064,128]{2,1,0:T(8,128)(2,1)S(1)}, u32[]{:S(2)}, u32[]{:S(2)}) collective-permute-start(bf16[2,2064,128]{2,1,0:T(8,128)(2,1)} %fusion.25), channel_id=1, source_target_pairs={{0,6},{1,7},{2,0},{3,1},{4,2},{5,3},{6,4},{7,5},{8,14},{9,15},{10,... | collective-permute-start | bytes 3170312 | tf_op jit(solution)/shard_map/ppermute | solution.py:157
  65.4 68.2 %collective-permute-start.6 = (bf16[2,2064,128]{2,1,0:T(8,128)(2,1)}, bf16[2,2064,128]{2,1,0:T(8,128)(2,1)S(1)}, u32[]{:S(2)}, u32[]{:S(2)}) collective-permute-start(bf16[2,2064,128]{2,1,0:T(8,128)(2,1)} %fusion.25), channel_id=1, source_target_pairs={{0,7},{1,0},{2,1},{3,2},{4,3},{5,4},{6,5},{7,6},{8,15},{9,8},{10,9... | collective-permute-start | bytes 3170312 | tf_op jit(solution)/shard_map/ppermute | solution.py:157
  185.8 3.5 copy-start.12
  190.2 10.7 %all-to-all-start.2 = ((bf16[8,64,128]{2,1,0:T(8,128)(2,1)}), bf16[8,64,128]{2,1,0:T(8,128)(2,1)S(1)}, u32[]{:S(2)}, u32[]{:S(2)}) async-start(bf16[8,64,128]{2,1,0:T(8,128)(2,1)} %bitcast.24), calls=%async_computation.2 | async-start | bytes 262144 | tf_op jit(solution)/shard_map/all_to_all | solution.py:126
  213.9 1.2 copy-start.2
  221.9 7.5 %copy-start.3 = (bf16[8,64,128]{2,1,0:T(8,128)(2,1)S(1)}, bf16[8,64,128]{2,1,0:T(8,128)(2,1)}, u32[]{:S(2)}) copy-start(bf16[8,64,128]{2,1,0:T(8,128)(2,1)} %copy-done.2) | copy-start | bytes 393220
  221.9 8.7 %copy-start.11 = (s32[8]{0:T(128)S(1)}, s32[8]{0:T(128)}, u32[]{:S(2)}) copy-start(s32[8]{0:T(128)} %param.24) | copy-start | bytes 100
  221.9 144.9 %all-to-all-start.4 = ((bf16[64,272,128]{2,1,0:T(8,128)(2,1)}), bf16[64,272,128]{2,1,0:T(8,128)(2,1)}, u32[]{:S(2)}, u32[]{:S(2)}) async-start(bf16[64,272,128]{2,1,0:T(8,128)(2,1)} %shard_map.137), calls=%async_computation.4 | async-start | bytes 8912896 | tf_op jit(solution)/shard_map/all_to_all | solution.py:104
  230.9 138.3 %copy-start.7 = (s32[128]{0:T(128)S(1)}, s32[128]{0:T(128)}, u32[]{:S(2)}) copy-start(s32[128]{0:T(128)} %copy-done.6) | copy-start | bytes 1540
  369.3 3.4 copy-start.10

commit v6 on v5

--- a/solution.py
+++ b/solution.py
@@ -150,16 +150,20 @@
     layer_count, depth, slice_width = w_self.shape
     gain_rows = jnp.zeros((layer_count, HUB_PAD, slice_width), gains.dtype).at[:, 0, :].set(gains)
     stacked = jnp.concatenate([w_self, w_neigh, gain_rows], axis=1)
-    own = lax.axis_index("feat")
     pieces = [stacked]
     for shift in range(1, feat_count):
         pairs = [(source, (source + shift) % feat_count) for source in range(feat_count)]
         pieces.append(lax.ppermute(stacked, "feat", pairs))
-    received = jnp.stack(pieces)
-    order = (own - jnp.arange(feat_count, dtype=jnp.int32)) % feat_count
-    ordered = jnp.take(received, jnp.argsort(order), axis=0)
-    full = ordered.transpose(1, 2, 0, 3).reshape(layer_count, stacked.shape[1], feat_count * slice_width)
+    full = jnp.concatenate(pieces, axis=2)
     return full[:, :depth], full[:, depth : 2 * depth], full[:, 2 * depth]
+
+
+def natural_columns(shifted):
+    feat_count = lax.axis_size("feat")
+    row_count, width = shifted.shape
+    order = (lax.axis_index("feat") - jnp.arange(feat_count, dtype=jnp.int32)) % feat_count
+    blocks = shifted.reshape(row_count, feat_count, width // feat_count)
+    return jnp.take(blocks, order, axis=1).reshape(row_count, width)
 
 
 def per_device(
@@ -203,12 +207,14 @@
         if anchored is not None:
             own_rows = anchored
         neigh_rows = feat_to_rows(neighbours)
-        own_rows = mix(
-            own_rows,
-            neigh_rows,
-            full_self[layer_idx],
-            full_neigh[layer_idx],
-            full_gains[layer_idx],
+        own_rows = natural_columns(
+            mix(
+                own_rows,
+                neigh_rows,
+                full_self[layer_idx],
+                full_neigh[layer_idx],
+                full_gains[layer_idx],
+            )
         )
         current = rows_to_feat(own_rows)
     return current

time: 397 us -> 397 us (level)
  waiting for transfers between devices: 214 us -> 228 us
  other arithmetic: 19.8 us -> 6.6 us
  local copies, waits for them, and re-layouts: 35.2 us -> 29 us
  blocking collectives: 25.6 us -> 30.2 us
    all_to_all x2, waiting for transfers between devices: 167 us -> 177 us  [aggregate(): lax.all_to_all(payload, 'dom', split_axis=0, concat_axis=0, tiled=True)]
    reshape x1 -> x2, other arithmetic: 8.99 us -> 0.2 us  [natural_columns(): blocks = shifted.reshape(row_count, feat_count, width // feat_count)]
    gather x1 -> x2, local copies, waits for them, and re-layouts: 8.11 us -> 1.39 us  [natural_columns(): return jnp.take(blocks, order, axis=1).reshape(row_count, width)]
    all_to_all x1, blocking collectives: 8.52 us -> 13.2 us  [feat_to_rows(): lax.all_to_all(pieces, 'feat', split_axis=0, concat_axis=0, tiled=True)]
    unnamed x39 -> x45, local copies, waits for them, and re-layouts: 13 us -> 13.2 us
  transfers between devices with their start and end apart: 11 -> 11, of which waited for: 8 -> 8; matrix products, arithmetic and copies ran while one was open for 12% -> 7% of each run, Pallas kernels for 2% -> 2%
where the time goes in v6:
time: 397 us; the launch traced here: 396 us
  waiting for transfers between devices  228 us (57%)
  starting transfers between devices  72.4 us (18%)
  blocking collectives  30.2 us (8%)
  local copies, waits for them, and re-layouts  29 us (7%)
  matrix products  15.7 us (4%)
  Pallas kernels  13.7 us (3%)
  other arithmetic  6.6 us (2%)
    all_to_all x2, waiting for transfers between devices, aggregate(): lax.all_to_all(payload, 'dom', split_axis=0, concat_axis=0, tiled=True)  177 us
    ppermute x7, waiting for transfers between devices, gather_weights(): pieces.append(lax.ppermute(stacked, 'feat', pairs))  45.2 us
    ppermute x7, starting transfers between devices, gather_weights(): pieces.append(lax.ppermute(stacked, 'feat', pairs))  37.3 us
    all_to_all x2, starting transfers between devices, aggregate(): lax.all_to_all(payload, 'dom', split_axis=0, concat_axis=0, tiled=True)  23.9 us
    all_to_all x2, blocking collectives, rows_to_feat(): lax.all_to_all(pieces, 'feat', split_axis=0, concat_axis=0, tiled=True)  17 us
    pallas_call x2, Pallas kernels, build_payload(): pl.pallas_call(payload_kernel, out_shape=jax.ShapeDtypeStruct((node_count...  13.7 us
    unnamed x45, local copies, waits for them, and re-layouts  13.2 us
    all_to_all x1, blocking collectives, feat_to_rows(): lax.all_to_all(pieces, 'feat', split_axis=0, concat_axis=0, tiled=True)  13.2 us
  transfers between devices with their start and end apart: 11, of which 8 were waited for; matrix products, arithmetic and copies ran while one was open for 7% of the time, Pallas kernels for 2%

profile of v6, /device:TPU:40, one launch (start us, length us, event | category | flops | bytes accessed | tf_op | source)
XLA Modules:
  0.0 396.0 jit_solution(10230335917706176958)
XLA Ops:
  0.0 4.4 %all-to-all-start = ((bf16[8,64,128]{2,1,0:T(8,128)(2,1)}), bf16[8,64,128]{2,1,0:T(8,128)(2,1)S(1)}, u32[]{:S(2)}, u32[]{:S(2)}) async-start(bf16[8,64,128]{2,1,0:T(8,128)(2,1)} %bitcast.134), calls=%async_computation | async-start | bytes 262144 | tf_op jit(solution)/shard_map/all_to_all | solution.py:126
  4.4 0.7 compare_select_fusion.2
  5.1 1.5 gather_fusion
  6.6 0.9 convert_reduce_fusion
  7.5 0.6 scatter.11.hub_ref
  8.1 1.2 multiply_add_fusion.slot_ref
  9.3 6.8 %shard_map.136 = bf16[64,272,128]{2,1,0:T(8,128)(2,1)} custom-call(s32[64]{0:T(128)} %multiply_add_fusion.slot_ref, s32[64]{0:T(128)} %src_ref.3, bf16[64,128,128]{2,1,0:T(8,128)(2,1)} %tiles_ref.3, bf16[4,128,128]{2,1,0:T(8,128)(2,1)} %bitcast.135, bf16[16,128]{1,0:T(8,128)(2,1)} %scatter.11.hub_ref), custom_call_target="tpu_custom_call" | custom-call | tf_op jit(solution)/shard_map/pallas_call | solution.py:58
  16.2 16.4 %all-to-all-start.1 = ((bf16[64,272,128]{2,1,0:T(8,128)(2,1)}), bf16[64,272,128]{2,1,0:T(8,128)(2,1)}, u32[]{:S(2)}, u32[]{:S(2)}) async-start(bf16[64,272,128]{2,1,0:T(8,128)(2,1)} %shard_map.136), calls=%async_computation.1 | async-start | bytes 8912896 | tf_op jit(solution)/shard_map/all_to_all | solution.py:104
  32.7 1.4 fusion.25
  34.1 3.9 collective-permute-start.1
  38.0 4.0 %collective-permute-start.2 = (bf16[2,2064,128]{2,1,0:T(8,128)(2,1)S(1)}, bf16[2,2064,128]{2,1,0:T(8,128)(2,1)}, u32[]{:S(2)}, u32[]{:S(2)}) collective-permute-start(bf16[2,2064,128]{2,1,0:T(8,128)(2,1)S(1)} %get-tuple-element.48), channel_id=1, source_target_pairs={{0,3},{1,4},{2,5},{3,6},{4,7},{5,0},{6,1},{7,2},{8,11},{9,12},{10,... | collective-permute-start | bytes 3170312 | tf_op jit(solution)/shard_map/ppermute | solution.py:156
  42.0 4.0 %collective-permute-start.3 = (bf16[2,2064,128]{2,1,0:T(8,128)(2,1)S(1)}, bf16[2,2064,128]{2,1,0:T(8,128)(2,1)}, u32[]{:S(2)}, u32[]{:S(2)}) collective-permute-start(bf16[2,2064,128]{2,1,0:T(8,128)(2,1)S(1)} %get-tuple-element.48), channel_id=1, source_target_pairs={{0,4},{1,5},{2,6},{3,7},{4,0},{5,1},{6,2},{7,3},{8,12},{9,13},{10,... | collective-permute-start | bytes 3170312 | tf_op jit(solution)/shard_map/ppermute | solution.py:156
  46.0 3.4 collective-permute-start.4
  49.4 0.6 pad_clamp_fusion
  50.0 0.6 gather_fusion.1
  50.7 0.3 convolution_bitcast_fusion.1
  51.0 0.2 copy.60
  51.2 0.8 copy.57
  52.2 0.7 convert_element_type.47
  52.9 1.0 fusion.39
  53.9 4.6 %collective-permute-done = bf16[2,2064,128]{2,1,0:T(8,128)(2,1)} collective-permute-done((bf16[2,2064,128]{2,1,0:T(8,128)(2,1)S(1)}, bf16[2,2064,128]{2,1,0:T(8,128)(2,1)}, u32[]{:S(2)}, u32[]{:S(2)}) %collective-permute-start) | collective-permute-done | bytes 1056800 | tf_op jit(solution)/shard_map/ppermute | solution.py:156
  58.5 3.9 collective-permute-start.5
  62.4 2.4 constant_dynamic-update-slice_fusion.6
  64.8 18.1 %collective-permute-start.6 = (bf16[2,2064,128]{2,1,0:T(8,128)(2,1)S(1)}, bf16[2,2064,128]{2,1,0:T(8,128)(2,1)S(1)}, u32[]{:S(2)}, u32[]{:S(2)}) collective-permute-start(bf16[2,2064,128]{2,1,0:T(8,128)(2,1)S(1)} %get-tuple-element.48), channel_id=1, source_target_pairs={{0,7},{1,0},{2,1},{3,2},{4,3},{5,4},{6,5},{7,6},{8,15},{9,8},{10,9... | collective-permute-start | bytes 3170312 | tf_op jit(solution)/shard_map/ppermute | solution.py:156
  82.9 2.4 constant_dynamic-update-slice_fusion.5
  85.3 20.0 %collective-permute-done.2 = bf16[2,2064,128]{2,1,0:T(8,128)(2,1)} collective-permute-done((bf16[2,2064,128]{2,1,0:T(8,128)(2,1)S(1)}, bf16[2,2064,128]{2,1,0:T(8,128)(2,1)}, u32[]{:S(2)}, u32[]{:S(2)}) %collective-permute-start.2) | collective-permute-done | bytes 1056800 | tf_op jit(solution)/shard_map/ppermute | solution.py:156
  105.3 2.3 constant_dynamic-update-slice_fusion.4
  107.6 2.7 collective-permute-done.3
  110.3 2.3 constant_dynamic-update-slice_fusion.3
  112.6 14.6 %collective-permute-done.4 = bf16[2,2064,128]{2,1,0:T(8,128)(2,1)S(1)} collective-permute-done((bf16[2,2064,128]{2,1,0:T(8,128)(2,1)S(1)}, bf16[2,2064,128]{2,1,0:T(8,128)(2,1)S(1)}, u32[]{:S(2)}, u32[]{:S(2)}) %collective-permute-start.4) | collective-permute-done | bytes 1056800 | tf_op jit(solution)/shard_map/ppermute | solution.py:156
  127.2 1.2 constant_dynamic-update-slice_fusion.2
  128.4 1.1 constant_dynamic-update-slice_fusion.1
  129.5 3.3 collective-permute-done.6
  132.8 1.1 constant_dynamic-update-slice_fusion
  133.9 46.6 %all-to-all-done.1 = bf16[64,272,128]{2,1,0:T(8,128)(2,1)} async-done(((bf16[64,272,128]{2,1,0:T(8,128)(2,1)}), bf16[64,272,128]{2,1,0:T(8,128)(2,1)}, u32[]{:S(2)}, u32[]{:S(2)}) %all-to-all-start.1) | async-done | bytes 4456480 | tf_op jit(solution)/shard_map/all_to_all | solution.py:104
  180.5 2.5 slice.117
  183.0 2.3 fusion.13
  185.5 0.9 slice.118
  186.7 0.8 copy.63
  187.4 6.8 %all-to-all-start.2 = ((bf16[8,64,128]{2,1,0:T(8,128)(2,1)}), bf16[8,64,128]{2,1,0:T(8,128)(2,1)S(1)}, u32[]{:S(2)}, u32[]{:S(2)}) async-start(bf16[8,64,128]{2,1,0:T(8,128)(2,1)} %bitcast.15), calls=%async_computation.2 | async-start | bytes 262144 | tf_op jit(solution)/shard_map/all_to_all | solution.py:126
  194.2 0.7 slice_convert_fusion.1
  194.9 5.4 %all-to-all-done.2 = bf16[8,64,128]{2,1,0:T(8,128)(2,1)S(1)} async-done(((bf16[8,64,128]{2,1,0:T(8,128)(2,1)}), bf16[8,64,128]{2,1,0:T(8,128)(2,1)S(1)}, u32[]{:S(2)}, u32[]{:S(2)}) %all-to-all-start.2) | async-done | bytes 131104 | tf_op jit(solution)/shard_map/all_to_all | solution.py:126
  200.3 2.1 fusion.7
  202.4 2.2 multiply_reduce_fusion.1
  204.7 0.7 gather_fusion.4
  205.5 8.5 %all_to_all.35 = bf16[8,64,128]{2,1,0:T(8,128)(2,1)S(1)} all-to-all(bf16[8,64,128]{2,1,0:T(8,128)(2,1)S(1)} %broadcast_select_fusion), channel_id=1, replica_groups=mesh['dom'=64,'feat'=8] {'feat'}, dimensions={0} | all-to-all | bytes 262144 | tf_op jit(solution)/shard_map/all_to_all | solution.py:134
  214.1 0.7 gather_fusion.2
  214.7 0.6 scatter.14.hub_ref
  215.3 6.9 %shard_map.137 = bf16[64,272,128]{2,1,0:T(8,128)(2,1)} custom-call(s32[64]{0:T(128)} %multiply_add_fusion.slot_ref, s32[64]{0:T(128)} %src_ref.3, bf16[64,128,128]{2,1,0:T(8,128)(2,1)} %tiles_ref.3, bf16[4,128,128]{2,1,0:T(8,128)(2,1)} %bitcast.138, bf16[16,128]{1,0:T(8,128)(2,1)} %scatter.14.hub_ref), custom_call_target="tpu_custom_call" | custom-call | tf_op jit(solution)/shard_map/pallas_call | solution.py:58
  222.2 7.5 %all-to-all-start.4 = ((bf16[64,272,128]{2,1,0:T(8,128)(2,1)}), bf16[64,272,128]{2,1,0:T(8,128)(2,1)}, u32[]{:S(2)}, u32[]{:S(2)}) async-start(bf16[64,272,128]{2,1,0:T(8,128)(2,1)} %shard_map.137), calls=%async_computation.4 | async-start | bytes 8912896 | tf_op jit(solution)/shard_map/all_to_all | solution.py:104
  229.7 0.7 gather_fusion.3
  230.5 0.3 convolution_bitcast_fusion
  230.8 0.2 copy.69
  231.1 0.4 fusion.37
  231.4 130.8 %all-to-all-done.4 = bf16[64,272,128]{2,1,0:T(8,128)(2,1)} async-done(((bf16[64,272,128]{2,1,0:T(8,128)(2,1)}), bf16[64,272,128]{2,1,0:T(8,128)(2,1)}, u32[]{:S(2)}, u32[]{:S(2)}) %all-to-all-start.4) | async-done | bytes 4456480 | tf_op jit(solution)/shard_map/all_to_all | solution.py:104
  362.2 2.5 slice.121
  364.7 2.3 fusion.16
  367.2 0.9 slice.122
  368.5 13.2 %all_to_all.36 = bf16[8,64,128]{2,1,0:T(8,128)(2,1)S(1)} all-to-all(bf16[8,64,128]{2,1,0:T(8,128)(2,1)S(1)} %bitcast.141), channel_id=1, replica_groups=mesh['dom'=64,'feat'=8] {'feat'}, dimensions={0} | all-to-all | bytes 262144 | tf_op jit(solution)/shard_map/all_to_all | solution.py:126
  381.6 2.1 fusion.5
  383.7 2.2 multiply_reduce_fusion
  386.1 0.7 gather_fusion.5
  386.9 8.5 %all_to_all.37 = bf16[8,64,128]{2,1,0:T(8,128)(2,1)S(1)} all-to-all(bf16[8,64,128]{2,1,0:T(8,128)(2,1)S(1)} %broadcast_select_fusion.1), channel_id=1, replica_groups=mesh['dom'=64,'feat'=8] {'feat'}, dimensions={0} | all-to-all | bytes 262144 | tf_op jit(solution)/shard_map/all_to_all | solution.py:134
  395.4 0.7 copy.118
  (59 shorter events, 1.5 us)
Async XLA Ops:
  0.0 50.7 %copy-start = (bf16[8,128,128]{2,1,0:T(8,128)(2,1)S(1)}, bf16[8,128,128]{2,1,0:T(8,128)(2,1)}, u32[]{:S(2)}) copy-start(bf16[8,128,128]{2,1,0:T(8,128)(2,1)} %param.28) | copy-start | bytes 786436
  0.0 16.1 %all-to-all-start = ((bf16[8,64,128]{2,1,0:T(8,128)(2,1)}), bf16[8,64,128]{2,1,0:T(8,128)(2,1)S(1)}, u32[]{:S(2)}, u32[]{:S(2)}) async-start(bf16[8,64,128]{2,1,0:T(8,128)(2,1)} %bitcast.134), calls=%async_computation | async-start | bytes 262144 | tf_op jit(solution)/shard_map/all_to_all | solution.py:126
  5.1 11.0 %copy-start.7 = (s32[1024]{0:T(1024)}, s32[1024]{0:T(1024)S(1)}, u32[]{:S(2)}) copy-start(s32[1024]{0:T(1024)S(1)} %pad_clamp_fusion.2) | copy-start | bytes 12292
  16.2 16.5 %copy-start.16 = (bf16[2,128]{1,0:T(2,128)(2,1)S(1)}, bf16[2,128]{1,0:T(2,128)(2,1)}, u32[]{:S(2)}) copy-start(bf16[2,128]{1,0:T(2,128)(2,1)} %param.35) | copy-start | bytes 1540
  16.2 16.5 %copy-start.4 = (bf16[2,1024,128]{2,1,0:T(8,128)(2,1)S(1)}, bf16[2,1024,128]{2,1,0:T(8,128)(2,1)}, u32[]{:S(2)}) copy-start(bf16[2,1024,128]{2,1,0:T(8,128)(2,1)} %param.34) | copy-start | bytes 1572868
  16.2 16.5 %copy-start.5 = (bf16[2,1024,128]{2,1,0:T(8,128)(2,1)S(1)}, bf16[2,1024,128]{2,1,0:T(8,128)(2,1)}, u32[]{:S(2)}) copy-start(bf16[2,1024,128]{2,1,0:T(8,128)(2,1)} %param.33) | copy-start | bytes 1572868
  16.2 33.2 %copy-start.17 = (s32[8]{0:T(128)S(1)}, s32[8]{0:T(128)}, u32[]{:S(2)}) copy-start(s32[8]{0:T(128)} %param.27) | copy-start | bytes 100
  16.2 33.8 %copy-start.1 = (bf16[512,128]{1,0:T(8,128)(2,1)S(1)}, bf16[512,128]{1,0:T(8,128)(2,1)}, u32[]{:S(2)}) copy-start(bf16[512,128]{1,0:T(8,128)(2,1)} %param.22) | copy-start | bytes 393220
  16.2 164.3 %all-to-all-start.1 = ((bf16[64,272,128]{2,1,0:T(8,128)(2,1)}), bf16[64,272,128]{2,1,0:T(8,128)(2,1)}, u32[]{:S(2)}, u32[]{:S(2)}) async-start(bf16[64,272,128]{2,1,0:T(8,128)(2,1)} %shard_map.136), calls=%async_computation.1 | async-start | bytes 8912896 | tf_op jit(solution)/shard_map/all_to_all | solution.py:104
  34.1 24.4 %collective-permute-start = (bf16[2,2064,128]{2,1,0:T(8,128)(2,1)S(1)}, bf16[2,2064,128]{2,1,0:T(8,128)(2,1)}, u32[]{:S(2)}, u32[]{:S(2)}) collective-permute-start(bf16[2,2064,128]{2,1,0:T(8,128)(2,1)S(1)} %get-tuple-element.48), channel_id=1, source_target_pairs={{0,1},{1,2},{2,3},{3,4},{4,5},{5,6},{6,7},{7,0},{8,9},{9,10},{10,1... | collective-permute-start | bytes 3170312 | tf_op jit(solution)/shard_map/ppermute | solution.py:156
  34.1 30.7 %collective-permute-start.1 = (bf16[2,2064,128]{2,1,0:T(8,128)(2,1)S(1)}, bf16[2,2064,128]{2,1,0:T(8,128)(2,1)}, u32[]{:S(2)}, u32[]{:S(2)}) collective-permute-start(bf16[2,2064,128]{2,1,0:T(8,128)(2,1)S(1)} %get-tuple-element.48), channel_id=1, source_target_pairs={{0,2},{1,3},{2,4},{3,5},{4,6},{5,7},{6,0},{7,1},{8,10},{9,11},{10,... | collective-permute-start | bytes 3170312 | tf_op jit(solution)/shard_map/ppermute | solution.py:156
  38.0 67.2 %collective-permute-start.2 = (bf16[2,2064,128]{2,1,0:T(8,128)(2,1)S(1)}, bf16[2,2064,128]{2,1,0:T(8,128)(2,1)}, u32[]{:S(2)}, u32[]{:S(2)}) collective-permute-start(bf16[2,2064,128]{2,1,0:T(8,128)(2,1)S(1)} %get-tuple-element.48), channel_id=1, source_target_pairs={{0,3},{1,4},{2,5},{3,6},{4,7},{5,0},{6,1},{7,2},{8,11},{9,12},{10,... | collective-permute-start | bytes 3170312 | tf_op jit(solution)/shard_map/ppermute | solution.py:156
  42.0 68.3 %collective-permute-start.3 = (bf16[2,2064,128]{2,1,0:T(8,128)(2,1)S(1)}, bf16[2,2064,128]{2,1,0:T(8,128)(2,1)}, u32[]{:S(2)}, u32[]{:S(2)}) collective-permute-start(bf16[2,2064,128]{2,1,0:T(8,128)(2,1)S(1)} %get-tuple-element.48), channel_id=1, source_target_pairs={{0,4},{1,5},{2,6},{3,7},{4,0},{5,1},{6,2},{7,3},{8,12},{9,13},{10,... | collective-permute-start | bytes 3170312 | tf_op jit(solution)/shard_map/ppermute | solution.py:156
  46.0 81.2 %collective-permute-start.4 = (bf16[2,2064,128]{2,1,0:T(8,128)(2,1)S(1)}, bf16[2,2064,128]{2,1,0:T(8,128)(2,1)S(1)}, u32[]{:S(2)}, u32[]{:S(2)}) collective-permute-start(bf16[2,2064,128]{2,1,0:T(8,128)(2,1)S(1)} %get-tuple-element.48), channel_id=1, source_target_pairs={{0,5},{1,6},{2,7},{3,0},{4,1},{5,2},{6,3},{7,4},{8,13},{9,14},{10,... | collective-permute-start | bytes 3170312 | tf_op jit(solution)/shard_map/ppermute | solution.py:156
  50.0 0.6 copy-start.6
  52.2 130.8 %copy-start.8 = (s32[128]{0:T(128)}, s32[128]{0:T(128)S(1)}, u32[]{:S(2)}) copy-start(s32[128]{0:T(128)S(1)} %eq.26) | copy-start | bytes 1540
  52.8 133.6 %copy-start.12 = (f32[512]{0:T(512)}, f32[512]{0:T(512)S(1)}, u32[]{:S(2)}) copy-start(f32[512]{0:T(512)S(1)} %convert_element_type.47) | copy-start | bytes 6148
  52.9 152.6 %copy-start.10 = (pred[8]{0:T(512)(128)(4,1)}, pred[8]{0:T(512)(128)(4,1)S(1)}, u32[]{:S(2)}) copy-start(pred[8]{0:T(512)(128)(4,1)S(1)} %compare_and_fusion) | copy-start | bytes 28
  58.5 69.9 %collective-permute-start.5 = (bf16[2,2064,128]{2,1,0:T(8,128)(2,1)S(1)}, bf16[2,2064,128]{2,1,0:T(8,128)(2,1)S(1)}, u32[]{:S(2)}, u32[]{:S(2)}) collective-permute-start(bf16[2,2064,128]{2,1,0:T(8,128)(2,1)S(1)} %get-tuple-element.48), channel_id=1, source_target_pairs={{0,6},{1,7},{2,0},{3,1},{4,2},{5,3},{6,4},{7,5},{8,14},{9,15},{10,... | collective-permute-start | bytes 3170312 | tf_op jit(solution)/shard_map/ppermute | solution.py:156
  64.8 68.0 %collective-permute-start.6 = (bf16[2,2064,128]{2,1,0:T(8,128)(2,1)S(1)}, bf16[2,2064,128]{2,1,0:T(8,128)(2,1)S(1)}, u32[]{:S(2)}, u32[]{:S(2)}) collective-permute-start(bf16[2,2064,128]{2,1,0:T(8,128)(2,1)S(1)} %get-tuple-element.48), channel_id=1, source_target_pairs={{0,7},{1,0},{2,1},{3,2},{4,3},{5,4},{6,5},{7,6},{8,15},{9,8},{10,9... | collective-permute-start | bytes 3170312 | tf_op jit(solution)/shard_map/ppermute | solution.py:156
  183.0 3.5 copy-start.15
  187.4 12.9 %all-to-all-start.2 = ((bf16[8,64,128]{2,1,0:T(8,128)(2,1)}), bf16[8,64,128]{2,1,0:T(8,128)(2,1)S(1)}, u32[]{:S(2)}, u32[]{:S(2)}) async-start(bf16[8,64,128]{2,1,0:T(8,128)(2,1)} %bitcast.15), calls=%async_computation.2 | async-start | bytes 262144 | tf_op jit(solution)/shard_map/all_to_all | solution.py:126
  214.0 1.3 copy-start.2
  222.2 7.5 %copy-start.3 = (bf16[8,64,128]{2,1,0:T(8,128)(2,1)S(1)}, bf16[8,64,128]{2,1,0:T(8,128)(2,1)}, u32[]{:S(2)}) copy-start(bf16[8,64,128]{2,1,0:T(8,128)(2,1)} %copy-done.2) | copy-start | bytes 393220
  222.2 8.8 %copy-start.14 = (s32[8]{0:T(128)S(1)}, s32[8]{0:T(128)}, u32[]{:S(2)}) copy-start(s32[8]{0:T(128)} %param.26) | copy-start | bytes 100
  222.2 140.0 %all-to-all-start.4 = ((bf16[64,272,128]{2,1,0:T(8,128)(2,1)}), bf16[64,272,128]{2,1,0:T(8,128)(2,1)}, u32[]{:S(2)}, u32[]{:S(2)}) async-start(bf16[64,272,128]{2,1,0:T(8,128)(2,1)} %shard_map.137), calls=%async_computation.4 | async-start | bytes 8912896 | tf_op jit(solution)/shard_map/all_to_all | solution.py:104
  231.4 133.2 %copy-start.9 = (s32[128]{0:T(128)S(1)}, s32[128]{0:T(128)}, u32[]{:S(2)}) copy-start(s32[128]{0:T(128)} %copy-done.8) | copy-start | bytes 1540
  364.7 3.5 copy-start.13
  364.7 19.0 %copy-start.11 = (pred[8]{0:T(512)(128)(4,1)S(1)}, pred[8]{0:T(512)(128)(4,1)}, u32[]{:S(2)}) copy-start(pred[8]{0:T(512)(128)(4,1)} %copy-done.10) | copy-start | bytes 28

commit v7 on v6

--- a/solution.py
+++ b/solution.py
@@ -10,27 +10,35 @@
 
 
 def routing(out_dest, recv_target, block_count, node_count):
-    capacity = recv_target.shape[2]
-    destination = out_dest[:, 0]
-    positions = jnp.arange(destination.shape[0], dtype=jnp.int32)
-    matches = (destination[None, :] == destination[:, None]) & (
-        positions[None, :] < positions[:, None]
-    )
-    slot_rank = jnp.sum(matches.astype(jnp.int32), axis=1)
-    slots = destination * capacity + slot_rank
     targets = recv_target[0].reshape(-1)
     block_ids = jnp.arange(block_count, dtype=jnp.int32)
     landing = (targets[None, :] == block_ids[:, None]).astype(jnp.bfloat16)
-    return slots.astype(jnp.int32), landing
-
-
-def payload_kernel(slot_ref, src_ref, tiles_ref, blocks_ref, hub_ref, out_ref):
-    node_count, rows_per_node, _ = out_ref.shape
+    return out_dest[:, 0].astype(jnp.int32), landing
+
+
+def payload_kernel(dest_ref, src_ref, hub_ref, tiles_ref, blocks_ref, out_ref, counts_ref):
+    node_count, rows_per_node, col_count = out_ref.shape
     tile_count, tile_side, _ = tiles_ref.shape
     tail = rows_per_node - HUB_PAD
     capacity = tail // tile_side
     out_ref[...] = jnp.zeros(out_ref.shape, out_ref.dtype)
-    hub = hub_ref[...]
+
+    def clear(node, carry):
+        counts_ref[node] = 0
+        return carry
+
+    lax.fori_loop(0, node_count, clear, 0, unroll=8)
+    lanes = lax.broadcasted_iota(jnp.int32, (HUB_PAD, col_count), 0)
+    hub = jnp.zeros((HUB_PAD, col_count), jnp.float32)
+    for index in range(hub_ref.shape[0]):
+        vertex = hub_ref[index]
+        block = vertex // tile_side
+        row = vertex % tile_side
+        start = pl.multiple_of((row // HUB_PAD) * HUB_PAD, HUB_PAD)
+        window = blocks_ref[block, pl.ds(start, HUB_PAD), :].astype(jnp.float32)
+        picked = jnp.sum(jnp.where(lanes == row % HUB_PAD, window, 0.0), axis=0, keepdims=True)
+        hub = jnp.where(lanes == index, picked, hub)
+    hub = hub.astype(out_ref.dtype)
 
     def put_hub(node, carry):
         out_ref[node, pl.ds(tail, HUB_PAD), :] = hub
@@ -39,9 +47,10 @@
     lax.fori_loop(0, node_count, put_hub, 0, unroll=8)
 
     def put_tile(tile, carry):
-        slot = slot_ref[tile]
-        node = slot // capacity
-        first = pl.multiple_of((slot % capacity) * tile_side, tile_side)
+        node = dest_ref[tile]
+        rank = counts_ref[node]
+        counts_ref[node] = rank + 1
+        first = pl.multiple_of(jnp.minimum(rank, capacity - 1) * tile_side, tile_side)
         product = jnp.dot(
             tiles_ref[tile], blocks_ref[src_ref[tile]], preferred_element_type=jnp.float32
         )
@@ -51,7 +60,7 @@
     lax.fori_loop(0, tile_count, put_tile, 0, unroll=8)
 
 
-def build_payload(slots, sources, tiles, blocks, hub_block, node_count, capacity):
+def build_payload(destination, sources, hubs, tiles, blocks, node_count, capacity):
     tile_side = tiles.shape[1]
     col_count = blocks.shape[2]
     rows_per_node = capacity * tile_side + HUB_PAD
@@ -59,16 +68,16 @@
         payload_kernel,
         out_shape=jax.ShapeDtypeStruct((node_count, rows_per_node, col_count), blocks.dtype),
         grid_spec=pltpu.PrefetchScalarGridSpec(
-            num_scalar_prefetch=2,
+            num_scalar_prefetch=3,
             grid=(1,),
             in_specs=[
                 pl.BlockSpec(memory_space=pltpu.VMEM),
                 pl.BlockSpec(memory_space=pltpu.VMEM),
-                pl.BlockSpec(memory_space=pltpu.VMEM),
             ],
             out_specs=pl.BlockSpec(memory_space=pltpu.VMEM),
+            scratch_shapes=[pltpu.SMEM((node_count,), jnp.int32)],
         ),
-    )(slots, sources, tiles, blocks, hub_block)
+    )(destination, sources, hubs, tiles, blocks)
 
 
 def aggregate(
@@ -81,7 +90,7 @@
     local_tiles,
     out_src,
     out_tiles,
-    slots,
+    destination,
     landing,
     anchor,
 ):
@@ -94,10 +103,9 @@
     hub_count = hub_ids.shape[0]
     blocks = inputs.reshape(block_count, tile_side, col_count)
     block_ids = jnp.arange(block_count, dtype=jnp.int32)
-    hub_local = inputs[hub_ids]
-    hub_block = jnp.zeros((HUB_PAD, col_count), jnp.bfloat16).at[:hub_count].set(hub_local)
     payload = build_payload(
-        slots, out_src.astype(jnp.int32), out_tiles, blocks, hub_block, node_count, capacity
+        destination, out_src.astype(jnp.int32), hub_ids.astype(jnp.int32), out_tiles, blocks,
+        node_count, capacity,
     )
     if anchor is not None:
         payload, anchor = lax.optimization_barrier((payload, anchor))
@@ -183,7 +191,7 @@
     gains,
 ):
     tile_side = local_tiles.shape[1]
-    slots, landing = routing(
+    destination, landing = routing(
         out_dest, recv_target, features.shape[0] // tile_side, lax.axis_size("dom")
     )
     full_self, full_neigh, full_gains = gather_weights(w_self, w_neigh, gains)
@@ -200,7 +208,7 @@
             local_tiles,
             out_src,
             out_tiles,
-            slots,
+            destination,
             landing,
             own_rows if layer_idx == 0 else None,
         )

time: 397 us -> 394 us (level)
    unnamed x45 -> x41, local copies, waits for them, and re-layouts: 13.2 us -> 13.2 us
  transfers between devices with their start and end apart: 11 -> 11, of which waited for: 8 -> 8; matrix products, arithmetic and copies ran while one was open for 7% -> 5% of each run, Pallas kernels for 2% -> 2%
where the time goes in v7:
time: 394 us; the launch traced here: 392 us
  waiting for transfers between devices  229 us (58%)
  starting transfers between devices  72.7 us (18%)
  blocking collectives  30.9 us (8%)
  local copies, waits for them, and re-layouts  25.6 us (6%)
  matrix products  15.7 us (4%)
  Pallas kernels  13.7 us (3%)
    all_to_all x2, waiting for transfers between devices, aggregate(): lax.all_to_all(payload, 'dom', split_axis=0, concat_axis=0, tiled=True)  179 us
    ppermute x7, waiting for transfers between devices, gather_weights(): pieces.append(lax.ppermute(stacked, 'feat', pairs))  45.2 us
    ppermute x7, starting transfers between devices, gather_weights(): pieces.append(lax.ppermute(stacked, 'feat', pairs))  37.3 us
    all_to_all x2, starting transfers between devices, aggregate(): lax.all_to_all(payload, 'dom', split_axis=0, concat_axis=0, tiled=True)  23.9 us
    all_to_all x2, blocking collectives, rows_to_feat(): lax.all_to_all(pieces, 'feat', split_axis=0, concat_axis=0, tiled=True)  17.7 us
    pallas_call x2, Pallas kernels, build_payload(): pl.pallas_call(payload_kernel, out_shape=jax.ShapeDtypeStruct((node_count...  13.7 us
    unnamed x41, local copies, waits for them, and re-layouts  13.2 us
    all_to_all x1, blocking collectives, feat_to_rows(): lax.all_to_all(pieces, 'feat', split_axis=0, concat_axis=0, tiled=True)  13.2 us
  transfers between devices with their start and end apart: 11, of which 8 were waited for; matrix products, arithmetic and copies ran while one was open for 5% of the time, Pallas kernels for 2%

profile of v7, /device:TPU:40, one launch (start us, length us, event | category | flops | bytes accessed | tf_op | source)
XLA Modules:
  0.0 392.3 jit_solution(13034137669354819049)
XLA Ops:
  0.0 4.4 %all-to-all-start = ((bf16[8,64,128]{2,1,0:T(8,128)(2,1)}), bf16[8,64,128]{2,1,0:T(8,128)(2,1)S(1)}, u32[]{:S(2)}, u32[]{:S(2)}) async-start(bf16[8,64,128]{2,1,0:T(8,128)(2,1)} %bitcast.132), calls=%async_computation | async-start | bytes 262144 | tf_op jit(solution)/shard_map/all_to_all | solution.py:134
  4.4 6.9 %shard_map.136 = bf16[64,272,128]{2,1,0:T(8,128)(2,1)} custom-call(s32[64]{0:T(128)} %bitcast.145, s32[64]{0:T(128)} %src_ref.3, s32[2]{0:T(128)} %hub_ref.3, bf16[64,128,128]{2,1,0:T(8,128)(2,1)} %tiles_ref.3, bf16[4,128,128]{2,1,0:T(8,128)(2,1)} %bitcast.133), custom_call_target="tpu_custom_call" | custom-call | tf_op jit(solution)/shard_map/pallas_call | solution.py:67
  11.4 16.4 %all-to-all-start.1 = ((bf16[64,272,128]{2,1,0:T(8,128)(2,1)}), bf16[64,272,128]{2,1,0:T(8,128)(2,1)}, u32[]{:S(2)}, u32[]{:S(2)}) async-start(bf16[64,272,128]{2,1,0:T(8,128)(2,1)} %shard_map.136), calls=%async_computation.1 | async-start | bytes 8912896 | tf_op jit(solution)/shard_map/all_to_all | solution.py:112
  27.9 1.4 fusion.25
  29.2 3.9 collective-permute-start.1
  33.2 4.0 %collective-permute-start.2 = (bf16[2,2064,128]{2,1,0:T(8,128)(2,1)S(1)}, bf16[2,2064,128]{2,1,0:T(8,128)(2,1)}, u32[]{:S(2)}, u32[]{:S(2)}) collective-permute-start(bf16[2,2064,128]{2,1,0:T(8,128)(2,1)S(1)} %get-tuple-element.24), channel_id=1, source_target_pairs={{0,3},{1,4},{2,5},{3,6},{4,7},{5,0},{6,1},{7,2},{8,11},{9,12},{10,... | collective-permute-start | bytes 3170312 | tf_op jit(solution)/shard_map/ppermute | solution.py:164
  37.1 4.0 %collective-permute-start.3 = (bf16[2,2064,128]{2,1,0:T(8,128)(2,1)S(1)}, bf16[2,2064,128]{2,1,0:T(8,128)(2,1)}, u32[]{:S(2)}, u32[]{:S(2)}) collective-permute-start(bf16[2,2064,128]{2,1,0:T(8,128)(2,1)S(1)} %get-tuple-element.24), channel_id=1, source_target_pairs={{0,4},{1,5},{2,6},{3,7},{4,0},{5,1},{6,2},{7,3},{8,12},{9,13},{10,... | collective-permute-start | bytes 3170312 | tf_op jit(solution)/shard_map/ppermute | solution.py:164
  41.1 3.4 collective-permute-start.4
  44.6 0.6 pad_clamp_fusion
  45.2 0.6 gather_fusion
  45.8 0.3 convolution_bitcast_fusion.1
  46.1 0.2 copy.41
  46.4 0.8 copy.38
  47.2 0.1 eq.17
  47.3 0.7 convert_element_type.43
  48.0 1.0 fusion.38
  49.0 4.6 %collective-permute-done = bf16[2,2064,128]{2,1,0:T(8,128)(2,1)} collective-permute-done((bf16[2,2064,128]{2,1,0:T(8,128)(2,1)S(1)}, bf16[2,2064,128]{2,1,0:T(8,128)(2,1)}, u32[]{:S(2)}, u32[]{:S(2)}) %collective-permute-start) | collective-permute-done | bytes 1056800 | tf_op jit(solution)/shard_map/ppermute | solution.py:164
  53.6 3.9 collective-permute-start.5
  57.6 2.4 constant_dynamic-update-slice_fusion.6
  59.9 18.1 %collective-permute-start.6 = (bf16[2,2064,128]{2,1,0:T(8,128)(2,1)S(1)}, bf16[2,2064,128]{2,1,0:T(8,128)(2,1)S(1)}, u32[]{:S(2)}, u32[]{:S(2)}) collective-permute-start(bf16[2,2064,128]{2,1,0:T(8,128)(2,1)S(1)} %get-tuple-element.24), channel_id=1, source_target_pairs={{0,7},{1,0},{2,1},{3,2},{4,3},{5,4},{6,5},{7,6},{8,15},{9,8},{10,9... | collective-permute-start | bytes 3170312 | tf_op jit(solution)/shard_map/ppermute | solution.py:164
  78.0 2.4 constant_dynamic-update-slice_fusion.5
  80.4 20.0 %collective-permute-done.2 = bf16[2,2064,128]{2,1,0:T(8,128)(2,1)} collective-permute-done((bf16[2,2064,128]{2,1,0:T(8,128)(2,1)S(1)}, bf16[2,2064,128]{2,1,0:T(8,128)(2,1)}, u32[]{:S(2)}, u32[]{:S(2)}) %collective-permute-start.2) | collective-permute-done | bytes 1056800 | tf_op jit(solution)/shard_map/ppermute | solution.py:164
  100.4 2.3 constant_dynamic-update-slice_fusion.4
  102.7 2.7 collective-permute-done.3
  105.4 2.3 constant_dynamic-update-slice_fusion.3
  107.8 14.5 %collective-permute-done.4 = bf16[2,2064,128]{2,1,0:T(8,128)(2,1)S(1)} collective-permute-done((bf16[2,2064,128]{2,1,0:T(8,128)(2,1)S(1)}, bf16[2,2064,128]{2,1,0:T(8,128)(2,1)S(1)}, u32[]{:S(2)}, u32[]{:S(2)}) %collective-permute-start.4) | collective-permute-done | bytes 1056800 | tf_op jit(solution)/shard_map/ppermute | solution.py:164
  122.3 1.2 constant_dynamic-update-slice_fusion.2
  123.5 1.1 constant_dynamic-update-slice_fusion.1
  124.6 3.3 collective-permute-done.6
  127.9 1.1 constant_dynamic-update-slice_fusion
  129.1 46.6 %all-to-all-done.1 = bf16[64,272,128]{2,1,0:T(8,128)(2,1)} async-done(((bf16[64,272,128]{2,1,0:T(8,128)(2,1)}), bf16[64,272,128]{2,1,0:T(8,128)(2,1)}, u32[]{:S(2)}, u32[]{:S(2)}) %all-to-all-start.1) | async-done | bytes 4456480 | tf_op jit(solution)/shard_map/all_to_all | solution.py:112
  175.7 2.5 slice.81
  178.1 2.3 fusion.13
  180.5 0.1 copy.43
  180.6 0.9 slice.82
  181.6 0.2 fusion.23
  181.8 0.8 copy.44
  182.6 7.1 %all-to-all-start.2 = ((bf16[8,64,128]{2,1,0:T(8,128)(2,1)}), bf16[8,64,128]{2,1,0:T(8,128)(2,1)S(1)}, u32[]{:S(2)}, u32[]{:S(2)}) async-start(bf16[8,64,128]{2,1,0:T(8,128)(2,1)} %bitcast.15), calls=%async_computation.2 | async-start | bytes 262144 | tf_op jit(solution)/shard_map/all_to_all | solution.py:134
  189.6 0.7 slice_convert_fusion.1
  190.4 5.4 %all-to-all-done.2 = bf16[8,64,128]{2,1,0:T(8,128)(2,1)S(1)} async-done(((bf16[8,64,128]{2,1,0:T(8,128)(2,1)}), bf16[8,64,128]{2,1,0:T(8,128)(2,1)S(1)}, u32[]{:S(2)}, u32[]{:S(2)}) %all-to-all-start.2) | async-done | bytes 131104 | tf_op jit(solution)/shard_map/all_to_all | solution.py:134
  195.8 2.1 fusion.7
  197.8 2.2 multiply_reduce_fusion.1
  200.1 0.1 copy_bitcast_fusion.2
  200.2 0.7 gather_fusion.2
  201.0 9.2 %all_to_all.35 = bf16[8,64,128]{2,1,0:T(8,128)(2,1)} all-to-all(bf16[8,64,128]{2,1,0:T(8,128)(2,1)S(1)} %broadcast_select_fusion), channel_id=1, replica_groups=mesh['dom'=64,'feat'=8] {'feat'}, dimensions={0} | all-to-all | bytes 262144 | tf_op jit(solution)/shard_map/all_to_all | solution.py:142
  210.2 6.8 %shard_map.137 = bf16[64,272,128]{2,1,0:T(8,128)(2,1)} custom-call(s32[64]{0:T(128)} %bitcast.146, s32[64]{0:T(128)} %src_ref.3, s32[2]{0:T(128)} %hub_ref.3, bf16[64,128,128]{2,1,0:T(8,128)(2,1)} %tiles_ref.3, bf16[4,128,128]{2,1,0:T(8,128)(2,1)} %bitcast.135), custom_call_target="tpu_custom_call" | custom-call | tf_op jit(solution)/shard_map/pallas_call | solution.py:67
  217.0 7.5 %all-to-all-start.4 = ((bf16[64,272,128]{2,1,0:T(8,128)(2,1)}), bf16[64,272,128]{2,1,0:T(8,128)(2,1)}, u32[]{:S(2)}, u32[]{:S(2)}) async-start(bf16[64,272,128]{2,1,0:T(8,128)(2,1)} %shard_map.137), calls=%async_computation.4 | async-start | bytes 8912896 | tf_op jit(solution)/shard_map/all_to_all | solution.py:112
  224.5 0.7 gather_fusion.1
  225.2 0.3 convolution_bitcast_fusion
  225.6 0.2 copy.50
  225.8 0.4 fusion.36
  226.2 132.3 %all-to-all-done.4 = bf16[64,272,128]{2,1,0:T(8,128)(2,1)} async-done(((bf16[64,272,128]{2,1,0:T(8,128)(2,1)}), bf16[64,272,128]{2,1,0:T(8,128)(2,1)}, u32[]{:S(2)}, u32[]{:S(2)}) %all-to-all-start.4) | async-done | bytes 4456480 | tf_op jit(solution)/shard_map/all_to_all | solution.py:112
  358.4 2.5 slice.85
  360.9 2.3 fusion.16
  363.3 0.2 copy.51
  363.4 0.9 slice.86
  364.4 0.2 fusion.24
  364.6 0.1 copy.52
  364.7 13.2 %all_to_all.36 = bf16[8,64,128]{2,1,0:T(8,128)(2,1)S(1)} all-to-all(bf16[8,64,128]{2,1,0:T(8,128)(2,1)S(1)} %bitcast.138), channel_id=1, replica_groups=mesh['dom'=64,'feat'=8] {'feat'}, dimensions={0} | all-to-all | bytes 262144 | tf_op jit(solution)/shard_map/all_to_all | solution.py:134
  377.9 2.1 fusion.5
  380.0 2.2 multiply_reduce_fusion
  382.3 0.7 gather_fusion.3
  383.1 8.5 %all_to_all.37 = bf16[8,64,128]{2,1,0:T(8,128)(2,1)S(1)} all-to-all(bf16[8,64,128]{2,1,0:T(8,128)(2,1)S(1)} %broadcast_select_fusion.1), channel_id=1, replica_groups=mesh['dom'=64,'feat'=8] {'feat'}, dimensions={0} | all-to-all | bytes 262144 | tf_op jit(solution)/shard_map/all_to_all | solution.py:142
  391.6 0.7 copy.99
  (47 shorter events, 0.4 us)
Async XLA Ops:
  0.0 45.8 %copy-start = (bf16[8,128,128]{2,1,0:T(8,128)(2,1)S(1)}, bf16[8,128,128]{2,1,0:T(8,128)(2,1)}, u32[]{:S(2)}) copy-start(bf16[8,128,128]{2,1,0:T(8,128)(2,1)} %param.24) | copy-start | bytes 786436
  0.0 11.3 %all-to-all-start = ((bf16[8,64,128]{2,1,0:T(8,128)(2,1)}), bf16[8,64,128]{2,1,0:T(8,128)(2,1)S(1)}, u32[]{:S(2)}, u32[]{:S(2)}) async-start(bf16[8,64,128]{2,1,0:T(8,128)(2,1)} %bitcast.132), calls=%async_computation | async-start | bytes 262144 | tf_op jit(solution)/shard_map/all_to_all | solution.py:134
  11.3 16.5 %copy-start.14 = (bf16[2,128]{1,0:T(2,128)(2,1)S(1)}, bf16[2,128]{1,0:T(2,128)(2,1)}, u32[]{:S(2)}) copy-start(bf16[2,128]{1,0:T(2,128)(2,1)} %param.31) | copy-start | bytes 1540
  11.3 16.5 %copy-start.3 = (bf16[2,1024,128]{2,1,0:T(8,128)(2,1)S(1)}, bf16[2,1024,128]{2,1,0:T(8,128)(2,1)}, u32[]{:S(2)}) copy-start(bf16[2,1024,128]{2,1,0:T(8,128)(2,1)} %param.30) | copy-start | bytes 1572868
  11.3 16.5 %copy-start.4 = (bf16[2,1024,128]{2,1,0:T(8,128)(2,1)S(1)}, bf16[2,1024,128]{2,1,0:T(8,128)(2,1)}, u32[]{:S(2)}) copy-start(bf16[2,1024,128]{2,1,0:T(8,128)(2,1)} %param.29) | copy-start | bytes 1572868
  11.3 33.2 %copy-start.15 = (s32[8]{0:T(128)S(1)}, s32[8]{0:T(128)}, u32[]{:S(2)}) copy-start(s32[8]{0:T(128)} %param.23) | copy-start | bytes 100
  11.4 33.8 %copy-start.1 = (bf16[512,128]{1,0:T(8,128)(2,1)S(1)}, bf16[512,128]{1,0:T(8,128)(2,1)}, u32[]{:S(2)}) copy-start(bf16[512,128]{1,0:T(8,128)(2,1)} %param.18) | copy-start | bytes 393220
  11.4 164.3 %all-to-all-start.1 = ((bf16[64,272,128]{2,1,0:T(8,128)(2,1)}), bf16[64,272,128]{2,1,0:T(8,128)(2,1)}, u32[]{:S(2)}, u32[]{:S(2)}) async-start(bf16[64,272,128]{2,1,0:T(8,128)(2,1)} %shard_map.136), calls=%async_computation.1 | async-start | bytes 8912896 | tf_op jit(solution)/shard_map/all_to_all | solution.py:112
  29.2 24.4 %collective-permute-start = (bf16[2,2064,128]{2,1,0:T(8,128)(2,1)S(1)}, bf16[2,2064,128]{2,1,0:T(8,128)(2,1)}, u32[]{:S(2)}, u32[]{:S(2)}) collective-permute-start(bf16[2,2064,128]{2,1,0:T(8,128)(2,1)S(1)} %get-tuple-element.24), channel_id=1, source_target_pairs={{0,1},{1,2},{2,3},{3,4},{4,5},{5,6},{6,7},{7,0},{8,9},{9,10},{10,1... | collective-permute-start | bytes 3170312 | tf_op jit(solution)/shard_map/ppermute | solution.py:164
  29.2 30.7 %collective-permute-start.1 = (bf16[2,2064,128]{2,1,0:T(8,128)(2,1)S(1)}, bf16[2,2064,128]{2,1,0:T(8,128)(2,1)}, u32[]{:S(2)}, u32[]{:S(2)}) collective-permute-start(bf16[2,2064,128]{2,1,0:T(8,128)(2,1)S(1)} %get-tuple-element.24), channel_id=1, source_target_pairs={{0,2},{1,3},{2,4},{3,5},{4,6},{5,7},{6,0},{7,1},{8,10},{9,11},{10,... | collective-permute-start | bytes 3170312 | tf_op jit(solution)/shard_map/ppermute | solution.py:164
  33.2 67.2 %collective-permute-start.2 = (bf16[2,2064,128]{2,1,0:T(8,128)(2,1)S(1)}, bf16[2,2064,128]{2,1,0:T(8,128)(2,1)}, u32[]{:S(2)}, u32[]{:S(2)}) collective-permute-start(bf16[2,2064,128]{2,1,0:T(8,128)(2,1)S(1)} %get-tuple-element.24), channel_id=1, source_target_pairs={{0,3},{1,4},{2,5},{3,6},{4,7},{5,0},{6,1},{7,2},{8,11},{9,12},{10,... | collective-permute-start | bytes 3170312 | tf_op jit(solution)/shard_map/ppermute | solution.py:164
  37.1 68.3 %collective-permute-start.3 = (bf16[2,2064,128]{2,1,0:T(8,128)(2,1)S(1)}, bf16[2,2064,128]{2,1,0:T(8,128)(2,1)}, u32[]{:S(2)}, u32[]{:S(2)}) collective-permute-start(bf16[2,2064,128]{2,1,0:T(8,128)(2,1)S(1)} %get-tuple-element.24), channel_id=1, source_target_pairs={{0,4},{1,5},{2,6},{3,7},{4,0},{5,1},{6,2},{7,3},{8,12},{9,13},{10,... | collective-permute-start | bytes 3170312 | tf_op jit(solution)/shard_map/ppermute | solution.py:164
  41.1 81.2 %collective-permute-start.4 = (bf16[2,2064,128]{2,1,0:T(8,128)(2,1)S(1)}, bf16[2,2064,128]{2,1,0:T(8,128)(2,1)S(1)}, u32[]{:S(2)}, u32[]{:S(2)}) collective-permute-start(bf16[2,2064,128]{2,1,0:T(8,128)(2,1)S(1)} %get-tuple-element.24), channel_id=1, source_target_pairs={{0,5},{1,6},{2,7},{3,0},{4,1},{5,2},{6,3},{7,4},{8,13},{9,14},{10,... | collective-permute-start | bytes 3170312 | tf_op jit(solution)/shard_map/ppermute | solution.py:164
  45.2 0.6 copy-start.5
  47.3 130.8 %copy-start.6 = (s32[128]{0:T(128)}, s32[128]{0:T(128)S(1)}, u32[]{:S(2)}) copy-start(s32[128]{0:T(128)S(1)} %eq.17) | copy-start | bytes 1540
  48.0 133.6 %copy-start.10 = (f32[512]{0:T(512)}, f32[512]{0:T(512)S(1)}, u32[]{:S(2)}) copy-start(f32[512]{0:T(512)S(1)} %convert_element_type.43) | copy-start | bytes 6148
  48.0 152.9 %copy-start.8 = (pred[8]{0:T(512)(128)(4,1)}, pred[8]{0:T(512)(128)(4,1)S(1)}, u32[]{:S(2)}) copy-start(pred[8]{0:T(512)(128)(4,1)S(1)} %compare_and_fusion) | copy-start | bytes 28
  53.6 69.8 %collective-permute-start.5 = (bf16[2,2064,128]{2,1,0:T(8,128)(2,1)S(1)}, bf16[2,2064,128]{2,1,0:T(8,128)(2,1)S(1)}, u32[]{:S(2)}, u32[]{:S(2)}) collective-permute-start(bf16[2,2064,128]{2,1,0:T(8,128)(2,1)S(1)} %get-tuple-element.24), channel_id=1, source_target_pairs={{0,6},{1,7},{2,0},{3,1},{4,2},{5,3},{6,4},{7,5},{8,14},{9,15},{10,... | collective-permute-start | bytes 3170312 | tf_op jit(solution)/shard_map/ppermute | solution.py:164
  59.9 68.0 %collective-permute-start.6 = (bf16[2,2064,128]{2,1,0:T(8,128)(2,1)S(1)}, bf16[2,2064,128]{2,1,0:T(8,128)(2,1)S(1)}, u32[]{:S(2)}, u32[]{:S(2)}) collective-permute-start(bf16[2,2064,128]{2,1,0:T(8,128)(2,1)S(1)} %get-tuple-element.24), channel_id=1, source_target_pairs={{0,7},{1,0},{2,1},{3,2},{4,3},{5,4},{6,5},{7,6},{8,15},{9,8},{10,9... | collective-permute-start | bytes 3170312 | tf_op jit(solution)/shard_map/ppermute | solution.py:164
  178.1 3.5 copy-start.13
  182.6 13.2 %all-to-all-start.2 = ((bf16[8,64,128]{2,1,0:T(8,128)(2,1)}), bf16[8,64,128]{2,1,0:T(8,128)(2,1)S(1)}, u32[]{:S(2)}, u32[]{:S(2)}) async-start(bf16[8,64,128]{2,1,0:T(8,128)(2,1)} %bitcast.15), calls=%async_computation.2 | async-start | bytes 262144 | tf_op jit(solution)/shard_map/all_to_all | solution.py:134
  217.0 7.5 %copy-start.2 = (bf16[8,64,128]{2,1,0:T(8,128)(2,1)S(1)}, bf16[8,64,128]{2,1,0:T(8,128)(2,1)}, u32[]{:S(2)}) copy-start(bf16[8,64,128]{2,1,0:T(8,128)(2,1)} %all_to_all.35) | copy-start | bytes 393220
  217.0 8.8 %copy-start.12 = (s32[8]{0:T(128)S(1)}, s32[8]{0:T(128)}, u32[]{:S(2)}) copy-start(s32[8]{0:T(128)} %param.22) | copy-start | bytes 100
  217.0 141.4 %all-to-all-start.4 = ((bf16[64,272,128]{2,1,0:T(8,128)(2,1)}), bf16[64,272,128]{2,1,0:T(8,128)(2,1)}, u32[]{:S(2)}, u32[]{:S(2)}) async-start(bf16[64,272,128]{2,1,0:T(8,128)(2,1)} %shard_map.137), calls=%async_computation.4 | async-start | bytes 8912896 | tf_op jit(solution)/shard_map/all_to_all | solution.py:112
  226.2 134.7 %copy-start.7 = (s32[128]{0:T(128)S(1)}, s32[128]{0:T(128)}, u32[]{:S(2)}) copy-start(s32[128]{0:T(128)} %copy-done.6) | copy-start | bytes 1540
  360.9 3.5 copy-start.11
  360.9 19.0 %copy-start.9 = (pred[8]{0:T(512)(128)(4,1)S(1)}, pred[8]{0:T(512)(128)(4,1)}, u32[]{:S(2)}) copy-start(pred[8]{0:T(512)(128)(4,1)} %copy-done.8) | copy-start | bytes 28

commit v8 on v7

--- a/solution.py
+++ b/solution.py
@@ -174,6 +174,18 @@
     return jnp.take(blocks, order, axis=1).reshape(row_count, width)
 
 
+def feat_to_rows_by_permutes(block):
+    feat_count = lax.axis_size("feat")
+    row_count, col_count = block.shape
+    own = lax.axis_index("feat")
+    chunks = block.reshape(feat_count, row_count // feat_count, col_count)
+    pieces = [chunks[own]]
+    for shift in range(1, feat_count):
+        pairs = [(source, (source + shift) % feat_count) for source in range(feat_count)]
+        pieces.append(lax.ppermute(chunks[(own + shift) % feat_count], "feat", pairs))
+    return natural_columns(jnp.concatenate(pieces, axis=1))
+
+
 def per_device(
     features,
     degree,
@@ -196,7 +208,7 @@
     )
     full_self, full_neigh, full_gains = gather_weights(w_self, w_neigh, gains)
     current = features
-    own_rows = feat_to_rows(features)
+    own_rows = feat_to_rows_by_permutes(features)
     for layer_idx in range(w_self.shape[0]):
         neighbours, anchored = aggregate(
             current,
@@ -210,7 +222,7 @@
             out_tiles,
             destination,
             landing,
-            own_rows if layer_idx == 0 else None,
+            None,
         )
         if anchored is not None:
             own_rows = anchored

time: 394 us -> 427 us (1.084)
  starting transfers between devices: 72.7 us -> 104 us
    ppermute x0 -> x7, starting transfers between devices: none -> 51.2 us  [feat_to_rows_by_permutes(): lax.ppermute(chunks[(own + shift) % feat_count], 'feat', pairs)]
    ppermute x0 -> x7, waiting for transfers between devices: none -> 48.1 us  [feat_to_rows_by_permutes(): lax.ppermute(chunks[(own + shift) % feat_count], 'feat', pairs)]
    all_to_all x2, waiting for transfers between devices: 179 us -> 133 us  [aggregate(): lax.all_to_all(payload, 'dom', split_axis=0, concat_axis=0, tiled=True)]
    ppermute x7, starting transfers between devices: 37.3 us -> 19.5 us  [gather_weights(): pieces.append(lax.ppermute(stacked, 'feat', pairs))]
    all_to_all x2 -> x1, starting transfers between devices: 11.5 us -> 4.39 us  [feat_to_rows(): lax.all_to_all(pieces, 'feat', split_axis=0, concat_axis=0, tiled=True)]
    all_to_all x2, starting transfers between devices: 23.9 us -> 29.4 us  [aggregate(): lax.all_to_all(payload, 'dom', split_axis=0, concat_axis=0, tiled=True)]
    ppermute x7, waiting for transfers between devices: 45.2 us -> 40.5 us  [gather_weights(): pieces.append(lax.ppermute(stacked, 'feat', pairs))]
    unnamed x41 -> x42, local copies, waits for them, and re-layouts: 13.2 us -> 13.4 us
  transfers between devices with their start and end apart: 11 -> 17, of which waited for: 8 -> 12; matrix products, arithmetic and copies ran while one was open for 5% -> 6% of each run, Pallas kernels for 2% -> 0%
where the time goes in v8:
time: 427 us; the launch traced here: 426 us
  waiting for transfers between devices  227 us (53%)
  starting transfers between devices  104 us (24%)
  blocking collectives  31.6 us (7%)
  local copies, waits for them, and re-layouts  29 us (7%)
  matrix products  16.4 us (4%)
  Pallas kernels  13.8 us (3%)
    all_to_all x2, waiting for transfers between devices, aggregate(): lax.all_to_all(payload, 'dom', split_axis=0, concat_axis=0, tiled=True)  133 us
    ppermute x7, starting transfers between devices, feat_to_rows_by_permutes(): lax.ppermute(chunks[(own + shift) % feat_count], 'feat', pairs)  51.2 us
    ppermute x7, waiting for transfers between devices, feat_to_rows_by_permutes(): lax.ppermute(chunks[(own + shift) % feat_count], 'feat', pairs)  48.1 us
    ppermute x7, waiting for transfers between devices, gather_weights(): pieces.append(lax.ppermute(stacked, 'feat', pairs))  40.5 us
    all_to_all x2, starting transfers between devices, aggregate(): lax.all_to_all(payload, 'dom', split_axis=0, concat_axis=0, tiled=True)  29.4 us
    ppermute x7, starting transfers between devices, gather_weights(): pieces.append(lax.ppermute(stacked, 'feat', pairs))  19.5 us
    all_to_all x2, blocking collectives, rows_to_feat(): lax.all_to_all(pieces, 'feat', split_axis=0, concat_axis=0, tiled=True)  17.7 us
    all_to_all x1, blocking collectives, feat_to_rows(): lax.all_to_all(pieces, 'feat', split_axis=0, concat_axis=0, tiled=True)  13.9 us
  transfers between devices with their start and end apart: 17, of which 12 were waited for; matrix products, arithmetic and copies ran while one was open for 6% of the time, Pallas kernels for 0%

profile of v8, /device:TPU:40, one launch (start us, length us, event | category | flops | bytes accessed | tf_op | source)
XLA Modules:
  0.0 425.9 jit_solution(2868255178079533357)
XLA Ops:
  0.0 7.0 %shard_map.136 = bf16[64,272,128]{2,1,0:T(8,128)(2,1)} custom-call(s32[64]{0:T(128)} %bitcast.179, s32[64]{0:T(128)} %src_ref.3, s32[2]{0:T(128)} %hub_ref.3, bf16[64,128,128]{2,1,0:T(8,128)(2,1)} %tiles_ref.3, bf16[4,128,128]{2,1,0:T(8,128)(2,1)} %bitcast.165), custom_call_target="tpu_custom_call" | custom-call | tf_op jit(solution)/shard_map/pallas_call | solution.py:67
  7.0 16.4 %all-to-all-start = ((bf16[64,272,128]{2,1,0:T(8,128)(2,1)}), bf16[64,272,128]{2,1,0:T(8,128)(2,1)}, u32[]{:S(2)}, u32[]{:S(2)}) async-start(bf16[64,272,128]{2,1,0:T(8,128)(2,1)} %shard_map.136), calls=%async_computation | async-start | bytes 8912896 | tf_op jit(solution)/shard_map/all_to_all | solution.py:112
  23.5 1.4 fusion.25
  24.9 3.4 collective-permute-start.1
  28.3 4.0 collective-permute-start.2
  32.3 3.9 collective-permute-start.3
  36.3 0.6 dynamic-slice_bitcast_fusion
  37.0 0.6 gather_fusion
  38.3 1.7 fusion.40
  40.0 0.8 copy.37
  40.9 0.7 convert_element_type.43
  41.6 30.7 %collective-permute-done.7 = bf16[64,128]{1,0:T(8,128)(2,1)} collective-permute-done((bf16[64,128]{1,0:T(8,128)(2,1)}, bf16[64,128]{1,0:T(8,128)(2,1)}, u32[]{:S(2)}, u32[]{:S(2)}) %collective-permute-start.7) | collective-permute-done | bytes 16416 | tf_op jit(solution)/shard_map/ppermute | solution.py:185
  72.3 38.5 %collective-permute-start.8 = (bf16[64,128]{1,0:T(8,128)(2,1)}, bf16[64,128]{1,0:T(8,128)(2,1)S(1)}, u32[]{:S(2)}, u32[]{:S(2)}) collective-permute-start(bf16[64,128]{1,0:T(8,128)(2,1)} %get-tuple-element.27), channel_id=1, source_target_pairs={{0,2},{1,3},{2,4},{3,5},{4,6},{5,7},{6,0},{7,1},{8,10},{9,11},{10,... | collective-permute-start | bytes 49160 | tf_op jit(solution)/shard_map/ppermute | solution.py:185
  110.8 0.7 constant_dynamic-update-slice_fusion.14
  111.6 2.4 collective-permute-done.8
  114.0 1.9 collective-permute-start.9
  115.9 4.8 %collective-permute-done.9 = bf16[64,128]{1,0:T(8,128)(2,1)S(1)} collective-permute-done((bf16[64,128]{1,0:T(8,128)(2,1)}, bf16[64,128]{1,0:T(8,128)(2,1)S(1)}, u32[]{:S(2)}, u32[]{:S(2)}) %collective-permute-start.9) | collective-permute-done | bytes 16416 | tf_op jit(solution)/shard_map/ppermute | solution.py:185
  120.7 3.1 collective-permute-start.10
  123.8 4.2 collective-permute-done.10
  128.1 1.9 collective-permute-start.11
  130.0 3.3 collective-permute-done.11
  133.3 5.1 %collective-permute-start.12 = (bf16[64,128]{1,0:T(8,128)(2,1)}, bf16[64,128]{1,0:T(8,128)(2,1)S(1)}, u32[]{:S(2)}, u32[]{:S(2)}) collective-permute-start(bf16[64,128]{1,0:T(8,128)(2,1)} %get-tuple-element.23), channel_id=1, source_target_pairs={{0,6},{1,7},{2,0},{3,1},{4,2},{5,3},{6,4},{7,5},{8,14},{9,15},{10,... | collective-permute-start | bytes 49160 | tf_op jit(solution)/shard_map/ppermute | solution.py:185
  138.5 1.6 collective-permute-done.12
  140.1 0.6 collective-permute-start.13
  140.7 0.7 copy-done.6
  141.3 1.0 collective-permute-done.13
  142.3 6.0 %collective-permute-start.4 = (bf16[2,2064,128]{2,1,0:T(8,128)(2,1)S(1)}, bf16[2,2064,128]{2,1,0:T(8,128)(2,1)S(1)}, u32[]{:S(2)}, u32[]{:S(2)}) collective-permute-start(bf16[2,2064,128]{2,1,0:T(8,128)(2,1)S(1)} %get-tuple-element.20), channel_id=1, source_target_pairs={{0,5},{1,6},{2,7},{3,0},{4,1},{5,2},{6,3},{7,4},{8,13},{9,14},{10,... | collective-permute-start | bytes 3170312 | tf_op jit(solution)/shard_map/ppermute | solution.py:164
  148.3 0.6 constant_dynamic-update-slice_fusion.8
  148.9 2.1 gather_fusion.2
  151.0 1.9 collective-permute-start.5
  153.0 2.4 constant_dynamic-update-slice_fusion.6
  155.6 2.4 constant_dynamic-update-slice_fusion.5
  158.0 2.3 constant_dynamic-update-slice_fusion.4
  160.3 1.1 constant_dynamic-update-slice_fusion.3
  161.5 6.0 %collective-permute-done.4 = bf16[2,2064,128]{2,1,0:T(8,128)(2,1)S(1)} collective-permute-done((bf16[2,2064,128]{2,1,0:T(8,128)(2,1)S(1)}, bf16[2,2064,128]{2,1,0:T(8,128)(2,1)S(1)}, u32[]{:S(2)}, u32[]{:S(2)}) %collective-permute-start.4) | collective-permute-done | bytes 1056800 | tf_op jit(solution)/shard_map/ppermute | solution.py:164
  167.4 1.2 constant_dynamic-update-slice_fusion.2
  168.6 23.9 %collective-permute-done.5 = bf16[2,2064,128]{2,1,0:T(8,128)(2,1)S(1)} collective-permute-done((bf16[2,2064,128]{2,1,0:T(8,128)(2,1)S(1)}, bf16[2,2064,128]{2,1,0:T(8,128)(2,1)S(1)}, u32[]{:S(2)}, u32[]{:S(2)}) %collective-permute-start.5) | collective-permute-done | bytes 1056800 | tf_op jit(solution)/shard_map/ppermute | solution.py:164
  192.5 1.1 constant_dynamic-update-slice_fusion.1
  193.6 10.6 %collective-permute-done.6 = bf16[2,2064,128]{2,1,0:T(8,128)(2,1)S(1)} collective-permute-done((bf16[2,2064,128]{2,1,0:T(8,128)(2,1)S(1)}, bf16[2,2064,128]{2,1,0:T(8,128)(2,1)S(1)}, u32[]{:S(2)}, u32[]{:S(2)}) %collective-permute-start.6) | collective-permute-done | bytes 1056800 | tf_op jit(solution)/shard_map/ppermute | solution.py:164
  204.2 1.1 constant_dynamic-update-slice_fusion
  205.4 2.5 slice.83
  207.9 2.3 fusion.13
  210.4 0.9 slice.84
  211.6 0.8 copy.43
  212.3 4.4 %all-to-all-start.1 = ((bf16[8,64,128]{2,1,0:T(8,128)(2,1)}), bf16[8,64,128]{2,1,0:T(8,128)(2,1)S(1)}, u32[]{:S(2)}, u32[]{:S(2)}) async-start(bf16[8,64,128]{2,1,0:T(8,128)(2,1)} %bitcast.30), calls=%async_computation.1 | async-start | bytes 262144 | tf_op jit(solution)/shard_map/all_to_all | solution.py:134
  216.7 0.7 slice_convert_fusion.1
  217.5 5.4 %all-to-all-done.1 = bf16[8,64,128]{2,1,0:T(8,128)(2,1)S(1)} async-done(((bf16[8,64,128]{2,1,0:T(8,128)(2,1)}), bf16[8,64,128]{2,1,0:T(8,128)(2,1)S(1)}, u32[]{:S(2)}, u32[]{:S(2)}) %all-to-all-start.1) | async-done | bytes 131104 | tf_op jit(solution)/shard_map/all_to_all | solution.py:134
  222.9 2.1 fusion.7
  224.9 2.2 multiply_reduce_fusion.1
  227.3 0.6 gather_fusion.3
  228.0 9.2 %all_to_all.30 = bf16[8,64,128]{2,1,0:T(8,128)(2,1)} all-to-all(bf16[8,64,128]{2,1,0:T(8,128)(2,1)S(1)} %broadcast_select_fusion), channel_id=1, replica_groups=mesh['dom'=64,'feat'=8] {'feat'}, dimensions={0} | all-to-all | bytes 262144 | tf_op jit(solution)/shard_map/all_to_all | solution.py:142
  237.2 6.8 %shard_map.137 = bf16[64,272,128]{2,1,0:T(8,128)(2,1)} custom-call(s32[64]{0:T(128)} %bitcast.180, s32[64]{0:T(128)} %src_ref.3, s32[2]{0:T(128)} %hub_ref.3, bf16[64,128,128]{2,1,0:T(8,128)(2,1)} %tiles_ref.3, bf16[4,128,128]{2,1,0:T(8,128)(2,1)} %bitcast.169), custom_call_target="tpu_custom_call" | custom-call | tf_op jit(solution)/shard_map/pallas_call | solution.py:67
  244.0 13.0 %all-to-all-start.3 = ((bf16[64,272,128]{2,1,0:T(8,128)(2,1)}), bf16[64,272,128]{2,1,0:T(8,128)(2,1)}, u32[]{:S(2)}, u32[]{:S(2)}) async-start(bf16[64,272,128]{2,1,0:T(8,128)(2,1)} %shard_map.137), calls=%async_computation.3 | async-start | bytes 8912896 | tf_op jit(solution)/shard_map/all_to_all | solution.py:112
  257.0 0.7 gather_fusion.1
  258.7 132.8 %all-to-all-done.3 = bf16[64,272,128]{2,1,0:T(8,128)(2,1)} async-done(((bf16[64,272,128]{2,1,0:T(8,128)(2,1)}), bf16[64,272,128]{2,1,0:T(8,128)(2,1)}, u32[]{:S(2)}, u32[]{:S(2)}) %all-to-all-start.3) | async-done | bytes 4456480 | tf_op jit(solution)/shard_map/all_to_all | solution.py:112
  391.5 2.5 slice.87
  393.9 2.3 fusion.16
  396.4 0.9 slice.88
  397.7 13.9 %all_to_all.31 = bf16[8,64,128]{2,1,0:T(8,128)(2,1)S(1)} all-to-all(bf16[8,64,128]{2,1,0:T(8,128)(2,1)S(1)} %bitcast.172), channel_id=1, replica_groups=mesh['dom'=64,'feat'=8] {'feat'}, dimensions={0} | all-to-all | bytes 262144 | tf_op jit(solution)/shard_map/all_to_all | solution.py:134
  411.6 2.1 fusion.5
  413.7 2.2 multiply_reduce_fusion
  416.1 0.6 gather_fusion.4
  416.7 8.5 %all_to_all.32 = bf16[8,64,128]{2,1,0:T(8,128)(2,1)S(1)} all-to-all(bf16[8,64,128]{2,1,0:T(8,128)(2,1)S(1)} %broadcast_select_fusion.1), channel_id=1, replica_groups=mesh['dom'=64,'feat'=8] {'feat'}, dimensions={0} | all-to-all | bytes 262144 | tf_op jit(solution)/shard_map/all_to_all | solution.py:142
  425.2 0.7 copy.110
  (63 shorter events, 3.3 us)
Async XLA Ops:
  0.0 37.6 %copy-start = (bf16[8,128,128]{2,1,0:T(8,128)(2,1)S(1)}, bf16[8,128,128]{2,1,0:T(8,128)(2,1)}, u32[]{:S(2)}) copy-start(bf16[8,128,128]{2,1,0:T(8,128)(2,1)} %param.24) | copy-start | bytes 786436
  7.0 16.5 %copy-start.11 = (bf16[2,128]{1,0:T(2,128)(2,1)S(1)}, bf16[2,128]{1,0:T(2,128)(2,1)}, u32[]{:S(2)}) copy-start(bf16[2,128]{1,0:T(2,128)(2,1)} %param.31) | copy-start | bytes 1540
  7.0 16.5 %copy-start.4 = (bf16[2,1024,128]{2,1,0:T(8,128)(2,1)S(1)}, bf16[2,1024,128]{2,1,0:T(8,128)(2,1)}, u32[]{:S(2)}) copy-start(bf16[2,1024,128]{2,1,0:T(8,128)(2,1)} %param.30) | copy-start | bytes 1572868
  7.0 16.5 %copy-start.5 = (bf16[2,1024,128]{2,1,0:T(8,128)(2,1)S(1)}, bf16[2,1024,128]{2,1,0:T(8,128)(2,1)}, u32[]{:S(2)}) copy-start(bf16[2,1024,128]{2,1,0:T(8,128)(2,1)} %param.29) | copy-start | bytes 1572868
  7.0 29.3 %copy-start.1 = (bf16[512,128]{1,0:T(8,128)(2,1)S(1)}, bf16[512,128]{1,0:T(8,128)(2,1)}, u32[]{:S(2)}) copy-start(bf16[512,128]{1,0:T(8,128)(2,1)} %param.18) | copy-start | bytes 393220
  7.0 30.0 %copy-start.12 = (s32[8]{0:T(128)S(1)}, s32[8]{0:T(128)}, u32[]{:S(2)}) copy-start(s32[8]{0:T(128)} %param.23) | copy-start | bytes 100
  7.0 198.4 %all-to-all-start = ((bf16[64,272,128]{2,1,0:T(8,128)(2,1)}), bf16[64,272,128]{2,1,0:T(8,128)(2,1)}, u32[]{:S(2)}, u32[]{:S(2)}) async-start(bf16[64,272,128]{2,1,0:T(8,128)(2,1)} %shard_map.136), calls=%async_computation | async-start | bytes 8912896 | tf_op jit(solution)/shard_map/all_to_all | solution.py:112
  24.9 126.2 %collective-permute-start = (bf16[2,2064,128]{2,1,0:T(8,128)(2,1)S(1)}, bf16[2,2064,128]{2,1,0:T(8,128)(2,1)}, u32[]{:S(2)}, u32[]{:S(2)}) collective-permute-start(bf16[2,2064,128]{2,1,0:T(8,128)(2,1)S(1)} %get-tuple-element.20), channel_id=1, source_target_pairs={{0,1},{1,2},{2,3},{3,4},{4,5},{5,6},{6,7},{7,0},{8,9},{9,10},{10,1... | collective-permute-start | bytes 3170312 | tf_op jit(solution)/shard_map/ppermute | solution.py:164
  24.9 130.5 %collective-permute-start.1 = (bf16[2,2064,128]{2,1,0:T(8,128)(2,1)S(1)}, bf16[2,2064,128]{2,1,0:T(8,128)(2,1)}, u32[]{:S(2)}, u32[]{:S(2)}) collective-permute-start(bf16[2,2064,128]{2,1,0:T(8,128)(2,1)S(1)} %get-tuple-element.20), channel_id=1, source_target_pairs={{0,2},{1,3},{2,4},{3,5},{4,6},{5,7},{6,0},{7,1},{8,10},{9,11},{10,... | collective-permute-start | bytes 3170312 | tf_op jit(solution)/shard_map/ppermute | solution.py:164
  28.3 129.8 %collective-permute-start.2 = (bf16[2,2064,128]{2,1,0:T(8,128)(2,1)S(1)}, bf16[2,2064,128]{2,1,0:T(8,128)(2,1)}, u32[]{:S(2)}, u32[]{:S(2)}) collective-permute-start(bf16[2,2064,128]{2,1,0:T(8,128)(2,1)S(1)} %get-tuple-element.20), channel_id=1, source_target_pairs={{0,3},{1,4},{2,5},{3,6},{4,7},{5,0},{6,1},{7,2},{8,11},{9,12},{10,... | collective-permute-start | bytes 3170312 | tf_op jit(solution)/shard_map/ppermute | solution.py:164
  32.3 128.0 %collective-permute-start.3 = (bf16[2,2064,128]{2,1,0:T(8,128)(2,1)S(1)}, bf16[2,2064,128]{2,1,0:T(8,128)(2,1)S(1)}, u32[]{:S(2)}, u32[]{:S(2)}) collective-permute-start(bf16[2,2064,128]{2,1,0:T(8,128)(2,1)S(1)} %get-tuple-element.20), channel_id=1, source_target_pairs={{0,4},{1,5},{2,6},{3,7},{4,0},{5,1},{6,2},{7,3},{8,12},{9,13},{10,... | collective-permute-start | bytes 3170312 | tf_op jit(solution)/shard_map/ppermute | solution.py:164
  37.0 35.3 %collective-permute-start.7 = (bf16[64,128]{1,0:T(8,128)(2,1)}, bf16[64,128]{1,0:T(8,128)(2,1)}, u32[]{:S(2)}, u32[]{:S(2)}) collective-permute-start(bf16[64,128]{1,0:T(8,128)(2,1)} %get-tuple-element.28), channel_id=1, source_target_pairs={{0,1},{1,2},{2,3},{3,4},{4,5},{5,6},{6,7},{7,0},{8,9},{9,10},{10,1... | collective-permute-start | bytes 49160 | tf_op jit(solution)/shard_map/ppermute | solution.py:185
  37.0 0.6 copy-start.8
  72.3 41.7 %collective-permute-start.8 = (bf16[64,128]{1,0:T(8,128)(2,1)}, bf16[64,128]{1,0:T(8,128)(2,1)S(1)}, u32[]{:S(2)}, u32[]{:S(2)}) collective-permute-start(bf16[64,128]{1,0:T(8,128)(2,1)} %get-tuple-element.27), channel_id=1, source_target_pairs={{0,2},{1,3},{2,4},{3,5},{4,6},{5,7},{6,0},{7,1},{8,10},{9,11},{10,... | collective-permute-start | bytes 49160 | tf_op jit(solution)/shard_map/ppermute | solution.py:185
  114.0 6.8 %collective-permute-start.9 = (bf16[64,128]{1,0:T(8,128)(2,1)}, bf16[64,128]{1,0:T(8,128)(2,1)S(1)}, u32[]{:S(2)}, u32[]{:S(2)}) collective-permute-start(bf16[64,128]{1,0:T(8,128)(2,1)} %get-tuple-element.26), channel_id=1, source_target_pairs={{0,3},{1,4},{2,5},{3,6},{4,7},{5,0},{6,1},{7,2},{8,11},{9,12},{10,... | collective-permute-start | bytes 49160 | tf_op jit(solution)/shard_map/ppermute | solution.py:185
  120.7 7.3 %collective-permute-start.10 = (bf16[64,128]{1,0:T(8,128)(2,1)}, bf16[64,128]{1,0:T(8,128)(2,1)S(1)}, u32[]{:S(2)}, u32[]{:S(2)}) collective-permute-start(bf16[64,128]{1,0:T(8,128)(2,1)} %get-tuple-element.25), channel_id=1, source_target_pairs={{0,4},{1,5},{2,6},{3,7},{4,0},{5,1},{6,2},{7,3},{8,12},{9,13},{10,... | collective-permute-start | bytes 49160 | tf_op jit(solution)/shard_map/ppermute | solution.py:185
  128.1 5.3 %collective-permute-start.11 = (bf16[64,128]{1,0:T(8,128)(2,1)}, bf16[64,128]{1,0:T(8,128)(2,1)S(1)}, u32[]{:S(2)}, u32[]{:S(2)}) collective-permute-start(bf16[64,128]{1,0:T(8,128)(2,1)} %get-tuple-element.24), channel_id=1, source_target_pairs={{0,5},{1,6},{2,7},{3,0},{4,1},{5,2},{6,3},{7,4},{8,13},{9,14},{10,... | collective-permute-start | bytes 49160 | tf_op jit(solution)/shard_map/ppermute | solution.py:185
  133.3 6.8 %collective-permute-start.12 = (bf16[64,128]{1,0:T(8,128)(2,1)}, bf16[64,128]{1,0:T(8,128)(2,1)S(1)}, u32[]{:S(2)}, u32[]{:S(2)}) collective-permute-start(bf16[64,128]{1,0:T(8,128)(2,1)} %get-tuple-element.23), channel_id=1, source_target_pairs={{0,6},{1,7},{2,0},{3,1},{4,2},{5,3},{6,4},{7,5},{8,14},{9,15},{10,... | collective-permute-start | bytes 49160 | tf_op jit(solution)/shard_map/ppermute | solution.py:185
  140.1 2.2 collective-permute-start.13
  140.7 0.7 copy-start.6
  142.3 25.1 %collective-permute-start.4 = (bf16[2,2064,128]{2,1,0:T(8,128)(2,1)S(1)}, bf16[2,2064,128]{2,1,0:T(8,128)(2,1)S(1)}, u32[]{:S(2)}, u32[]{:S(2)}) collective-permute-start(bf16[2,2064,128]{2,1,0:T(8,128)(2,1)S(1)} %get-tuple-element.20), channel_id=1, source_target_pairs={{0,5},{1,6},{2,7},{3,0},{4,1},{5,2},{6,3},{7,4},{8,13},{9,14},{10,... | collective-permute-start | bytes 3170312 | tf_op jit(solution)/shard_map/ppermute | solution.py:164
  151.0 41.5 %collective-permute-start.5 = (bf16[2,2064,128]{2,1,0:T(8,128)(2,1)S(1)}, bf16[2,2064,128]{2,1,0:T(8,128)(2,1)S(1)}, u32[]{:S(2)}, u32[]{:S(2)}) collective-permute-start(bf16[2,2064,128]{2,1,0:T(8,128)(2,1)S(1)} %get-tuple-element.20), channel_id=1, source_target_pairs={{0,6},{1,7},{2,0},{3,1},{4,2},{5,3},{6,4},{7,5},{8,14},{9,15},{10,... | collective-permute-start | bytes 3170312 | tf_op jit(solution)/shard_map/ppermute | solution.py:164
  155.3 48.9 %collective-permute-start.6 = (bf16[2,2064,128]{2,1,0:T(8,128)(2,1)S(1)}, bf16[2,2064,128]{2,1,0:T(8,128)(2,1)S(1)}, u32[]{:S(2)}, u32[]{:S(2)}) collective-permute-start(bf16[2,2064,128]{2,1,0:T(8,128)(2,1)S(1)} %get-tuple-element.20), channel_id=1, source_target_pairs={{0,7},{1,0},{2,1},{3,2},{4,3},{5,4},{6,5},{7,6},{8,15},{9,8},{10,9... | collective-permute-start | bytes 3170312 | tf_op jit(solution)/shard_map/ppermute | solution.py:164
  205.4 2.5 copy-start.3
  207.9 3.5 copy-start.10
  207.9 17.0 %copy-start.7 = (bf16[8,64,128]{2,1,0:T(8,128)(2,1)S(1)}, bf16[8,64,128]{2,1,0:T(8,128)(2,1)}, u32[]{:S(2)}) copy-start(bf16[8,64,128]{2,1,0:T(8,128)(2,1)} %gather_fusion.2) | copy-start | bytes 393220
  212.3 10.5 %all-to-all-start.1 = ((bf16[8,64,128]{2,1,0:T(8,128)(2,1)}), bf16[8,64,128]{2,1,0:T(8,128)(2,1)S(1)}, u32[]{:S(2)}, u32[]{:S(2)}) async-start(bf16[8,64,128]{2,1,0:T(8,128)(2,1)} %bitcast.30), calls=%async_computation.1 | async-start | bytes 262144 | tf_op jit(solution)/shard_map/all_to_all | solution.py:134
  244.0 13.0 %copy-start.2 = (bf16[8,64,128]{2,1,0:T(8,128)(2,1)S(1)}, bf16[8,64,128]{2,1,0:T(8,128)(2,1)}, u32[]{:S(2)}) copy-start(bf16[8,64,128]{2,1,0:T(8,128)(2,1)} %all_to_all.30) | copy-start | bytes 393220
  244.0 14.3 %copy-start.9 = (s32[8]{0:T(128)S(1)}, s32[8]{0:T(128)}, u32[]{:S(2)}) copy-start(s32[8]{0:T(128)} %param.22) | copy-start | bytes 100
  244.0 147.4 %all-to-all-start.3 = ((bf16[64,272,128]{2,1,0:T(8,128)(2,1)}), bf16[64,272,128]{2,1,0:T(8,128)(2,1)}, u32[]{:S(2)}, u32[]{:S(2)}) async-start(bf16[64,272,128]{2,1,0:T(8,128)(2,1)} %shard_map.137), calls=%async_computation.3 | async-start | bytes 8912896 | tf_op jit(solution)/shard_map/all_to_all | solution.py:112

commit v9 on v7

--- a/solution.py
+++ b/solution.py
@@ -6,7 +6,8 @@
 from jax.sharding import PartitionSpec as P
 
 EPSILON = 1e-06
-HUB_PAD = 16
+HUB_PAD = 8
+WINDOW = 16
 
 
 def routing(out_dest, recv_target, block_count, node_count):
@@ -28,15 +29,16 @@
         return carry
 
     lax.fori_loop(0, node_count, clear, 0, unroll=8)
+    window_rows = lax.broadcasted_iota(jnp.int32, (WINDOW, col_count), 0)
     lanes = lax.broadcasted_iota(jnp.int32, (HUB_PAD, col_count), 0)
     hub = jnp.zeros((HUB_PAD, col_count), jnp.float32)
     for index in range(hub_ref.shape[0]):
         vertex = hub_ref[index]
         block = vertex // tile_side
         row = vertex % tile_side
-        start = pl.multiple_of((row // HUB_PAD) * HUB_PAD, HUB_PAD)
-        window = blocks_ref[block, pl.ds(start, HUB_PAD), :].astype(jnp.float32)
-        picked = jnp.sum(jnp.where(lanes == row % HUB_PAD, window, 0.0), axis=0, keepdims=True)
+        start = pl.multiple_of((row // WINDOW) * WINDOW, WINDOW)
+        window = blocks_ref[block, pl.ds(start, WINDOW), :].astype(jnp.float32)
+        picked = jnp.sum(jnp.where(window_rows == row % WINDOW, window, 0.0), axis=0, keepdims=True)
         hub = jnp.where(lanes == index, picked, hub)
     hub = hub.astype(out_ref.dtype)
 

time: 394 us -> 380 us (0.964)
  waiting for transfers between devices: 229 us -> 217 us
  starting transfers between devices: 72.7 us -> 76.7 us
    all_to_all x2, waiting for transfers between devices: 179 us -> 166 us  [aggregate(): lax.all_to_all(payload, 'dom', split_axis=0, concat_axis=0, tiled=True)]
    all_to_all x2, starting transfers between devices: 11.5 us -> 15.5 us  [feat_to_rows(): lax.all_to_all(pieces, 'feat', split_axis=0, concat_axis=0, tiled=True)]
    unnamed x41 -> x39, local copies, waits for them, and re-layouts: 13.2 us -> 13.2 us
where the time goes in v9:
time: 380 us; the launch traced here: 379 us
  waiting for transfers between devices  217 us (57%)
  starting transfers between devices  76.7 us (20%)
  blocking collectives  27.6 us (7%)
  local copies, waits for them, and re-layouts  25.2 us (7%)
  matrix products  15.7 us (4%)
  Pallas kernels  13.6 us (4%)
    all_to_all x2, waiting for transfers between devices, aggregate(): lax.all_to_all(payload, 'dom', split_axis=0, concat_axis=0, tiled=True)  166 us
    ppermute x7, waiting for transfers between devices, gather_weights(): pieces.append(lax.ppermute(stacked, 'feat', pairs))  45.5 us
    ppermute x7, starting transfers between devices, gather_weights(): pieces.append(lax.ppermute(stacked, 'feat', pairs))  37.2 us
    all_to_all x2, starting transfers between devices, aggregate(): lax.all_to_all(payload, 'dom', split_axis=0, concat_axis=0, tiled=True)  24 us
    all_to_all x2, blocking collectives, rows_to_feat(): lax.all_to_all(pieces, 'feat', split_axis=0, concat_axis=0, tiled=True)  17.7 us
    all_to_all x2, starting transfers between devices, feat_to_rows(): lax.all_to_all(pieces, 'feat', split_axis=0, concat_axis=0, tiled=True)  15.5 us
    pallas_call x2, Pallas kernels, build_payload(): pl.pallas_call(payload_kernel, out_shape=jax.ShapeDtypeStruct((node_count...  13.6 us
    unnamed x39, local copies, waits for them, and re-layouts  13.2 us
  transfers between devices with their start and end apart: 11, of which 8 were waited for; matrix products, arithmetic and copies ran while one was open for 5% of the time, Pallas kernels for 2%

profile of v9, /device:TPU:40, one launch (start us, length us, event | category | flops | bytes accessed | tf_op | source)
XLA Modules:
  0.0 379.2 jit_solution(17457053161180219529)
XLA Ops:
  0.0 4.4 %all-to-all-start = ((bf16[8,64,128]{2,1,0:T(8,128)(2,1)}), bf16[8,64,128]{2,1,0:T(8,128)(2,1)S(1)}, u32[]{:S(2)}, u32[]{:S(2)}) async-start(bf16[8,64,128]{2,1,0:T(8,128)(2,1)} %bitcast.132), calls=%async_computation | async-start | bytes 262144 | tf_op jit(solution)/shard_map/all_to_all | solution.py:136
  4.4 6.8 %shard_map.136 = bf16[64,264,128]{2,1,0:T(8,128)(2,1)} custom-call(s32[64]{0:T(128)} %bitcast.145, s32[64]{0:T(128)} %src_ref.3, s32[2]{0:T(128)} %hub_ref.3, bf16[64,128,128]{2,1,0:T(8,128)(2,1)} %tiles_ref.3, bf16[4,128,128]{2,1,0:T(8,128)(2,1)} %bitcast.133), custom_call_target="tpu_custom_call" | custom-call | tf_op jit(solution)/shard_map/pallas_call | solution.py:69
  11.3 16.4 %all-to-all-start.1 = ((bf16[64,264,128]{2,1,0:T(8,128)(2,1)}), bf16[64,264,128]{2,1,0:T(8,128)(2,1)}, u32[]{:S(2)}, u32[]{:S(2)}) async-start(bf16[64,264,128]{2,1,0:T(8,128)(2,1)} %shard_map.136), calls=%async_computation.1 | async-start | bytes 8650752 | tf_op jit(solution)/shard_map/all_to_all | solution.py:114
  27.8 1.4 fusion.25
  29.2 3.9 %collective-permute-start.1 = (bf16[2,2056,128]{2,1,0:T(8,128)(2,1)S(1)}, bf16[2,2056,128]{2,1,0:T(8,128)(2,1)}, u32[]{:S(2)}, u32[]{:S(2)}) collective-permute-start(bf16[2,2056,128]{2,1,0:T(8,128)(2,1)S(1)} %get-tuple-element.24), channel_id=1, source_target_pairs={{0,2},{1,3},{2,4},{3,5},{4,6},{5,7},{6,0},{7,1},{8,10},{9,11},{10,... | collective-permute-start | bytes 3158024 | tf_op jit(solution)/shard_map/ppermute | solution.py:166
  33.1 4.0 %collective-permute-start.2 = (bf16[2,2056,128]{2,1,0:T(8,128)(2,1)S(1)}, bf16[2,2056,128]{2,1,0:T(8,128)(2,1)}, u32[]{:S(2)}, u32[]{:S(2)}) collective-permute-start(bf16[2,2056,128]{2,1,0:T(8,128)(2,1)S(1)} %get-tuple-element.24), channel_id=1, source_target_pairs={{0,3},{1,4},{2,5},{3,6},{4,7},{5,0},{6,1},{7,2},{8,11},{9,12},{10,... | collective-permute-start | bytes 3158024 | tf_op jit(solution)/shard_map/ppermute | solution.py:166
  37.1 4.0 %collective-permute-start.3 = (bf16[2,2056,128]{2,1,0:T(8,128)(2,1)S(1)}, bf16[2,2056,128]{2,1,0:T(8,128)(2,1)}, u32[]{:S(2)}, u32[]{:S(2)}) collective-permute-start(bf16[2,2056,128]{2,1,0:T(8,128)(2,1)S(1)} %get-tuple-element.24), channel_id=1, source_target_pairs={{0,4},{1,5},{2,6},{3,7},{4,0},{5,1},{6,2},{7,3},{8,12},{9,13},{10,... | collective-permute-start | bytes 3158024 | tf_op jit(solution)/shard_map/ppermute | solution.py:166
  41.1 3.4 collective-permute-start.4
  44.5 0.6 gather_fusion
  45.2 0.3 convolution_bitcast_fusion.1
  45.5 0.2 copy.41
  45.7 0.8 copy.38
  46.5 0.1 eq.17
  46.7 0.7 convert_element_type.43
  47.4 1.0 fusion.38
  48.4 5.1 %collective-permute-done = bf16[2,2056,128]{2,1,0:T(8,128)(2,1)} collective-permute-done((bf16[2,2056,128]{2,1,0:T(8,128)(2,1)S(1)}, bf16[2,2056,128]{2,1,0:T(8,128)(2,1)}, u32[]{:S(2)}, u32[]{:S(2)}) %collective-permute-start) | collective-permute-done | bytes 1052704 | tf_op jit(solution)/shard_map/ppermute | solution.py:166
  53.5 3.9 %collective-permute-start.5 = (bf16[2,2056,128]{2,1,0:T(8,128)(2,1)S(1)}, bf16[2,2056,128]{2,1,0:T(8,128)(2,1)S(1)}, u32[]{:S(2)}, u32[]{:S(2)}) collective-permute-start(bf16[2,2056,128]{2,1,0:T(8,128)(2,1)S(1)} %get-tuple-element.24), channel_id=1, source_target_pairs={{0,6},{1,7},{2,0},{3,1},{4,2},{5,3},{6,4},{7,5},{8,14},{9,15},{10,... | collective-permute-start | bytes 3158024 | tf_op jit(solution)/shard_map/ppermute | solution.py:166
  57.4 2.4 constant_dynamic-update-slice_fusion.6
  59.8 18.0 %collective-permute-start.6 = (bf16[2,2056,128]{2,1,0:T(8,128)(2,1)S(1)}, bf16[2,2056,128]{2,1,0:T(8,128)(2,1)S(1)}, u32[]{:S(2)}, u32[]{:S(2)}) collective-permute-start(bf16[2,2056,128]{2,1,0:T(8,128)(2,1)S(1)} %get-tuple-element.24), channel_id=1, source_target_pairs={{0,7},{1,0},{2,1},{3,2},{4,3},{5,4},{6,5},{7,6},{8,15},{9,8},{10,9... | collective-permute-start | bytes 3158024 | tf_op jit(solution)/shard_map/ppermute | solution.py:166
  77.8 2.4 constant_dynamic-update-slice_fusion.5
  80.2 19.9 %collective-permute-done.2 = bf16[2,2056,128]{2,1,0:T(8,128)(2,1)} collective-permute-done((bf16[2,2056,128]{2,1,0:T(8,128)(2,1)S(1)}, bf16[2,2056,128]{2,1,0:T(8,128)(2,1)}, u32[]{:S(2)}, u32[]{:S(2)}) %collective-permute-start.2) | collective-permute-done | bytes 1052704 | tf_op jit(solution)/shard_map/ppermute | solution.py:166
  100.1 2.3 constant_dynamic-update-slice_fusion.4
  102.4 2.7 collective-permute-done.3
  105.1 2.3 constant_dynamic-update-slice_fusion.3
  107.5 14.5 %collective-permute-done.4 = bf16[2,2056,128]{2,1,0:T(8,128)(2,1)S(1)} collective-permute-done((bf16[2,2056,128]{2,1,0:T(8,128)(2,1)S(1)}, bf16[2,2056,128]{2,1,0:T(8,128)(2,1)S(1)}, u32[]{:S(2)}, u32[]{:S(2)}) %collective-permute-start.4) | collective-permute-done | bytes 1052704 | tf_op jit(solution)/shard_map/ppermute | solution.py:166
  121.9 1.2 constant_dynamic-update-slice_fusion.2
  123.1 1.1 constant_dynamic-update-slice_fusion.1
  124.2 3.3 collective-permute-done.6
  127.5 1.1 constant_dynamic-update-slice_fusion
  128.6 36.5 %all-to-all-done.1 = bf16[64,264,128]{2,1,0:T(8,128)(2,1)} async-done(((bf16[64,264,128]{2,1,0:T(8,128)(2,1)}), bf16[64,264,128]{2,1,0:T(8,128)(2,1)}, u32[]{:S(2)}, u32[]{:S(2)}) %all-to-all-start.1) | async-done | bytes 4325408 | tf_op jit(solution)/shard_map/all_to_all | solution.py:114
  165.1 2.5 slice.81
  167.6 2.3 fusion.13
  169.9 0.1 copy.43
  170.1 0.9 slice.82
  171.0 0.2 fusion.23
  171.2 0.8 copy.44
  172.0 11.1 %all-to-all-start.2 = ((bf16[8,64,128]{2,1,0:T(8,128)(2,1)}), bf16[8,64,128]{2,1,0:T(8,128)(2,1)S(1)}, u32[]{:S(2)}, u32[]{:S(2)}) async-start(bf16[8,64,128]{2,1,0:T(8,128)(2,1)} %bitcast.15), calls=%async_computation.2 | async-start | bytes 262144 | tf_op jit(solution)/shard_map/all_to_all | solution.py:136
  183.1 0.7 slice_convert_fusion.1
  183.8 5.4 %all-to-all-done.2 = bf16[8,64,128]{2,1,0:T(8,128)(2,1)S(1)} async-done(((bf16[8,64,128]{2,1,0:T(8,128)(2,1)}), bf16[8,64,128]{2,1,0:T(8,128)(2,1)S(1)}, u32[]{:S(2)}, u32[]{:S(2)}) %all-to-all-start.2) | async-done | bytes 131104 | tf_op jit(solution)/shard_map/all_to_all | solution.py:136
  189.2 2.1 fusion.7
  191.3 2.2 multiply_reduce_fusion.1
  193.5 0.1 copy_bitcast_fusion.2
  193.6 0.6 gather_fusion.2
  194.3 9.2 %all_to_all.35 = bf16[8,64,128]{2,1,0:T(8,128)(2,1)} all-to-all(bf16[8,64,128]{2,1,0:T(8,128)(2,1)S(1)} %broadcast_select_fusion), channel_id=1, replica_groups=mesh['dom'=64,'feat'=8] {'feat'}, dimensions={0} | all-to-all | bytes 262144 | tf_op jit(solution)/shard_map/all_to_all | solution.py:144
  203.5 6.8 %shard_map.137 = bf16[64,264,128]{2,1,0:T(8,128)(2,1)} custom-call(s32[64]{0:T(128)} %bitcast.146, s32[64]{0:T(128)} %src_ref.3, s32[2]{0:T(128)} %hub_ref.3, bf16[64,128,128]{2,1,0:T(8,128)(2,1)} %tiles_ref.3, bf16[4,128,128]{2,1,0:T(8,128)(2,1)} %bitcast.135), custom_call_target="tpu_custom_call" | custom-call | tf_op jit(solution)/shard_map/pallas_call | solution.py:69
  210.3 7.5 %all-to-all-start.4 = ((bf16[64,264,128]{2,1,0:T(8,128)(2,1)}), bf16[64,264,128]{2,1,0:T(8,128)(2,1)}, u32[]{:S(2)}, u32[]{:S(2)}) async-start(bf16[64,264,128]{2,1,0:T(8,128)(2,1)} %shard_map.137), calls=%async_computation.4 | async-start | bytes 8650752 | tf_op jit(solution)/shard_map/all_to_all | solution.py:114
  217.8 0.6 gather_fusion.1
  218.4 0.3 convolution_bitcast_fusion
  218.7 0.2 copy.50
  219.0 0.4 fusion.36
  219.4 129.4 %all-to-all-done.4 = bf16[64,264,128]{2,1,0:T(8,128)(2,1)} async-done(((bf16[64,264,128]{2,1,0:T(8,128)(2,1)}), bf16[64,264,128]{2,1,0:T(8,128)(2,1)}, u32[]{:S(2)}, u32[]{:S(2)}) %all-to-all-start.4) | async-done | bytes 4325408 | tf_op jit(solution)/shard_map/all_to_all | solution.py:114
  348.8 2.5 slice.85
  351.3 2.3 fusion.16
  353.6 0.2 copy.51
  353.8 0.9 slice.86
  354.7 0.2 fusion.24
  354.9 0.1 copy.52
  355.1 9.9 %all_to_all.36 = bf16[8,64,128]{2,1,0:T(8,128)(2,1)S(1)} all-to-all(bf16[8,64,128]{2,1,0:T(8,128)(2,1)S(1)} %bitcast.138), channel_id=1, replica_groups=mesh['dom'=64,'feat'=8] {'feat'}, dimensions={0} | all-to-all | bytes 262144 | tf_op jit(solution)/shard_map/all_to_all | solution.py:136
  364.9 2.1 fusion.5
  367.0 2.2 multiply_reduce_fusion
  369.2 0.1 copy_bitcast_fusion.1
  369.4 0.6 gather_fusion.3
  370.0 8.5 %all_to_all.37 = bf16[8,64,128]{2,1,0:T(8,128)(2,1)S(1)} all-to-all(bf16[8,64,128]{2,1,0:T(8,128)(2,1)S(1)} %broadcast_select_fusion.1), channel_id=1, replica_groups=mesh['dom'=64,'feat'=8] {'feat'}, dimensions={0} | all-to-all | bytes 262144 | tf_op jit(solution)/shard_map/all_to_all | solution.py:144
  378.5 0.7 copy.99
  (45 shorter events, 0.3 us)
Async XLA Ops:
  0.0 45.1 %copy-start = (bf16[8,128,128]{2,1,0:T(8,128)(2,1)S(1)}, bf16[8,128,128]{2,1,0:T(8,128)(2,1)}, u32[]{:S(2)}) copy-start(bf16[8,128,128]{2,1,0:T(8,128)(2,1)} %param.24) | copy-start | bytes 786436
  0.0 11.2 %all-to-all-start = ((bf16[8,64,128]{2,1,0:T(8,128)(2,1)}), bf16[8,64,128]{2,1,0:T(8,128)(2,1)S(1)}, u32[]{:S(2)}, u32[]{:S(2)}) async-start(bf16[8,64,128]{2,1,0:T(8,128)(2,1)} %bitcast.132), calls=%async_computation | async-start | bytes 262144 | tf_op jit(solution)/shard_map/all_to_all | solution.py:136
  11.2 16.5 %copy-start.13 = (bf16[2,128]{1,0:T(2,128)(2,1)S(1)}, bf16[2,128]{1,0:T(2,128)(2,1)}, u32[]{:S(2)}) copy-start(bf16[2,128]{1,0:T(2,128)(2,1)} %param.31) | copy-start | bytes 1540
  11.3 16.5 %copy-start.3 = (bf16[2,1024,128]{2,1,0:T(8,128)(2,1)S(1)}, bf16[2,1024,128]{2,1,0:T(8,128)(2,1)}, u32[]{:S(2)}) copy-start(bf16[2,1024,128]{2,1,0:T(8,128)(2,1)} %param.30) | copy-start | bytes 1572868
  11.3 16.5 %copy-start.4 = (bf16[2,1024,128]{2,1,0:T(8,128)(2,1)S(1)}, bf16[2,1024,128]{2,1,0:T(8,128)(2,1)}, u32[]{:S(2)}) copy-start(bf16[2,1024,128]{2,1,0:T(8,128)(2,1)} %param.29) | copy-start | bytes 1572868
  11.3 33.2 %copy-start.14 = (s32[8]{0:T(128)S(1)}, s32[8]{0:T(128)}, u32[]{:S(2)}) copy-start(s32[8]{0:T(128)} %param.23) | copy-start | bytes 100
  11.3 33.2 %copy-start.1 = (bf16[512,128]{1,0:T(8,128)(2,1)S(1)}, bf16[512,128]{1,0:T(8,128)(2,1)}, u32[]{:S(2)}) copy-start(bf16[512,128]{1,0:T(8,128)(2,1)} %param.18) | copy-start | bytes 393220
  11.3 153.8 %all-to-all-start.1 = ((bf16[64,264,128]{2,1,0:T(8,128)(2,1)}), bf16[64,264,128]{2,1,0:T(8,128)(2,1)}, u32[]{:S(2)}, u32[]{:S(2)}) async-start(bf16[64,264,128]{2,1,0:T(8,128)(2,1)} %shard_map.136), calls=%async_computation.1 | async-start | bytes 8650752 | tf_op jit(solution)/shard_map/all_to_all | solution.py:114
  29.2 24.3 %collective-permute-start = (bf16[2,2056,128]{2,1,0:T(8,128)(2,1)S(1)}, bf16[2,2056,128]{2,1,0:T(8,128)(2,1)}, u32[]{:S(2)}, u32[]{:S(2)}) collective-permute-start(bf16[2,2056,128]{2,1,0:T(8,128)(2,1)S(1)} %get-tuple-element.24), channel_id=1, source_target_pairs={{0,1},{1,2},{2,3},{3,4},{4,5},{5,6},{6,7},{7,0},{8,9},{9,10},{10,1... | collective-permute-start | bytes 3158024 | tf_op jit(solution)/shard_map/ppermute | solution.py:166
  29.2 30.6 %collective-permute-start.1 = (bf16[2,2056,128]{2,1,0:T(8,128)(2,1)S(1)}, bf16[2,2056,128]{2,1,0:T(8,128)(2,1)}, u32[]{:S(2)}, u32[]{:S(2)}) collective-permute-start(bf16[2,2056,128]{2,1,0:T(8,128)(2,1)S(1)} %get-tuple-element.24), channel_id=1, source_target_pairs={{0,2},{1,3},{2,4},{3,5},{4,6},{5,7},{6,0},{7,1},{8,10},{9,11},{10,... | collective-permute-start | bytes 3158024 | tf_op jit(solution)/shard_map/ppermute | solution.py:166
  33.1 67.0 %collective-permute-start.2 = (bf16[2,2056,128]{2,1,0:T(8,128)(2,1)S(1)}, bf16[2,2056,128]{2,1,0:T(8,128)(2,1)}, u32[]{:S(2)}, u32[]{:S(2)}) collective-permute-start(bf16[2,2056,128]{2,1,0:T(8,128)(2,1)S(1)} %get-tuple-element.24), channel_id=1, source_target_pairs={{0,3},{1,4},{2,5},{3,6},{4,7},{5,0},{6,1},{7,2},{8,11},{9,12},{10,... | collective-permute-start | bytes 3158024 | tf_op jit(solution)/shard_map/ppermute | solution.py:166
  37.1 68.0 %collective-permute-start.3 = (bf16[2,2056,128]{2,1,0:T(8,128)(2,1)S(1)}, bf16[2,2056,128]{2,1,0:T(8,128)(2,1)}, u32[]{:S(2)}, u32[]{:S(2)}) collective-permute-start(bf16[2,2056,128]{2,1,0:T(8,128)(2,1)S(1)} %get-tuple-element.24), channel_id=1, source_target_pairs={{0,4},{1,5},{2,6},{3,7},{4,0},{5,1},{6,2},{7,3},{8,12},{9,13},{10,... | collective-permute-start | bytes 3158024 | tf_op jit(solution)/shard_map/ppermute | solution.py:166
  41.1 80.9 %collective-permute-start.4 = (bf16[2,2056,128]{2,1,0:T(8,128)(2,1)S(1)}, bf16[2,2056,128]{2,1,0:T(8,128)(2,1)S(1)}, u32[]{:S(2)}, u32[]{:S(2)}) collective-permute-start(bf16[2,2056,128]{2,1,0:T(8,128)(2,1)S(1)} %get-tuple-element.24), channel_id=1, source_target_pairs={{0,5},{1,6},{2,7},{3,0},{4,1},{5,2},{6,3},{7,4},{8,13},{9,14},{10,... | collective-permute-start | bytes 3158024 | tf_op jit(solution)/shard_map/ppermute | solution.py:166
  46.6 120.9 %copy-start.5 = (s32[128]{0:T(128)}, s32[128]{0:T(128)S(1)}, u32[]{:S(2)}) copy-start(s32[128]{0:T(128)S(1)} %eq.17) | copy-start | bytes 1540
  47.3 123.7 %copy-start.9 = (f32[512]{0:T(512)}, f32[512]{0:T(512)S(1)}, u32[]{:S(2)}) copy-start(f32[512]{0:T(512)S(1)} %convert_element_type.43) | copy-start | bytes 6148
  47.4 146.8 %copy-start.7 = (pred[8]{0:T(512)(128)(4,1)}, pred[8]{0:T(512)(128)(4,1)S(1)}, u32[]{:S(2)}) copy-start(pred[8]{0:T(512)(128)(4,1)S(1)} %compare_and_fusion) | copy-start | bytes 28
  53.5 69.6 %collective-permute-start.5 = (bf16[2,2056,128]{2,1,0:T(8,128)(2,1)S(1)}, bf16[2,2056,128]{2,1,0:T(8,128)(2,1)S(1)}, u32[]{:S(2)}, u32[]{:S(2)}) collective-permute-start(bf16[2,2056,128]{2,1,0:T(8,128)(2,1)S(1)} %get-tuple-element.24), channel_id=1, source_target_pairs={{0,6},{1,7},{2,0},{3,1},{4,2},{5,3},{6,4},{7,5},{8,14},{9,15},{10,... | collective-permute-start | bytes 3158024 | tf_op jit(solution)/shard_map/ppermute | solution.py:166
  59.8 67.7 %collective-permute-start.6 = (bf16[2,2056,128]{2,1,0:T(8,128)(2,1)S(1)}, bf16[2,2056,128]{2,1,0:T(8,128)(2,1)S(1)}, u32[]{:S(2)}, u32[]{:S(2)}) collective-permute-start(bf16[2,2056,128]{2,1,0:T(8,128)(2,1)S(1)} %get-tuple-element.24), channel_id=1, source_target_pairs={{0,7},{1,0},{2,1},{3,2},{4,3},{5,4},{6,5},{7,6},{8,15},{9,8},{10,9... | collective-permute-start | bytes 3158024 | tf_op jit(solution)/shard_map/ppermute | solution.py:166
  167.6 3.5 copy-start.12
  172.0 17.2 %all-to-all-start.2 = ((bf16[8,64,128]{2,1,0:T(8,128)(2,1)}), bf16[8,64,128]{2,1,0:T(8,128)(2,1)S(1)}, u32[]{:S(2)}, u32[]{:S(2)}) async-start(bf16[8,64,128]{2,1,0:T(8,128)(2,1)} %bitcast.15), calls=%async_computation.2 | async-start | bytes 262144 | tf_op jit(solution)/shard_map/all_to_all | solution.py:136
  210.3 7.5 %copy-start.2 = (bf16[8,64,128]{2,1,0:T(8,128)(2,1)S(1)}, bf16[8,64,128]{2,1,0:T(8,128)(2,1)}, u32[]{:S(2)}) copy-start(bf16[8,64,128]{2,1,0:T(8,128)(2,1)} %all_to_all.35) | copy-start | bytes 393220
  210.3 8.7 %copy-start.11 = (s32[8]{0:T(128)S(1)}, s32[8]{0:T(128)}, u32[]{:S(2)}) copy-start(s32[8]{0:T(128)} %param.22) | copy-start | bytes 100
  210.3 138.5 %all-to-all-start.4 = ((bf16[64,264,128]{2,1,0:T(8,128)(2,1)}), bf16[64,264,128]{2,1,0:T(8,128)(2,1)}, u32[]{:S(2)}, u32[]{:S(2)}) async-start(bf16[64,264,128]{2,1,0:T(8,128)(2,1)} %shard_map.137), calls=%async_computation.4 | async-start | bytes 8650752 | tf_op jit(solution)/shard_map/all_to_all | solution.py:114
  219.3 131.9 %copy-start.6 = (s32[128]{0:T(128)S(1)}, s32[128]{0:T(128)}, u32[]{:S(2)}) copy-start(s32[128]{0:T(128)} %copy-done.5) | copy-start | bytes 1540
  351.3 3.5 copy-start.10
  351.3 15.7 %copy-start.8 = (pred[8]{0:T(512)(128)(4,1)S(1)}, pred[8]{0:T(512)(128)(4,1)}, u32[]{:S(2)}) copy-start(pred[8]{0:T(512)(128)(4,1)} %copy-done.7) | copy-start | bytes 28

commit v10 on v9

--- a/solution.py
+++ b/solution.py
@@ -59,7 +59,7 @@
         out_ref[node, pl.ds(first, tile_side), :] = product.astype(out_ref.dtype)
         return carry
 
-    lax.fori_loop(0, tile_count, put_tile, 0, unroll=8)
+    lax.fori_loop(0, tile_count, put_tile, 0, unroll=True)
 
 
 def build_payload(destination, sources, hubs, tiles, blocks, node_count, capacity):

time: 380 us -> 385 us (1.013)
  starting transfers between devices: 76.7 us -> 82.7 us
    all_to_all x2, starting transfers between devices: 15.5 us -> 22.4 us  [feat_to_rows(): lax.all_to_all(pieces, 'feat', split_axis=0, concat_axis=0, tiled=True)]
  transfers between devices with their start and end apart: 11 -> 11, of which waited for: 8 -> 9; matrix products, arithmetic and copies ran while one was open for 5% -> 5% of each run, Pallas kernels for 2% -> 1%
where the time goes in v10:
time: 385 us; the launch traced here: 384 us
  waiting for transfers between devices  215 us (56%)
  starting transfers between devices  82.7 us (21%)
  blocking collectives  29.7 us (8%)
  local copies, waits for them, and re-layouts  25.2 us (7%)
  matrix products  15.7 us (4%)
  Pallas kernels  11.3 us (3%)
    all_to_all x2, waiting for transfers between devices, aggregate(): lax.all_to_all(payload, 'dom', split_axis=0, concat_axis=0, tiled=True)  163 us
    ppermute x7, waiting for transfers between devices, gather_weights(): pieces.append(lax.ppermute(stacked, 'feat', pairs))  46.1 us
    ppermute x7, starting transfers between devices, gather_weights(): pieces.append(lax.ppermute(stacked, 'feat', pairs))  36.3 us
    all_to_all x2, starting transfers between devices, aggregate(): lax.all_to_all(payload, 'dom', split_axis=0, concat_axis=0, tiled=True)  24 us
    all_to_all x2, starting transfers between devices, feat_to_rows(): lax.all_to_all(pieces, 'feat', split_axis=0, concat_axis=0, tiled=True)  22.4 us
    all_to_all x2, blocking collectives, rows_to_feat(): lax.all_to_all(pieces, 'feat', split_axis=0, concat_axis=0, tiled=True)  17.7 us
    unnamed x39, local copies, waits for them, and re-layouts  13.2 us
    all_to_all x1, blocking collectives, feat_to_rows(): lax.all_to_all(pieces, 'feat', split_axis=0, concat_axis=0, tiled=True)  12 us
  transfers between devices with their start and end apart: 11, of which 9 were waited for; matrix products, arithmetic and copies ran while one was open for 5% of the time, Pallas kernels for 1%

profile of v10, /device:TPU:40, one launch (start us, length us, event | category | flops | bytes accessed | tf_op | source)
XLA Modules:
  0.0 383.5 jit_solution(15570123509451020072)
XLA Ops:
  0.0 4.4 %all-to-all-start = ((bf16[8,64,128]{2,1,0:T(8,128)(2,1)}), bf16[8,64,128]{2,1,0:T(8,128)(2,1)S(1)}, u32[]{:S(2)}, u32[]{:S(2)}) async-start(bf16[8,64,128]{2,1,0:T(8,128)(2,1)} %bitcast.132), calls=%async_computation | async-start | bytes 262144 | tf_op jit(solution)/shard_map/all_to_all | solution.py:136
  4.4 5.7 %shard_map.136 = bf16[64,264,128]{2,1,0:T(8,128)(2,1)} custom-call(s32[64]{0:T(128)} %bitcast.145, s32[64]{0:T(128)} %src_ref.3, s32[2]{0:T(128)} %hub_ref.3, bf16[64,128,128]{2,1,0:T(8,128)(2,1)} %tiles_ref.3, bf16[4,128,128]{2,1,0:T(8,128)(2,1)} %bitcast.133), custom_call_target="tpu_custom_call" | custom-call | tf_op jit(solution)/shard_map/pallas_call | solution.py:69
  10.1 0.5 all-to-all-done
  10.7 16.4 %all-to-all-start.1 = ((bf16[64,264,128]{2,1,0:T(8,128)(2,1)}), bf16[64,264,128]{2,1,0:T(8,128)(2,1)}, u32[]{:S(2)}, u32[]{:S(2)}) async-start(bf16[64,264,128]{2,1,0:T(8,128)(2,1)} %shard_map.136), calls=%async_computation.1 | async-start | bytes 8650752 | tf_op jit(solution)/shard_map/all_to_all | solution.py:114
  27.1 1.4 fusion.25
  28.5 3.5 collective-permute-start.1
  32.0 4.0 %collective-permute-start.2 = (bf16[2,2056,128]{2,1,0:T(8,128)(2,1)S(1)}, bf16[2,2056,128]{2,1,0:T(8,128)(2,1)}, u32[]{:S(2)}, u32[]{:S(2)}) collective-permute-start(bf16[2,2056,128]{2,1,0:T(8,128)(2,1)S(1)} %get-tuple-element.24), channel_id=1, source_target_pairs={{0,3},{1,4},{2,5},{3,6},{4,7},{5,0},{6,1},{7,2},{8,11},{9,12},{10,... | collective-permute-start | bytes 3158024 | tf_op jit(solution)/shard_map/ppermute | solution.py:166
  36.0 4.0 %collective-permute-start.3 = (bf16[2,2056,128]{2,1,0:T(8,128)(2,1)S(1)}, bf16[2,2056,128]{2,1,0:T(8,128)(2,1)}, u32[]{:S(2)}, u32[]{:S(2)}) collective-permute-start(bf16[2,2056,128]{2,1,0:T(8,128)(2,1)S(1)} %get-tuple-element.24), channel_id=1, source_target_pairs={{0,4},{1,5},{2,6},{3,7},{4,0},{5,1},{6,2},{7,3},{8,12},{9,13},{10,... | collective-permute-start | bytes 3158024 | tf_op jit(solution)/shard_map/ppermute | solution.py:166
  39.9 3.4 collective-permute-start.4
  43.4 0.6 gather_fusion
  44.0 0.3 convolution_bitcast_fusion.1
  44.4 0.2 copy.41
  44.6 0.8 copy.38
  45.4 0.1 eq.17
  45.5 0.7 convert_element_type.43
  46.3 1.0 fusion.38
  47.3 5.6 %collective-permute-done = bf16[2,2056,128]{2,1,0:T(8,128)(2,1)} collective-permute-done((bf16[2,2056,128]{2,1,0:T(8,128)(2,1)S(1)}, bf16[2,2056,128]{2,1,0:T(8,128)(2,1)}, u32[]{:S(2)}, u32[]{:S(2)}) %collective-permute-start) | collective-permute-done | bytes 1052704 | tf_op jit(solution)/shard_map/ppermute | solution.py:166
  52.8 3.5 collective-permute-start.5
  56.3 2.4 constant_dynamic-update-slice_fusion.6
  58.7 18.0 %collective-permute-start.6 = (bf16[2,2056,128]{2,1,0:T(8,128)(2,1)S(1)}, bf16[2,2056,128]{2,1,0:T(8,128)(2,1)S(1)}, u32[]{:S(2)}, u32[]{:S(2)}) collective-permute-start(bf16[2,2056,128]{2,1,0:T(8,128)(2,1)S(1)} %get-tuple-element.24), channel_id=1, source_target_pairs={{0,7},{1,0},{2,1},{3,2},{4,3},{5,4},{6,5},{7,6},{8,15},{9,8},{10,9... | collective-permute-start | bytes 3158024 | tf_op jit(solution)/shard_map/ppermute | solution.py:166
  76.7 2.4 constant_dynamic-update-slice_fusion.5
  79.1 19.9 %collective-permute-done.2 = bf16[2,2056,128]{2,1,0:T(8,128)(2,1)} collective-permute-done((bf16[2,2056,128]{2,1,0:T(8,128)(2,1)S(1)}, bf16[2,2056,128]{2,1,0:T(8,128)(2,1)}, u32[]{:S(2)}, u32[]{:S(2)}) %collective-permute-start.2) | collective-permute-done | bytes 1052704 | tf_op jit(solution)/shard_map/ppermute | solution.py:166
  99.0 2.3 constant_dynamic-update-slice_fusion.4
  101.3 2.7 collective-permute-done.3
  104.0 2.3 constant_dynamic-update-slice_fusion.3
  106.3 14.5 %collective-permute-done.4 = bf16[2,2056,128]{2,1,0:T(8,128)(2,1)S(1)} collective-permute-done((bf16[2,2056,128]{2,1,0:T(8,128)(2,1)S(1)}, bf16[2,2056,128]{2,1,0:T(8,128)(2,1)S(1)}, u32[]{:S(2)}, u32[]{:S(2)}) %collective-permute-start.4) | collective-permute-done | bytes 1052704 | tf_op jit(solution)/shard_map/ppermute | solution.py:166
  120.8 1.2 constant_dynamic-update-slice_fusion.2
  122.0 1.1 constant_dynamic-update-slice_fusion.1
  123.1 3.5 collective-permute-done.6
  126.6 1.1 constant_dynamic-update-slice_fusion
  127.7 35.9 %all-to-all-done.1 = bf16[64,264,128]{2,1,0:T(8,128)(2,1)} async-done(((bf16[64,264,128]{2,1,0:T(8,128)(2,1)}), bf16[64,264,128]{2,1,0:T(8,128)(2,1)}, u32[]{:S(2)}, u32[]{:S(2)}) %all-to-all-start.1) | async-done | bytes 4325408 | tf_op jit(solution)/shard_map/all_to_all | solution.py:114
  163.6 2.5 slice.81
  166.1 2.3 fusion.13
  168.5 0.1 copy.43
  168.6 0.9 slice.82
  169.5 0.2 fusion.23
  169.8 0.8 copy.44
  170.5 18.0 %all-to-all-start.2 = ((bf16[8,64,128]{2,1,0:T(8,128)(2,1)}), bf16[8,64,128]{2,1,0:T(8,128)(2,1)S(1)}, u32[]{:S(2)}, u32[]{:S(2)}) async-start(bf16[8,64,128]{2,1,0:T(8,128)(2,1)} %bitcast.15), calls=%async_computation.2 | async-start | bytes 262144 | tf_op jit(solution)/shard_map/all_to_all | solution.py:136
  188.5 0.7 slice_convert_fusion.1
  189.2 5.4 %all-to-all-done.2 = bf16[8,64,128]{2,1,0:T(8,128)(2,1)S(1)} async-done(((bf16[8,64,128]{2,1,0:T(8,128)(2,1)}), bf16[8,64,128]{2,1,0:T(8,128)(2,1)S(1)}, u32[]{:S(2)}, u32[]{:S(2)}) %all-to-all-start.2) | async-done | bytes 131104 | tf_op jit(solution)/shard_map/all_to_all | solution.py:136
  194.6 2.1 fusion.7
  196.7 2.2 multiply_reduce_fusion.1
  198.9 0.1 copy_bitcast_fusion.2
  199.0 0.6 gather_fusion.2
  199.7 9.2 %all_to_all.35 = bf16[8,64,128]{2,1,0:T(8,128)(2,1)} all-to-all(bf16[8,64,128]{2,1,0:T(8,128)(2,1)S(1)} %broadcast_select_fusion), channel_id=1, replica_groups=mesh['dom'=64,'feat'=8] {'feat'}, dimensions={0} | all-to-all | bytes 262144 | tf_op jit(solution)/shard_map/all_to_all | solution.py:144
  208.9 5.7 %shard_map.137 = bf16[64,264,128]{2,1,0:T(8,128)(2,1)} custom-call(s32[64]{0:T(128)} %bitcast.146, s32[64]{0:T(128)} %src_ref.3, s32[2]{0:T(128)} %hub_ref.3, bf16[64,128,128]{2,1,0:T(8,128)(2,1)} %tiles_ref.3, bf16[4,128,128]{2,1,0:T(8,128)(2,1)} %bitcast.135), custom_call_target="tpu_custom_call" | custom-call | tf_op jit(solution)/shard_map/pallas_call | solution.py:69
  214.6 7.5 %all-to-all-start.4 = ((bf16[64,264,128]{2,1,0:T(8,128)(2,1)}), bf16[64,264,128]{2,1,0:T(8,128)(2,1)}, u32[]{:S(2)}, u32[]{:S(2)}) async-start(bf16[64,264,128]{2,1,0:T(8,128)(2,1)} %shard_map.137), calls=%async_computation.4 | async-start | bytes 8650752 | tf_op jit(solution)/shard_map/all_to_all | solution.py:114
  222.1 0.6 gather_fusion.1
  222.7 0.3 convolution_bitcast_fusion
  223.1 0.2 copy.50
  223.3 0.4 fusion.36
  223.7 127.2 %all-to-all-done.4 = bf16[64,264,128]{2,1,0:T(8,128)(2,1)} async-done(((bf16[64,264,128]{2,1,0:T(8,128)(2,1)}), bf16[64,264,128]{2,1,0:T(8,128)(2,1)}, u32[]{:S(2)}, u32[]{:S(2)}) %all-to-all-start.4) | async-done | bytes 4325408 | tf_op jit(solution)/shard_map/all_to_all | solution.py:114
  350.9 2.5 slice.85
  353.4 2.3 fusion.16
  355.8 0.2 copy.51
  355.9 0.9 slice.86
  356.9 0.2 fusion.24
  357.1 0.1 copy.52
  357.2 12.0 %all_to_all.36 = bf16[8,64,128]{2,1,0:T(8,128)(2,1)S(1)} all-to-all(bf16[8,64,128]{2,1,0:T(8,128)(2,1)S(1)} %bitcast.138), channel_id=1, replica_groups=mesh['dom'=64,'feat'=8] {'feat'}, dimensions={0} | all-to-all | bytes 262144 | tf_op jit(solution)/shard_map/all_to_all | solution.py:136
  369.2 2.1 fusion.5
  371.3 2.2 multiply_reduce_fusion
  373.7 0.6 gather_fusion.3
  374.3 8.5 %all_to_all.37 = bf16[8,64,128]{2,1,0:T(8,128)(2,1)S(1)} all-to-all(bf16[8,64,128]{2,1,0:T(8,128)(2,1)S(1)} %broadcast_select_fusion.1), channel_id=1, replica_groups=mesh['dom'=64,'feat'=8] {'feat'}, dimensions={0} | all-to-all | bytes 262144 | tf_op jit(solution)/shard_map/all_to_all | solution.py:144
  382.9 0.7 copy.99
  (45 shorter events, 0.4 us)
Async XLA Ops:
  0.0 44.0 %copy-start = (bf16[8,128,128]{2,1,0:T(8,128)(2,1)S(1)}, bf16[8,128,128]{2,1,0:T(8,128)(2,1)}, u32[]{:S(2)}) copy-start(bf16[8,128,128]{2,1,0:T(8,128)(2,1)} %param.24) | copy-start | bytes 786436
  0.0 10.6 %all-to-all-start = ((bf16[8,64,128]{2,1,0:T(8,128)(2,1)}), bf16[8,64,128]{2,1,0:T(8,128)(2,1)S(1)}, u32[]{:S(2)}, u32[]{:S(2)}) async-start(bf16[8,64,128]{2,1,0:T(8,128)(2,1)} %bitcast.132), calls=%async_computation | async-start | bytes 262144 | tf_op jit(solution)/shard_map/all_to_all | solution.py:136
  10.6 16.5 %copy-start.13 = (bf16[2,128]{1,0:T(2,128)(2,1)S(1)}, bf16[2,128]{1,0:T(2,128)(2,1)}, u32[]{:S(2)}) copy-start(bf16[2,128]{1,0:T(2,128)(2,1)} %param.31) | copy-start | bytes 1540
  10.6 16.5 %copy-start.3 = (bf16[2,1024,128]{2,1,0:T(8,128)(2,1)S(1)}, bf16[2,1024,128]{2,1,0:T(8,128)(2,1)}, u32[]{:S(2)}) copy-start(bf16[2,1024,128]{2,1,0:T(8,128)(2,1)} %param.30) | copy-start | bytes 1572868
  10.6 16.5 %copy-start.4 = (bf16[2,1024,128]{2,1,0:T(8,128)(2,1)S(1)}, bf16[2,1024,128]{2,1,0:T(8,128)(2,1)}, u32[]{:S(2)}) copy-start(bf16[2,1024,128]{2,1,0:T(8,128)(2,1)} %param.29) | copy-start | bytes 1572868
  10.6 32.8 %copy-start.14 = (s32[8]{0:T(128)S(1)}, s32[8]{0:T(128)}, u32[]{:S(2)}) copy-start(s32[8]{0:T(128)} %param.23) | copy-start | bytes 100
  10.6 32.8 %copy-start.1 = (bf16[512,128]{1,0:T(8,128)(2,1)S(1)}, bf16[512,128]{1,0:T(8,128)(2,1)}, u32[]{:S(2)}) copy-start(bf16[512,128]{1,0:T(8,128)(2,1)} %param.18) | copy-start | bytes 393220
  10.7 152.9 %all-to-all-start.1 = ((bf16[64,264,128]{2,1,0:T(8,128)(2,1)}), bf16[64,264,128]{2,1,0:T(8,128)(2,1)}, u32[]{:S(2)}, u32[]{:S(2)}) async-start(bf16[64,264,128]{2,1,0:T(8,128)(2,1)} %shard_map.136), calls=%async_computation.1 | async-start | bytes 8650752 | tf_op jit(solution)/shard_map/all_to_all | solution.py:114
  28.5 24.3 %collective-permute-start = (bf16[2,2056,128]{2,1,0:T(8,128)(2,1)S(1)}, bf16[2,2056,128]{2,1,0:T(8,128)(2,1)}, u32[]{:S(2)}, u32[]{:S(2)}) collective-permute-start(bf16[2,2056,128]{2,1,0:T(8,128)(2,1)S(1)} %get-tuple-element.24), channel_id=1, source_target_pairs={{0,1},{1,2},{2,3},{3,4},{4,5},{5,6},{6,7},{7,0},{8,9},{9,10},{10,1... | collective-permute-start | bytes 3158024 | tf_op jit(solution)/shard_map/ppermute | solution.py:166
  28.5 30.2 %collective-permute-start.1 = (bf16[2,2056,128]{2,1,0:T(8,128)(2,1)S(1)}, bf16[2,2056,128]{2,1,0:T(8,128)(2,1)}, u32[]{:S(2)}, u32[]{:S(2)}) collective-permute-start(bf16[2,2056,128]{2,1,0:T(8,128)(2,1)S(1)} %get-tuple-element.24), channel_id=1, source_target_pairs={{0,2},{1,3},{2,4},{3,5},{4,6},{5,7},{6,0},{7,1},{8,10},{9,11},{10,... | collective-permute-start | bytes 3158024 | tf_op jit(solution)/shard_map/ppermute | solution.py:166
  32.0 67.0 %collective-permute-start.2 = (bf16[2,2056,128]{2,1,0:T(8,128)(2,1)S(1)}, bf16[2,2056,128]{2,1,0:T(8,128)(2,1)}, u32[]{:S(2)}, u32[]{:S(2)}) collective-permute-start(bf16[2,2056,128]{2,1,0:T(8,128)(2,1)S(1)} %get-tuple-element.24), channel_id=1, source_target_pairs={{0,3},{1,4},{2,5},{3,6},{4,7},{5,0},{6,1},{7,2},{8,11},{9,12},{10,... | collective-permute-start | bytes 3158024 | tf_op jit(solution)/shard_map/ppermute | solution.py:166
  36.0 68.0 %collective-permute-start.3 = (bf16[2,2056,128]{2,1,0:T(8,128)(2,1)S(1)}, bf16[2,2056,128]{2,1,0:T(8,128)(2,1)}, u32[]{:S(2)}, u32[]{:S(2)}) collective-permute-start(bf16[2,2056,128]{2,1,0:T(8,128)(2,1)S(1)} %get-tuple-element.24), channel_id=1, source_target_pairs={{0,4},{1,5},{2,6},{3,7},{4,0},{5,1},{6,2},{7,3},{8,12},{9,13},{10,... | collective-permute-start | bytes 3158024 | tf_op jit(solution)/shard_map/ppermute | solution.py:166
  39.9 80.9 %collective-permute-start.4 = (bf16[2,2056,128]{2,1,0:T(8,128)(2,1)S(1)}, bf16[2,2056,128]{2,1,0:T(8,128)(2,1)S(1)}, u32[]{:S(2)}, u32[]{:S(2)}) collective-permute-start(bf16[2,2056,128]{2,1,0:T(8,128)(2,1)S(1)} %get-tuple-element.24), channel_id=1, source_target_pairs={{0,5},{1,6},{2,7},{3,0},{4,1},{5,2},{6,3},{7,4},{8,13},{9,14},{10,... | collective-permute-start | bytes 3158024 | tf_op jit(solution)/shard_map/ppermute | solution.py:166
  45.5 120.5 %copy-start.5 = (s32[128]{0:T(128)}, s32[128]{0:T(128)S(1)}, u32[]{:S(2)}) copy-start(s32[128]{0:T(128)S(1)} %eq.17) | copy-start | bytes 1540
  46.2 123.3 %copy-start.9 = (f32[512]{0:T(512)}, f32[512]{0:T(512)S(1)}, u32[]{:S(2)}) copy-start(f32[512]{0:T(512)S(1)} %convert_element_type.43) | copy-start | bytes 6148
  46.2 153.4 %copy-start.7 = (pred[8]{0:T(512)(128)(4,1)}, pred[8]{0:T(512)(128)(4,1)S(1)}, u32[]{:S(2)}) copy-start(pred[8]{0:T(512)(128)(4,1)S(1)} %compare_and_fusion) | copy-start | bytes 28
  52.8 69.1 %collective-permute-start.5 = (bf16[2,2056,128]{2,1,0:T(8,128)(2,1)S(1)}, bf16[2,2056,128]{2,1,0:T(8,128)(2,1)S(1)}, u32[]{:S(2)}, u32[]{:S(2)}) collective-permute-start(bf16[2,2056,128]{2,1,0:T(8,128)(2,1)S(1)} %get-tuple-element.24), channel_id=1, source_target_pairs={{0,6},{1,7},{2,0},{3,1},{4,2},{5,3},{6,4},{7,5},{8,14},{9,15},{10,... | collective-permute-start | bytes 3158024 | tf_op jit(solution)/shard_map/ppermute | solution.py:166
  58.7 67.9 %collective-permute-start.6 = (bf16[2,2056,128]{2,1,0:T(8,128)(2,1)S(1)}, bf16[2,2056,128]{2,1,0:T(8,128)(2,1)S(1)}, u32[]{:S(2)}, u32[]{:S(2)}) collective-permute-start(bf16[2,2056,128]{2,1,0:T(8,128)(2,1)S(1)} %get-tuple-element.24), channel_id=1, source_target_pairs={{0,7},{1,0},{2,1},{3,2},{4,3},{5,4},{6,5},{7,6},{8,15},{9,8},{10,9... | collective-permute-start | bytes 3158024 | tf_op jit(solution)/shard_map/ppermute | solution.py:166
  166.1 3.5 copy-start.12
  170.5 24.1 %all-to-all-start.2 = ((bf16[8,64,128]{2,1,0:T(8,128)(2,1)}), bf16[8,64,128]{2,1,0:T(8,128)(2,1)S(1)}, u32[]{:S(2)}, u32[]{:S(2)}) async-start(bf16[8,64,128]{2,1,0:T(8,128)(2,1)} %bitcast.15), calls=%async_computation.2 | async-start | bytes 262144 | tf_op jit(solution)/shard_map/all_to_all | solution.py:136
  214.6 7.5 %copy-start.2 = (bf16[8,64,128]{2,1,0:T(8,128)(2,1)S(1)}, bf16[8,64,128]{2,1,0:T(8,128)(2,1)}, u32[]{:S(2)}) copy-start(bf16[8,64,128]{2,1,0:T(8,128)(2,1)} %all_to_all.35) | copy-start | bytes 393220
  214.6 8.7 %copy-start.11 = (s32[8]{0:T(128)S(1)}, s32[8]{0:T(128)}, u32[]{:S(2)}) copy-start(s32[8]{0:T(128)} %param.22) | copy-start | bytes 100
  214.6 136.4 %all-to-all-start.4 = ((bf16[64,264,128]{2,1,0:T(8,128)(2,1)}), bf16[64,264,128]{2,1,0:T(8,128)(2,1)}, u32[]{:S(2)}, u32[]{:S(2)}) async-start(bf16[64,264,128]{2,1,0:T(8,128)(2,1)} %shard_map.137), calls=%async_computation.4 | async-start | bytes 8650752 | tf_op jit(solution)/shard_map/all_to_all | solution.py:114
  223.7 129.7 %copy-start.6 = (s32[128]{0:T(128)S(1)}, s32[128]{0:T(128)}, u32[]{:S(2)}) copy-start(s32[128]{0:T(128)} %copy-done.5) | copy-start | bytes 1540
  353.4 3.5 copy-start.10
  353.4 17.9 %copy-start.8 = (pred[8]{0:T(512)(128)(4,1)S(1)}, pred[8]{0:T(512)(128)(4,1)}, u32[]{:S(2)}) copy-start(pred[8]{0:T(512)(128)(4,1)} %copy-done.7) | copy-start | bytes 28

commit v11 on v9

--- a/solution.py
+++ b/solution.py
@@ -17,11 +17,10 @@
     return out_dest[:, 0].astype(jnp.int32), landing
 
 
-def payload_kernel(dest_ref, src_ref, hub_ref, tiles_ref, blocks_ref, out_ref, counts_ref):
+def payload_kernel(dest_ref, src_ref, hub_ref, tiles_ref, blocks_ref, out_ref, hub_out_ref, counts_ref):
     node_count, rows_per_node, col_count = out_ref.shape
     tile_count, tile_side, _ = tiles_ref.shape
-    tail = rows_per_node - HUB_PAD
-    capacity = tail // tile_side
+    capacity = rows_per_node // tile_side
     out_ref[...] = jnp.zeros(out_ref.shape, out_ref.dtype)
 
     def clear(node, carry):
@@ -43,7 +42,7 @@
     hub = hub.astype(out_ref.dtype)
 
     def put_hub(node, carry):
-        out_ref[node, pl.ds(tail, HUB_PAD), :] = hub
+        hub_out_ref[node] = hub
         return carry
 
     lax.fori_loop(0, node_count, put_hub, 0, unroll=8)
@@ -65,10 +64,13 @@
 def build_payload(destination, sources, hubs, tiles, blocks, node_count, capacity):
     tile_side = tiles.shape[1]
     col_count = blocks.shape[2]
-    rows_per_node = capacity * tile_side + HUB_PAD
+    rows_per_node = capacity * tile_side
     return pl.pallas_call(
         payload_kernel,
-        out_shape=jax.ShapeDtypeStruct((node_count, rows_per_node, col_count), blocks.dtype),
+        out_shape=(
+            jax.ShapeDtypeStruct((node_count, rows_per_node, col_count), blocks.dtype),
+            jax.ShapeDtypeStruct((node_count, HUB_PAD, col_count), blocks.dtype),
+        ),
         grid_spec=pltpu.PrefetchScalarGridSpec(
             num_scalar_prefetch=3,
             grid=(1,),
@@ -76,7 +78,10 @@
                 pl.BlockSpec(memory_space=pltpu.VMEM),
                 pl.BlockSpec(memory_space=pltpu.VMEM),
             ],
-            out_specs=pl.BlockSpec(memory_space=pltpu.VMEM),
+            out_specs=(
+                pl.BlockSpec(memory_space=pltpu.VMEM),
+                pl.BlockSpec(memory_space=pltpu.VMEM),
+            ),
             scratch_shapes=[pltpu.SMEM((node_count,), jnp.int32)],
         ),
     )(destination, sources, hubs, tiles, blocks)
@@ -111,11 +116,9 @@
     )
     if anchor is not None:
         payload, anchor = lax.optimization_barrier((payload, anchor))
-    arrived = lax.all_to_all(payload, "dom", split_axis=0, concat_axis=0, tiled=True)
-    tiles_in = arrived[:, : capacity * tile_side, :].reshape(slot_count, tile_side, col_count)
-    hub_rows = arrived[:, capacity * tile_side : capacity * tile_side + hub_count, :].reshape(
-        node_count * hub_count, col_count
-    )
+    tiles_in, hubs_in = lax.all_to_all(payload, "dom", split_axis=0, concat_axis=0, tiled=True)
+    tiles_in = tiles_in.reshape(slot_count, tile_side, col_count)
+    hub_rows = hubs_in[:, :hub_count, :].reshape(node_count * hub_count, col_count)
     from_peers = jnp.einsum(
         "bk,krd->brd", landing, tiles_in, preferred_element_type=jnp.float32
     )

time: 380 us -> 401 us (1.055)
  the two profiles are of different devices: /device:TPU:40 before, /device:TPU:112 now
where the time goes in v11:
time: 401 us; the launch traced here: 399 us
  waiting for transfers between devices  212 us (53%)
  blocking collectives  68.3 us (17%)
  starting transfers between devices  62.9 us (16%)
  matrix products  20.1 us (5%)
  local copies, waits for them, and re-layouts  19.1 us (5%)
  Pallas kernels  13.5 us (3%)
    all_to_all x2, waiting for transfers between devices, aggregate(): lax.all_to_all(payload, 'dom', split_axis=0, concat_axis=0, tiled=True)  160 us
    ppermute x7, waiting for transfers between devices, gather_weights(): pieces.append(lax.ppermute(stacked, 'feat', pairs))  46 us
    all_to_all x2, blocking collectives, aggregate(): lax.all_to_all(payload, 'dom', split_axis=0, concat_axis=0, tiled=True)  42.1 us
    ppermute x7, starting transfers between devices, gather_weights(): pieces.append(lax.ppermute(stacked, 'feat', pairs))  36.4 us
    all_to_all x2, starting transfers between devices, aggregate(): lax.all_to_all(payload, 'dom', split_axis=0, concat_axis=0, tiled=True)  18.7 us
    all_to_all x2, blocking collectives, rows_to_feat(): lax.all_to_all(pieces, 'feat', split_axis=0, concat_axis=0, tiled=True)  17.7 us
    pallas_call x2, Pallas kernels, build_payload(): pl.pallas_call(payload_kernel, out_shape=(jax.ShapeDtypeStruct((node_coun...  13.5 us
    unnamed x45, local copies, waits for them, and re-layouts  13.2 us
  transfers between devices with their start and end apart: 11, of which 8 were waited for; matrix products, arithmetic and copies ran while one was open for 5% of the time, Pallas kernels for 2%

profile of v11, /device:TPU:112, one launch (start us, length us, event | category | flops | bytes accessed | tf_op | source)
XLA Modules:
  0.0 399.4 jit_solution(17643642119338962615)
XLA Ops:
  0.0 4.4 %all-to-all-start = ((bf16[8,64,128]{2,1,0:T(8,128)(2,1)}), bf16[8,64,128]{2,1,0:T(8,128)(2,1)S(1)}, u32[]{:S(2)}, u32[]{:S(2)}) async-start(bf16[8,64,128]{2,1,0:T(8,128)(2,1)} %bitcast.130), calls=%async_computation | async-start | bytes 262144 | tf_op jit(solution)/shard_map/all_to_all | solution.py:139
  4.4 6.8 %shard_map.136 = (bf16[64,256,128]{2,1,0:T(8,128)(2,1)}, bf16[64,8,128]{2,1,0:T(8,128)(2,1)}) custom-call(s32[64]{0:T(128)} %bitcast.143, s32[64]{0:T(128)} %src_ref.3, s32[2]{0:T(128)} %hub_ref.3, bf16[64,128,128]{2,1,0:T(8,128)(2,1)} %tiles_ref.3, bf16[4,128,128]{2,1,0:T(8,128)(2,1)} %bitcast.131), custom_call_target="tpu_custom_call" | custom-call | tf_op jit(solution)/shard_map/pallas_call | solution.py:68
  11.2 0.7 copy_bitcast_fusion
  11.9 24.9 %all_to_all.45 = bf16[64,8,128]{2,1,0:T(8,128)(2,1)S(1)} all-to-all(bf16[64,8,128]{2,1,0:T(8,128)(2,1)} %get-tuple-element.29), channel_id=1, replica_groups=mesh['dom'=64,'feat'=8] {'dom'}, dimensions={0} | all-to-all | bytes 262144 | tf_op jit(solution)/shard_map/all_to_all | solution.py:119
  36.8 9.2 %all-to-all-start.1 = ((bf16[64,256,128]{2,1,0:T(8,128)(2,1)}), bf16[64,256,128]{2,1,0:T(8,128)(2,1)}, u32[]{:S(2)}, u32[]{:S(2)}) async-start(bf16[64,256,128]{2,1,0:T(8,128)(2,1)} %get-tuple-element.28), calls=%async_computation.1 | async-start | bytes 8388608 | tf_op jit(solution)/shard_map/all_to_all | solution.py:119
  46.1 1.4 fusion.25
  47.5 3.5 collective-permute-start.1
  51.0 4.0 collective-permute-start.2
  55.0 4.0 collective-permute-start.3
  59.0 3.4 collective-permute-start.4
  62.5 0.6 gather_fusion
  63.1 0.3 convolution_bitcast_fusion.1
  63.4 0.2 copy.41
  63.7 0.8 copy.38
  64.4 0.1 eq.17
  64.6 0.7 convert_element_type.43
  65.3 1.0 fusion.38
  66.3 5.5 %collective-permute-done = bf16[2,2056,128]{2,1,0:T(8,128)(2,1)} collective-permute-done((bf16[2,2056,128]{2,1,0:T(8,128)(2,1)S(1)}, bf16[2,2056,128]{2,1,0:T(8,128)(2,1)}, u32[]{:S(2)}, u32[]{:S(2)}) %collective-permute-start) | collective-permute-done | bytes 1052704 | tf_op jit(solution)/shard_map/ppermute | solution.py:169
  71.8 3.5 collective-permute-start.5
  75.4 2.4 constant_dynamic-update-slice_fusion.6
  77.7 18.0 %collective-permute-start.6 = (bf16[2,2056,128]{2,1,0:T(8,128)(2,1)S(1)}, bf16[2,2056,128]{2,1,0:T(8,128)(2,1)S(1)}, u32[]{:S(2)}, u32[]{:S(2)}) collective-permute-start(bf16[2,2056,128]{2,1,0:T(8,128)(2,1)S(1)} %get-tuple-element.34), channel_id=1, source_target_pairs={{0,7},{1,0},{2,1},{3,2},{4,3},{5,4},{6,5},{7,6},{8,15},{9,8},{10,9... | collective-permute-start | bytes 3158024 | tf_op jit(solution)/shard_map/ppermute | solution.py:169
  95.7 2.4 constant_dynamic-update-slice_fusion.5
  98.1 19.9 %collective-permute-done.2 = bf16[2,2056,128]{2,1,0:T(8,128)(2,1)} collective-permute-done((bf16[2,2056,128]{2,1,0:T(8,128)(2,1)S(1)}, bf16[2,2056,128]{2,1,0:T(8,128)(2,1)}, u32[]{:S(2)}, u32[]{:S(2)}) %collective-permute-start.2) | collective-permute-done | bytes 1052704 | tf_op jit(solution)/shard_map/ppermute | solution.py:169
  118.0 2.3 constant_dynamic-update-slice_fusion.4
  120.3 2.7 collective-permute-done.3
  123.1 2.3 constant_dynamic-update-slice_fusion.3
  125.4 14.5 %collective-permute-done.4 = bf16[2,2056,128]{2,1,0:T(8,128)(2,1)S(1)} collective-permute-done((bf16[2,2056,128]{2,1,0:T(8,128)(2,1)S(1)}, bf16[2,2056,128]{2,1,0:T(8,128)(2,1)S(1)}, u32[]{:S(2)}, u32[]{:S(2)}) %collective-permute-start.4) | collective-permute-done | bytes 1052704 | tf_op jit(solution)/shard_map/ppermute | solution.py:169
  139.9 1.2 constant_dynamic-update-slice_fusion.2
  141.0 1.1 constant_dynamic-update-slice_fusion.1
  142.1 3.4 collective-permute-done.6
  145.6 1.1 constant_dynamic-update-slice_fusion
  146.7 32.8 %all-to-all-done.1 = bf16[64,256,128]{2,1,0:T(8,128)(2,1)} async-done(((bf16[64,256,128]{2,1,0:T(8,128)(2,1)}), bf16[64,256,128]{2,1,0:T(8,128)(2,1)}, u32[]{:S(2)}, u32[]{:S(2)}) %all-to-all-start.1) | async-done | bytes 4194336 | tf_op jit(solution)/shard_map/all_to_all | solution.py:119
  179.5 4.6 %fusion.13 = f32[4,128,128]{2,0,1:T(4,128)S(1)} fusion(f32[4,128,128]{2,0,1:T(4,128)S(1)} %fusion.38, bf16[128,128,128]{2,1,0:T(8,128)(2,1)} %bitcast.9, s32[128]{0:T(128)S(1)} %eq.17), kind=kOutput, calls=%fused_computation.24 | convolution fusion | flops 16843264 | bytes 4719104 | tf_op jit(solution)/shard_map/bk,krd->brd/dot_general | solution.py:122
  184.1 0.1 copy.43
  184.3 0.2 fusion.23
  184.5 0.8 copy.44
  185.2 3.4 all-to-all-start.3
  188.6 0.7 slice_convert_fusion.1
  189.4 5.3 %all-to-all-done.3 = bf16[8,64,128]{2,1,0:T(8,128)(2,1)S(1)} async-done(((bf16[8,64,128]{2,1,0:T(8,128)(2,1)}), bf16[8,64,128]{2,1,0:T(8,128)(2,1)S(1)}, u32[]{:S(2)}, u32[]{:S(2)}) %all-to-all-start.3) | async-done | bytes 131104 | tf_op jit(solution)/shard_map/all_to_all | solution.py:139
  194.7 2.1 fusion.7
  196.8 2.2 multiply_reduce_fusion.1
  199.0 0.1 copy_bitcast_fusion.2
  199.1 0.6 gather_fusion.2
  199.7 0.1 broadcast_select_fusion
  199.8 9.2 %all_to_all.46 = bf16[8,64,128]{2,1,0:T(8,128)(2,1)} all-to-all(bf16[8,64,128]{2,1,0:T(8,128)(2,1)S(1)} %broadcast_select_fusion), channel_id=1, replica_groups=mesh['dom'=64,'feat'=8] {'feat'}, dimensions={0} | all-to-all | bytes 262144 | tf_op jit(solution)/shard_map/all_to_all | solution.py:147
  208.9 6.7 %shard_map.137 = (bf16[64,256,128]{2,1,0:T(8,128)(2,1)}, bf16[64,8,128]{2,1,0:T(8,128)(2,1)}) custom-call(s32[64]{0:T(128)} %bitcast.144, s32[64]{0:T(128)} %src_ref.3, s32[2]{0:T(128)} %hub_ref.3, bf16[64,128,128]{2,1,0:T(8,128)(2,1)} %tiles_ref.3, bf16[4,128,128]{2,1,0:T(8,128)(2,1)} %bitcast.133), custom_call_target="tpu_custom_call" | custom-call | tf_op jit(solution)/shard_map/pallas_call | solution.py:68
  215.7 17.2 %all_to_all.47 = bf16[64,8,128]{2,1,0:T(8,128)(2,1)S(1)} all-to-all(bf16[64,8,128]{2,1,0:T(8,128)(2,1)} %get-tuple-element.31), channel_id=1, replica_groups=mesh['dom'=64,'feat'=8] {'dom'}, dimensions={0} | all-to-all | bytes 262144 | tf_op jit(solution)/shard_map/all_to_all | solution.py:119
  232.9 9.5 %all-to-all-start.5 = ((bf16[64,256,128]{2,1,0:T(8,128)(2,1)}), bf16[64,256,128]{2,1,0:T(8,128)(2,1)}, u32[]{:S(2)}, u32[]{:S(2)}) async-start(bf16[64,256,128]{2,1,0:T(8,128)(2,1)} %get-tuple-element.30), calls=%async_computation.5 | async-start | bytes 8388608 | tf_op jit(solution)/shard_map/all_to_all | solution.py:119
  242.4 0.6 gather_fusion.1
  243.0 0.3 convolution_bitcast_fusion
  243.4 0.2 copy.50
  243.6 0.4 fusion.36
  244.0 127.6 %all-to-all-done.5 = bf16[64,256,128]{2,1,0:T(8,128)(2,1)} async-done(((bf16[64,256,128]{2,1,0:T(8,128)(2,1)}), bf16[64,256,128]{2,1,0:T(8,128)(2,1)}, u32[]{:S(2)}, u32[]{:S(2)}) %all-to-all-start.5) | async-done | bytes 4194336 | tf_op jit(solution)/shard_map/all_to_all | solution.py:119
  371.6 4.5 %fusion.16 = f32[4,128,128]{2,0,1:T(4,128)S(1)} fusion(f32[4,128,128]{2,0,1:T(4,128)S(1)} %fusion.36, bf16[128,128,128]{2,1,0:T(8,128)(2,1)} %bitcast.22, s32[128]{0:T(128)S(1)} %copy-done.9), kind=kOutput, calls=%fused_computation.25 | convolution fusion | flops 16843264 | bytes 4719104 | tf_op jit(solution)/shard_map/bk,krd->brd/dot_general | solution.py:122
  376.1 0.2 copy.51
  376.3 0.2 fusion.24
  376.5 0.1 copy.52
  376.6 8.5 %all_to_all.48 = bf16[8,64,128]{2,1,0:T(8,128)(2,1)S(1)} all-to-all(bf16[8,64,128]{2,1,0:T(8,128)(2,1)S(1)} %bitcast.136), channel_id=1, replica_groups=mesh['dom'=64,'feat'=8] {'feat'}, dimensions={0} | all-to-all | bytes 262144 | tf_op jit(solution)/shard_map/all_to_all | solution.py:139
  385.2 2.1 fusion.5
  387.2 2.2 multiply_reduce_fusion
  389.5 0.1 copy_bitcast_fusion.1
  389.6 0.6 gather_fusion.3
  390.3 8.5 %all_to_all.49 = bf16[8,64,128]{2,1,0:T(8,128)(2,1)S(1)} all-to-all(bf16[8,64,128]{2,1,0:T(8,128)(2,1)S(1)} %broadcast_select_fusion.1), channel_id=1, replica_groups=mesh['dom'=64,'feat'=8] {'feat'}, dimensions={0} | all-to-all | bytes 262144 | tf_op jit(solution)/shard_map/all_to_all | solution.py:147
  398.8 0.7 copy.99
  (53 shorter events, 0.2 us)
Async XLA Ops:
  0.0 63.1 %copy-start = (bf16[8,128,128]{2,1,0:T(8,128)(2,1)S(1)}, bf16[8,128,128]{2,1,0:T(8,128)(2,1)}, u32[]{:S(2)}) copy-start(bf16[8,128,128]{2,1,0:T(8,128)(2,1)} %param.24) | copy-start | bytes 786436
  0.0 11.2 %all-to-all-start = ((bf16[8,64,128]{2,1,0:T(8,128)(2,1)}), bf16[8,64,128]{2,1,0:T(8,128)(2,1)S(1)}, u32[]{:S(2)}, u32[]{:S(2)}) async-start(bf16[8,64,128]{2,1,0:T(8,128)(2,1)} %bitcast.130), calls=%async_computation | async-start | bytes 262144 | tf_op jit(solution)/shard_map/all_to_all | solution.py:139
  36.8 29.5 %copy-start.5 = (bf16[64,8,128]{2,1,0:T(8,128)(2,1)}, bf16[64,8,128]{2,1,0:T(8,128)(2,1)S(1)}, u32[]{:S(2)}) copy-start(bf16[64,8,128]{2,1,0:T(8,128)(2,1)S(1)} %all_to_all.45) | copy-start | bytes 393220
  36.8 9.3 %copy-start.16 = (bf16[2,128]{1,0:T(2,128)(2,1)S(1)}, bf16[2,128]{1,0:T(2,128)(2,1)}, u32[]{:S(2)}) copy-start(bf16[2,128]{1,0:T(2,128)(2,1)} %param.31) | copy-start | bytes 1540
  36.8 9.3 %copy-start.3 = (bf16[2,1024,128]{2,1,0:T(8,128)(2,1)S(1)}, bf16[2,1024,128]{2,1,0:T(8,128)(2,1)}, u32[]{:S(2)}) copy-start(bf16[2,1024,128]{2,1,0:T(8,128)(2,1)} %param.30) | copy-start | bytes 1572868
  36.8 9.3 %copy-start.4 = (bf16[2,1024,128]{2,1,0:T(8,128)(2,1)S(1)}, bf16[2,1024,128]{2,1,0:T(8,128)(2,1)}, u32[]{:S(2)}) copy-start(bf16[2,1024,128]{2,1,0:T(8,128)(2,1)} %param.29) | copy-start | bytes 1572868
  36.8 25.6 %copy-start.17 = (s32[8]{0:T(128)S(1)}, s32[8]{0:T(128)}, u32[]{:S(2)}) copy-start(s32[8]{0:T(128)} %param.23) | copy-start | bytes 100
  36.8 25.6 %copy-start.1 = (bf16[512,128]{1,0:T(8,128)(2,1)S(1)}, bf16[512,128]{1,0:T(8,128)(2,1)}, u32[]{:S(2)}) copy-start(bf16[512,128]{1,0:T(8,128)(2,1)} %param.18) | copy-start | bytes 393220
  36.8 142.7 %all-to-all-start.1 = ((bf16[64,256,128]{2,1,0:T(8,128)(2,1)}), bf16[64,256,128]{2,1,0:T(8,128)(2,1)}, u32[]{:S(2)}, u32[]{:S(2)}) async-start(bf16[64,256,128]{2,1,0:T(8,128)(2,1)} %get-tuple-element.28), calls=%async_computation.1 | async-start | bytes 8388608 | tf_op jit(solution)/shard_map/all_to_all | solution.py:119
  47.5 24.3 %collective-permute-start = (bf16[2,2056,128]{2,1,0:T(8,128)(2,1)S(1)}, bf16[2,2056,128]{2,1,0:T(8,128)(2,1)}, u32[]{:S(2)}, u32[]{:S(2)}) collective-permute-start(bf16[2,2056,128]{2,1,0:T(8,128)(2,1)S(1)} %get-tuple-element.34), channel_id=1, source_target_pairs={{0,1},{1,2},{2,3},{3,4},{4,5},{5,6},{6,7},{7,0},{8,9},{9,10},{10,1... | collective-permute-start | bytes 3158024 | tf_op jit(solution)/shard_map/ppermute | solution.py:169
  47.5 30.2 %collective-permute-start.1 = (bf16[2,2056,128]{2,1,0:T(8,128)(2,1)S(1)}, bf16[2,2056,128]{2,1,0:T(8,128)(2,1)}, u32[]{:S(2)}, u32[]{:S(2)}) collective-permute-start(bf16[2,2056,128]{2,1,0:T(8,128)(2,1)S(1)} %get-tuple-element.34), channel_id=1, source_target_pairs={{0,2},{1,3},{2,4},{3,5},{4,6},{5,7},{6,0},{7,1},{8,10},{9,11},{10,... | collective-permute-start | bytes 3158024 | tf_op jit(solution)/shard_map/ppermute | solution.py:169
  51.0 67.0 %collective-permute-start.2 = (bf16[2,2056,128]{2,1,0:T(8,128)(2,1)S(1)}, bf16[2,2056,128]{2,1,0:T(8,128)(2,1)}, u32[]{:S(2)}, u32[]{:S(2)}) collective-permute-start(bf16[2,2056,128]{2,1,0:T(8,128)(2,1)S(1)} %get-tuple-element.34), channel_id=1, source_target_pairs={{0,3},{1,4},{2,5},{3,6},{4,7},{5,0},{6,1},{7,2},{8,11},{9,12},{10,... | collective-permute-start | bytes 3158024 | tf_op jit(solution)/shard_map/ppermute | solution.py:169
  55.0 68.0 %collective-permute-start.3 = (bf16[2,2056,128]{2,1,0:T(8,128)(2,1)S(1)}, bf16[2,2056,128]{2,1,0:T(8,128)(2,1)}, u32[]{:S(2)}, u32[]{:S(2)}) collective-permute-start(bf16[2,2056,128]{2,1,0:T(8,128)(2,1)S(1)} %get-tuple-element.34), channel_id=1, source_target_pairs={{0,4},{1,5},{2,6},{3,7},{4,0},{5,1},{6,2},{7,3},{8,12},{9,13},{10,... | collective-permute-start | bytes 3158024 | tf_op jit(solution)/shard_map/ppermute | solution.py:169
  59.0 80.9 %collective-permute-start.4 = (bf16[2,2056,128]{2,1,0:T(8,128)(2,1)S(1)}, bf16[2,2056,128]{2,1,0:T(8,128)(2,1)S(1)}, u32[]{:S(2)}, u32[]{:S(2)}) collective-permute-start(bf16[2,2056,128]{2,1,0:T(8,128)(2,1)S(1)} %get-tuple-element.34), channel_id=1, source_target_pairs={{0,5},{1,6},{2,7},{3,0},{4,1},{5,2},{6,3},{7,4},{8,13},{9,14},{10,... | collective-permute-start | bytes 3158024 | tf_op jit(solution)/shard_map/ppermute | solution.py:169
  64.6 114.9 %copy-start.8 = (s32[128]{0:T(128)}, s32[128]{0:T(128)S(1)}, u32[]{:S(2)}) copy-start(s32[128]{0:T(128)S(1)} %eq.17) | copy-start | bytes 1540
  65.3 119.0 %copy-start.12 = (f32[512]{0:T(512)}, f32[512]{0:T(512)S(1)}, u32[]{:S(2)}) copy-start(f32[512]{0:T(512)S(1)} %convert_element_type.43) | copy-start | bytes 6148
  65.3 134.4 %copy-start.10 = (pred[8]{0:T(512)(128)(4,1)}, pred[8]{0:T(512)(128)(4,1)S(1)}, u32[]{:S(2)}) copy-start(pred[8]{0:T(512)(128)(4,1)S(1)} %compare_and_fusion) | copy-start | bytes 28
  71.8 69.2 %collective-permute-start.5 = (bf16[2,2056,128]{2,1,0:T(8,128)(2,1)S(1)}, bf16[2,2056,128]{2,1,0:T(8,128)(2,1)S(1)}, u32[]{:S(2)}, u32[]{:S(2)}) collective-permute-start(bf16[2,2056,128]{2,1,0:T(8,128)(2,1)S(1)} %get-tuple-element.34), channel_id=1, source_target_pairs={{0,6},{1,7},{2,0},{3,1},{4,2},{5,3},{6,4},{7,5},{8,14},{9,15},{10,... | collective-permute-start | bytes 3158024 | tf_op jit(solution)/shard_map/ppermute | solution.py:169
  77.7 67.9 %collective-permute-start.6 = (bf16[2,2056,128]{2,1,0:T(8,128)(2,1)S(1)}, bf16[2,2056,128]{2,1,0:T(8,128)(2,1)S(1)}, u32[]{:S(2)}, u32[]{:S(2)}) collective-permute-start(bf16[2,2056,128]{2,1,0:T(8,128)(2,1)S(1)} %get-tuple-element.34), channel_id=1, source_target_pairs={{0,7},{1,0},{2,1},{3,2},{4,3},{5,4},{6,5},{7,6},{8,15},{9,8},{10,9... | collective-permute-start | bytes 3158024 | tf_op jit(solution)/shard_map/ppermute | solution.py:169
  142.1 42.1 %slice-start = ((bf16[64,8,128]{2,1,0:T(8,128)(2,1)}), bf16[64,2,128]{2,1,0:T(2,128)(2,1)S(1)}, s32[]{:S(2)}) async-start(bf16[64,8,128]{2,1,0:T(8,128)(2,1)} %copy-done.5), calls=%async_computation.9 | async-start | bytes 65536 | tf_op jit(solution)/shard_map/slice | solution.py:121
  142.1 42.1 %copy-start.15 = (bf16[512,128]{1,0:T(8,128)(2,1)S(1)}, bf16[512,128]{1,0:T(8,128)(2,1)}, u32[]{:S(2)}) copy-start(bf16[512,128]{1,0:T(8,128)(2,1)} %param.21) | copy-start | bytes 393220
  179.5 17.2 %copy-start.7 = (bf16[64,1024]{1,0:T(8,128)(2,1)S(1)}, bf16[64,1024]{1,0:T(8,128)(2,1)}, u32[]{:S(2)}) copy-start(bf16[64,1024]{1,0:T(8,128)(2,1)} %copy_bitcast_fusion) | copy-start | bytes 393220
  185.2 9.4 %all-to-all-start.3 = ((bf16[8,64,128]{2,1,0:T(8,128)(2,1)}), bf16[8,64,128]{2,1,0:T(8,128)(2,1)S(1)}, u32[]{:S(2)}, u32[]{:S(2)}) async-start(bf16[8,64,128]{2,1,0:T(8,128)(2,1)} %bitcast.15), calls=%async_computation.3 | async-start | bytes 262144 | tf_op jit(solution)/shard_map/all_to_all | solution.py:139
  232.9 11.1 %copy-start.6 = (bf16[64,8,128]{2,1,0:T(8,128)(2,1)}, bf16[64,8,128]{2,1,0:T(8,128)(2,1)S(1)}, u32[]{:S(2)}) copy-start(bf16[64,8,128]{2,1,0:T(8,128)(2,1)S(1)} %all_to_all.47) | copy-start | bytes 393220
  232.9 9.5 %copy-start.2 = (bf16[8,64,128]{2,1,0:T(8,128)(2,1)S(1)}, bf16[8,64,128]{2,1,0:T(8,128)(2,1)}, u32[]{:S(2)}) copy-start(bf16[8,64,128]{2,1,0:T(8,128)(2,1)} %all_to_all.46) | copy-start | bytes 393220
  232.9 10.7 %copy-start.14 = (s32[8]{0:T(128)S(1)}, s32[8]{0:T(128)}, u32[]{:S(2)}) copy-start(s32[8]{0:T(128)} %param.22) | copy-start | bytes 100
  232.9 138.7 %copy-start.9 = (s32[128]{0:T(128)S(1)}, s32[128]{0:T(128)}, u32[]{:S(2)}) copy-start(s32[128]{0:T(128)} %copy-done.8) | copy-start | bytes 1540
  232.9 138.7 %all-to-all-start.5 = ((bf16[64,256,128]{2,1,0:T(8,128)(2,1)}), bf16[64,256,128]{2,1,0:T(8,128)(2,1)}, u32[]{:S(2)}, u32[]{:S(2)}) async-start(bf16[64,256,128]{2,1,0:T(8,128)(2,1)} %get-tuple-element.30), calls=%async_computation.5 | async-start | bytes 8388608 | tf_op jit(solution)/shard_map/all_to_all | solution.py:119
  243.0 133.2 %copy-start.13 = (f32[512]{0:T(512)S(1)}, f32[512]{0:T(512)}, u32[]{:S(2)}) copy-start(f32[512]{0:T(512)} %copy-done.12) | copy-start | bytes 6148
  244.0 132.3 %slice-start.1 = ((bf16[64,8,128]{2,1,0:T(8,128)(2,1)}), bf16[64,2,128]{2,1,0:T(2,128)(2,1)S(1)}, s32[]{:S(2)}) async-start(bf16[64,8,128]{2,1,0:T(8,128)(2,1)} %copy-done.6), calls=%async_computation.10 | async-start | bytes 65536 | tf_op jit(solution)/shard_map/slice | solution.py:121
  371.6 15.6 %copy-start.11 = (pred[8]{0:T(512)(128)(4,1)S(1)}, pred[8]{0:T(512)(128)(4,1)}, u32[]{:S(2)}) copy-start(pred[8]{0:T(512)(128)(4,1)} %copy-done.10) | copy-start | bytes 28

commit v12 on v9

--- a/solution.py
+++ b/solution.py
@@ -22,7 +22,6 @@
     tile_count, tile_side, _ = tiles_ref.shape
     tail = rows_per_node - HUB_PAD
     capacity = tail // tile_side
-    out_ref[...] = jnp.zeros(out_ref.shape, out_ref.dtype)
 
     def clear(node, carry):
         counts_ref[node] = 0
@@ -60,6 +59,17 @@
         return carry
 
     lax.fori_loop(0, tile_count, put_tile, 0, unroll=8)
+    empty = jnp.zeros((tile_side, col_count), out_ref.dtype)
+
+    def clear_unused(node, carry):
+        filled = counts_ref[node]
+        for slot in range(capacity):
+            @pl.when(filled <= slot)
+            def _():
+                out_ref[node, pl.ds(slot * tile_side, tile_side), :] = empty
+        return carry
+
+    lax.fori_loop(0, node_count, clear_unused, 0, unroll=8)
 
 
 def build_payload(destination, sources, hubs, tiles, blocks, node_count, capacity):

time: 380 us -> 381 us (level)
  no operation moved by 1% of the time
where the time goes in v12:
time: 381 us; the launch traced here: 380 us
  waiting for transfers between devices  217 us (57%)
  starting transfers between devices  76.7 us (20%)
  blocking collectives  27.6 us (7%)
  local copies, waits for them, and re-layouts  25.2 us (7%)
  matrix products  15.7 us (4%)
  Pallas kernels  14.3 us (4%)
    all_to_all x2, waiting for transfers between devices, aggregate(): lax.all_to_all(payload, 'dom', split_axis=0, concat_axis=0, tiled=True)  166 us
    ppermute x7, waiting for transfers between devices, gather_weights(): pieces.append(lax.ppermute(stacked, 'feat', pairs))  45.5 us
    ppermute x7, starting transfers between devices, gather_weights(): pieces.append(lax.ppermute(stacked, 'feat', pairs))  37.2 us
    all_to_all x2, starting transfers between devices, aggregate(): lax.all_to_all(payload, 'dom', split_axis=0, concat_axis=0, tiled=True)  24 us
    all_to_all x2, blocking collectives, rows_to_feat(): lax.all_to_all(pieces, 'feat', split_axis=0, concat_axis=0, tiled=True)  17.7 us
    all_to_all x2, starting transfers between devices, feat_to_rows(): lax.all_to_all(pieces, 'feat', split_axis=0, concat_axis=0, tiled=True)  15.5 us
    pallas_call x2, Pallas kernels, build_payload(): pl.pallas_call(payload_kernel, out_shape=jax.ShapeDtypeStruct((node_count...  14.3 us
    unnamed x39, local copies, waits for them, and re-layouts  13.2 us
  transfers between devices with their start and end apart: 11, of which 8 were waited for; matrix products, arithmetic and copies ran while one was open for 5% of the time, Pallas kernels for 2%

profile of v12, /device:TPU:40, one launch (start us, length us, event | category | flops | bytes accessed | tf_op | source)
XLA Modules:
  0.0 380.0 jit_solution(2301098126735943472)
XLA Ops:
  0.0 4.4 %all-to-all-start = ((bf16[8,64,128]{2,1,0:T(8,128)(2,1)}), bf16[8,64,128]{2,1,0:T(8,128)(2,1)S(1)}, u32[]{:S(2)}, u32[]{:S(2)}) async-start(bf16[8,64,128]{2,1,0:T(8,128)(2,1)} %bitcast.132), calls=%async_computation | async-start | bytes 262144 | tf_op jit(solution)/shard_map/all_to_all | solution.py:146
  4.4 7.2 %shard_map.136 = bf16[64,264,128]{2,1,0:T(8,128)(2,1)} custom-call(s32[64]{0:T(128)} %bitcast.145, s32[64]{0:T(128)} %src_ref.3, s32[2]{0:T(128)} %hub_ref.3, bf16[64,128,128]{2,1,0:T(8,128)(2,1)} %tiles_ref.3, bf16[4,128,128]{2,1,0:T(8,128)(2,1)} %bitcast.133), custom_call_target="tpu_custom_call" | custom-call | tf_op jit(solution)/shard_map/pallas_call | solution.py:79
  11.7 16.4 %all-to-all-start.1 = ((bf16[64,264,128]{2,1,0:T(8,128)(2,1)}), bf16[64,264,128]{2,1,0:T(8,128)(2,1)}, u32[]{:S(2)}, u32[]{:S(2)}) async-start(bf16[64,264,128]{2,1,0:T(8,128)(2,1)} %shard_map.136), calls=%async_computation.1 | async-start | bytes 8650752 | tf_op jit(solution)/shard_map/all_to_all | solution.py:124
  28.2 1.4 fusion.25
  29.6 3.9 %collective-permute-start.1 = (bf16[2,2056,128]{2,1,0:T(8,128)(2,1)S(1)}, bf16[2,2056,128]{2,1,0:T(8,128)(2,1)}, u32[]{:S(2)}, u32[]{:S(2)}) collective-permute-start(bf16[2,2056,128]{2,1,0:T(8,128)(2,1)S(1)} %get-tuple-element.24), channel_id=1, source_target_pairs={{0,2},{1,3},{2,4},{3,5},{4,6},{5,7},{6,0},{7,1},{8,10},{9,11},{10,... | collective-permute-start | bytes 3158024 | tf_op jit(solution)/shard_map/ppermute | solution.py:176
  33.5 4.0 %collective-permute-start.2 = (bf16[2,2056,128]{2,1,0:T(8,128)(2,1)S(1)}, bf16[2,2056,128]{2,1,0:T(8,128)(2,1)}, u32[]{:S(2)}, u32[]{:S(2)}) collective-permute-start(bf16[2,2056,128]{2,1,0:T(8,128)(2,1)S(1)} %get-tuple-element.24), channel_id=1, source_target_pairs={{0,3},{1,4},{2,5},{3,6},{4,7},{5,0},{6,1},{7,2},{8,11},{9,12},{10,... | collective-permute-start | bytes 3158024 | tf_op jit(solution)/shard_map/ppermute | solution.py:176
  37.5 4.0 %collective-permute-start.3 = (bf16[2,2056,128]{2,1,0:T(8,128)(2,1)S(1)}, bf16[2,2056,128]{2,1,0:T(8,128)(2,1)}, u32[]{:S(2)}, u32[]{:S(2)}) collective-permute-start(bf16[2,2056,128]{2,1,0:T(8,128)(2,1)S(1)} %get-tuple-element.24), channel_id=1, source_target_pairs={{0,4},{1,5},{2,6},{3,7},{4,0},{5,1},{6,2},{7,3},{8,12},{9,13},{10,... | collective-permute-start | bytes 3158024 | tf_op jit(solution)/shard_map/ppermute | solution.py:176
  41.4 3.4 collective-permute-start.4
  44.9 0.6 gather_fusion
  45.6 0.3 convolution_bitcast_fusion.1
  45.9 0.2 copy.41
  46.1 0.8 copy.38
  46.9 0.1 eq.17
  47.0 0.7 convert_element_type.43
  47.8 1.0 fusion.38
  48.8 5.1 %collective-permute-done = bf16[2,2056,128]{2,1,0:T(8,128)(2,1)} collective-permute-done((bf16[2,2056,128]{2,1,0:T(8,128)(2,1)S(1)}, bf16[2,2056,128]{2,1,0:T(8,128)(2,1)}, u32[]{:S(2)}, u32[]{:S(2)}) %collective-permute-start) | collective-permute-done | bytes 1052704 | tf_op jit(solution)/shard_map/ppermute | solution.py:176
  53.9 3.9 %collective-permute-start.5 = (bf16[2,2056,128]{2,1,0:T(8,128)(2,1)S(1)}, bf16[2,2056,128]{2,1,0:T(8,128)(2,1)S(1)}, u32[]{:S(2)}, u32[]{:S(2)}) collective-permute-start(bf16[2,2056,128]{2,1,0:T(8,128)(2,1)S(1)} %get-tuple-element.24), channel_id=1, source_target_pairs={{0,6},{1,7},{2,0},{3,1},{4,2},{5,3},{6,4},{7,5},{8,14},{9,15},{10,... | collective-permute-start | bytes 3158024 | tf_op jit(solution)/shard_map/ppermute | solution.py:176
  57.8 2.4 constant_dynamic-update-slice_fusion.6
  60.2 18.0 %collective-permute-start.6 = (bf16[2,2056,128]{2,1,0:T(8,128)(2,1)S(1)}, bf16[2,2056,128]{2,1,0:T(8,128)(2,1)S(1)}, u32[]{:S(2)}, u32[]{:S(2)}) collective-permute-start(bf16[2,2056,128]{2,1,0:T(8,128)(2,1)S(1)} %get-tuple-element.24), channel_id=1, source_target_pairs={{0,7},{1,0},{2,1},{3,2},{4,3},{5,4},{6,5},{7,6},{8,15},{9,8},{10,9... | collective-permute-start | bytes 3158024 | tf_op jit(solution)/shard_map/ppermute | solution.py:176
  78.2 2.4 constant_dynamic-update-slice_fusion.5
  80.6 19.9 %collective-permute-done.2 = bf16[2,2056,128]{2,1,0:T(8,128)(2,1)} collective-permute-done((bf16[2,2056,128]{2,1,0:T(8,128)(2,1)S(1)}, bf16[2,2056,128]{2,1,0:T(8,128)(2,1)}, u32[]{:S(2)}, u32[]{:S(2)}) %collective-permute-start.2) | collective-permute-done | bytes 1052704 | tf_op jit(solution)/shard_map/ppermute | solution.py:176
  100.5 2.3 constant_dynamic-update-slice_fusion.4
  102.8 2.7 collective-permute-done.3
  105.5 2.3 constant_dynamic-update-slice_fusion.3
  107.8 14.5 %collective-permute-done.4 = bf16[2,2056,128]{2,1,0:T(8,128)(2,1)S(1)} collective-permute-done((bf16[2,2056,128]{2,1,0:T(8,128)(2,1)S(1)}, bf16[2,2056,128]{2,1,0:T(8,128)(2,1)S(1)}, u32[]{:S(2)}, u32[]{:S(2)}) %collective-permute-start.4) | collective-permute-done | bytes 1052704 | tf_op jit(solution)/shard_map/ppermute | solution.py:176
  122.3 1.2 constant_dynamic-update-slice_fusion.2
  123.5 1.1 constant_dynamic-update-slice_fusion.1
  124.6 3.3 collective-permute-done.6
  127.9 1.1 constant_dynamic-update-slice_fusion
  129.0 36.5 %all-to-all-done.1 = bf16[64,264,128]{2,1,0:T(8,128)(2,1)} async-done(((bf16[64,264,128]{2,1,0:T(8,128)(2,1)}), bf16[64,264,128]{2,1,0:T(8,128)(2,1)}, u32[]{:S(2)}, u32[]{:S(2)}) %all-to-all-start.1) | async-done | bytes 4325408 | tf_op jit(solution)/shard_map/all_to_all | solution.py:124
  165.5 2.5 slice.81
  168.0 2.3 fusion.13
  170.3 0.1 copy.43
  170.5 0.9 slice.82
  171.4 0.2 fusion.23
  171.6 0.8 copy.44
  172.4 11.1 %all-to-all-start.2 = ((bf16[8,64,128]{2,1,0:T(8,128)(2,1)}), bf16[8,64,128]{2,1,0:T(8,128)(2,1)S(1)}, u32[]{:S(2)}, u32[]{:S(2)}) async-start(bf16[8,64,128]{2,1,0:T(8,128)(2,1)} %bitcast.15), calls=%async_computation.2 | async-start | bytes 262144 | tf_op jit(solution)/shard_map/all_to_all | solution.py:146
  183.5 0.7 slice_convert_fusion.1
  184.2 5.4 %all-to-all-done.2 = bf16[8,64,128]{2,1,0:T(8,128)(2,1)S(1)} async-done(((bf16[8,64,128]{2,1,0:T(8,128)(2,1)}), bf16[8,64,128]{2,1,0:T(8,128)(2,1)S(1)}, u32[]{:S(2)}, u32[]{:S(2)}) %all-to-all-start.2) | async-done | bytes 131104 | tf_op jit(solution)/shard_map/all_to_all | solution.py:146
  189.6 2.1 fusion.7
  191.7 2.2 multiply_reduce_fusion.1
  193.9 0.1 copy_bitcast_fusion.2
  194.0 0.6 gather_fusion.2
  194.7 9.2 %all_to_all.35 = bf16[8,64,128]{2,1,0:T(8,128)(2,1)} all-to-all(bf16[8,64,128]{2,1,0:T(8,128)(2,1)S(1)} %broadcast_select_fusion), channel_id=1, replica_groups=mesh['dom'=64,'feat'=8] {'feat'}, dimensions={0} | all-to-all | bytes 262144 | tf_op jit(solution)/shard_map/all_to_all | solution.py:154
  203.9 7.2 %shard_map.137 = bf16[64,264,128]{2,1,0:T(8,128)(2,1)} custom-call(s32[64]{0:T(128)} %bitcast.146, s32[64]{0:T(128)} %src_ref.3, s32[2]{0:T(128)} %hub_ref.3, bf16[64,128,128]{2,1,0:T(8,128)(2,1)} %tiles_ref.3, bf16[4,128,128]{2,1,0:T(8,128)(2,1)} %bitcast.135), custom_call_target="tpu_custom_call" | custom-call | tf_op jit(solution)/shard_map/pallas_call | solution.py:79
  211.1 7.5 %all-to-all-start.4 = ((bf16[64,264,128]{2,1,0:T(8,128)(2,1)}), bf16[64,264,128]{2,1,0:T(8,128)(2,1)}, u32[]{:S(2)}, u32[]{:S(2)}) async-start(bf16[64,264,128]{2,1,0:T(8,128)(2,1)} %shard_map.137), calls=%async_computation.4 | async-start | bytes 8650752 | tf_op jit(solution)/shard_map/all_to_all | solution.py:124
  218.6 0.6 gather_fusion.1
  219.2 0.3 convolution_bitcast_fusion
  219.5 0.2 copy.50
  219.8 0.4 fusion.36
  220.1 129.4 %all-to-all-done.4 = bf16[64,264,128]{2,1,0:T(8,128)(2,1)} async-done(((bf16[64,264,128]{2,1,0:T(8,128)(2,1)}), bf16[64,264,128]{2,1,0:T(8,128)(2,1)}, u32[]{:S(2)}, u32[]{:S(2)}) %all-to-all-start.4) | async-done | bytes 4325408 | tf_op jit(solution)/shard_map/all_to_all | solution.py:124
  349.6 2.5 slice.85
  352.1 2.3 fusion.16
  354.4 0.2 copy.51
  354.6 0.9 slice.86
  355.5 0.2 fusion.24
  355.7 0.1 copy.52
  355.9 9.9 %all_to_all.36 = bf16[8,64,128]{2,1,0:T(8,128)(2,1)S(1)} all-to-all(bf16[8,64,128]{2,1,0:T(8,128)(2,1)S(1)} %bitcast.138), channel_id=1, replica_groups=mesh['dom'=64,'feat'=8] {'feat'}, dimensions={0} | all-to-all | bytes 262144 | tf_op jit(solution)/shard_map/all_to_all | solution.py:146
  365.7 2.1 fusion.5
  367.8 2.2 multiply_reduce_fusion
  370.0 0.1 copy_bitcast_fusion.1
  370.1 0.6 gather_fusion.3
  370.8 8.5 %all_to_all.37 = bf16[8,64,128]{2,1,0:T(8,128)(2,1)S(1)} all-to-all(bf16[8,64,128]{2,1,0:T(8,128)(2,1)S(1)} %broadcast_select_fusion.1), channel_id=1, replica_groups=mesh['dom'=64,'feat'=8] {'feat'}, dimensions={0} | all-to-all | bytes 262144 | tf_op jit(solution)/shard_map/all_to_all | solution.py:154
  379.3 0.7 copy.99
  (45 shorter events, 0.3 us)
Async XLA Ops:
  0.0 45.5 %copy-start = (bf16[8,128,128]{2,1,0:T(8,128)(2,1)S(1)}, bf16[8,128,128]{2,1,0:T(8,128)(2,1)}, u32[]{:S(2)}) copy-start(bf16[8,128,128]{2,1,0:T(8,128)(2,1)} %param.24) | copy-start | bytes 786436
  0.0 11.6 %all-to-all-start = ((bf16[8,64,128]{2,1,0:T(8,128)(2,1)}), bf16[8,64,128]{2,1,0:T(8,128)(2,1)S(1)}, u32[]{:S(2)}, u32[]{:S(2)}) async-start(bf16[8,64,128]{2,1,0:T(8,128)(2,1)} %bitcast.132), calls=%async_computation | async-start | bytes 262144 | tf_op jit(solution)/shard_map/all_to_all | solution.py:146
  11.6 16.5 %copy-start.13 = (bf16[2,128]{1,0:T(2,128)(2,1)S(1)}, bf16[2,128]{1,0:T(2,128)(2,1)}, u32[]{:S(2)}) copy-start(bf16[2,128]{1,0:T(2,128)(2,1)} %param.31) | copy-start | bytes 1540
  11.6 16.5 %copy-start.3 = (bf16[2,1024,128]{2,1,0:T(8,128)(2,1)S(1)}, bf16[2,1024,128]{2,1,0:T(8,128)(2,1)}, u32[]{:S(2)}) copy-start(bf16[2,1024,128]{2,1,0:T(8,128)(2,1)} %param.30) | copy-start | bytes 1572868
  11.7 16.5 %copy-start.4 = (bf16[2,1024,128]{2,1,0:T(8,128)(2,1)S(1)}, bf16[2,1024,128]{2,1,0:T(8,128)(2,1)}, u32[]{:S(2)}) copy-start(bf16[2,1024,128]{2,1,0:T(8,128)(2,1)} %param.29) | copy-start | bytes 1572868
  11.7 33.2 %copy-start.14 = (s32[8]{0:T(128)S(1)}, s32[8]{0:T(128)}, u32[]{:S(2)}) copy-start(s32[8]{0:T(128)} %param.23) | copy-start | bytes 100
  11.7 33.2 %copy-start.1 = (bf16[512,128]{1,0:T(8,128)(2,1)S(1)}, bf16[512,128]{1,0:T(8,128)(2,1)}, u32[]{:S(2)}) copy-start(bf16[512,128]{1,0:T(8,128)(2,1)} %param.18) | copy-start | bytes 393220
  11.7 153.8 %all-to-all-start.1 = ((bf16[64,264,128]{2,1,0:T(8,128)(2,1)}), bf16[64,264,128]{2,1,0:T(8,128)(2,1)}, u32[]{:S(2)}, u32[]{:S(2)}) async-start(bf16[64,264,128]{2,1,0:T(8,128)(2,1)} %shard_map.136), calls=%async_computation.1 | async-start | bytes 8650752 | tf_op jit(solution)/shard_map/all_to_all | solution.py:124
  29.5 24.3 %collective-permute-start = (bf16[2,2056,128]{2,1,0:T(8,128)(2,1)S(1)}, bf16[2,2056,128]{2,1,0:T(8,128)(2,1)}, u32[]{:S(2)}, u32[]{:S(2)}) collective-permute-start(bf16[2,2056,128]{2,1,0:T(8,128)(2,1)S(1)} %get-tuple-element.24), channel_id=1, source_target_pairs={{0,1},{1,2},{2,3},{3,4},{4,5},{5,6},{6,7},{7,0},{8,9},{9,10},{10,1... | collective-permute-start | bytes 3158024 | tf_op jit(solution)/shard_map/ppermute | solution.py:176
  29.6 30.6 %collective-permute-start.1 = (bf16[2,2056,128]{2,1,0:T(8,128)(2,1)S(1)}, bf16[2,2056,128]{2,1,0:T(8,128)(2,1)}, u32[]{:S(2)}, u32[]{:S(2)}) collective-permute-start(bf16[2,2056,128]{2,1,0:T(8,128)(2,1)S(1)} %get-tuple-element.24), channel_id=1, source_target_pairs={{0,2},{1,3},{2,4},{3,5},{4,6},{5,7},{6,0},{7,1},{8,10},{9,11},{10,... | collective-permute-start | bytes 3158024 | tf_op jit(solution)/shard_map/ppermute | solution.py:176
  33.5 67.0 %collective-permute-start.2 = (bf16[2,2056,128]{2,1,0:T(8,128)(2,1)S(1)}, bf16[2,2056,128]{2,1,0:T(8,128)(2,1)}, u32[]{:S(2)}, u32[]{:S(2)}) collective-permute-start(bf16[2,2056,128]{2,1,0:T(8,128)(2,1)S(1)} %get-tuple-element.24), channel_id=1, source_target_pairs={{0,3},{1,4},{2,5},{3,6},{4,7},{5,0},{6,1},{7,2},{8,11},{9,12},{10,... | collective-permute-start | bytes 3158024 | tf_op jit(solution)/shard_map/ppermute | solution.py:176
  37.5 68.0 %collective-permute-start.3 = (bf16[2,2056,128]{2,1,0:T(8,128)(2,1)S(1)}, bf16[2,2056,128]{2,1,0:T(8,128)(2,1)}, u32[]{:S(2)}, u32[]{:S(2)}) collective-permute-start(bf16[2,2056,128]{2,1,0:T(8,128)(2,1)S(1)} %get-tuple-element.24), channel_id=1, source_target_pairs={{0,4},{1,5},{2,6},{3,7},{4,0},{5,1},{6,2},{7,3},{8,12},{9,13},{10,... | collective-permute-start | bytes 3158024 | tf_op jit(solution)/shard_map/ppermute | solution.py:176
  41.4 80.9 %collective-permute-start.4 = (bf16[2,2056,128]{2,1,0:T(8,128)(2,1)S(1)}, bf16[2,2056,128]{2,1,0:T(8,128)(2,1)S(1)}, u32[]{:S(2)}, u32[]{:S(2)}) collective-permute-start(bf16[2,2056,128]{2,1,0:T(8,128)(2,1)S(1)} %get-tuple-element.24), channel_id=1, source_target_pairs={{0,5},{1,6},{2,7},{3,0},{4,1},{5,2},{6,3},{7,4},{8,13},{9,14},{10,... | collective-permute-start | bytes 3158024 | tf_op jit(solution)/shard_map/ppermute | solution.py:176
  47.0 120.9 %copy-start.5 = (s32[128]{0:T(128)}, s32[128]{0:T(128)S(1)}, u32[]{:S(2)}) copy-start(s32[128]{0:T(128)S(1)} %eq.17) | copy-start | bytes 1540
  47.7 123.7 %copy-start.9 = (f32[512]{0:T(512)}, f32[512]{0:T(512)S(1)}, u32[]{:S(2)}) copy-start(f32[512]{0:T(512)S(1)} %convert_element_type.43) | copy-start | bytes 6148
  47.8 146.8 %copy-start.7 = (pred[8]{0:T(512)(128)(4,1)}, pred[8]{0:T(512)(128)(4,1)S(1)}, u32[]{:S(2)}) copy-start(pred[8]{0:T(512)(128)(4,1)S(1)} %compare_and_fusion) | copy-start | bytes 28
  53.9 69.6 %collective-permute-start.5 = (bf16[2,2056,128]{2,1,0:T(8,128)(2,1)S(1)}, bf16[2,2056,128]{2,1,0:T(8,128)(2,1)S(1)}, u32[]{:S(2)}, u32[]{:S(2)}) collective-permute-start(bf16[2,2056,128]{2,1,0:T(8,128)(2,1)S(1)} %get-tuple-element.24), channel_id=1, source_target_pairs={{0,6},{1,7},{2,0},{3,1},{4,2},{5,3},{6,4},{7,5},{8,14},{9,15},{10,... | collective-permute-start | bytes 3158024 | tf_op jit(solution)/shard_map/ppermute | solution.py:176
  60.2 67.7 %collective-permute-start.6 = (bf16[2,2056,128]{2,1,0:T(8,128)(2,1)S(1)}, bf16[2,2056,128]{2,1,0:T(8,128)(2,1)S(1)}, u32[]{:S(2)}, u32[]{:S(2)}) collective-permute-start(bf16[2,2056,128]{2,1,0:T(8,128)(2,1)S(1)} %get-tuple-element.24), channel_id=1, source_target_pairs={{0,7},{1,0},{2,1},{3,2},{4,3},{5,4},{6,5},{7,6},{8,15},{9,8},{10,9... | collective-permute-start | bytes 3158024 | tf_op jit(solution)/shard_map/ppermute | solution.py:176
  167.9 3.5 copy-start.12
  172.4 17.2 %all-to-all-start.2 = ((bf16[8,64,128]{2,1,0:T(8,128)(2,1)}), bf16[8,64,128]{2,1,0:T(8,128)(2,1)S(1)}, u32[]{:S(2)}, u32[]{:S(2)}) async-start(bf16[8,64,128]{2,1,0:T(8,128)(2,1)} %bitcast.15), calls=%async_computation.2 | async-start | bytes 262144 | tf_op jit(solution)/shard_map/all_to_all | solution.py:146
  211.0 7.5 %copy-start.2 = (bf16[8,64,128]{2,1,0:T(8,128)(2,1)S(1)}, bf16[8,64,128]{2,1,0:T(8,128)(2,1)}, u32[]{:S(2)}) copy-start(bf16[8,64,128]{2,1,0:T(8,128)(2,1)} %all_to_all.35) | copy-start | bytes 393220
  211.0 8.7 %copy-start.11 = (s32[8]{0:T(128)S(1)}, s32[8]{0:T(128)}, u32[]{:S(2)}) copy-start(s32[8]{0:T(128)} %param.22) | copy-start | bytes 100
  211.1 138.5 %all-to-all-start.4 = ((bf16[64,264,128]{2,1,0:T(8,128)(2,1)}), bf16[64,264,128]{2,1,0:T(8,128)(2,1)}, u32[]{:S(2)}, u32[]{:S(2)}) async-start(bf16[64,264,128]{2,1,0:T(8,128)(2,1)} %shard_map.137), calls=%async_computation.4 | async-start | bytes 8650752 | tf_op jit(solution)/shard_map/all_to_all | solution.py:124
  220.1 131.9 %copy-start.6 = (s32[128]{0:T(128)S(1)}, s32[128]{0:T(128)}, u32[]{:S(2)}) copy-start(s32[128]{0:T(128)} %copy-done.5) | copy-start | bytes 1540
  352.0 3.5 copy-start.10
  352.1 15.7 %copy-start.8 = (pred[8]{0:T(512)(128)(4,1)S(1)}, pred[8]{0:T(512)(128)(4,1)}, u32[]{:S(2)}) copy-start(pred[8]{0:T(512)(128)(4,1)} %copy-done.7) | copy-start | bytes 28

commit v13 on v9

--- a/solution.py
+++ b/solution.py
@@ -212,7 +212,7 @@
             out_tiles,
             destination,
             landing,
-            own_rows if layer_idx == 0 else None,
+            None,
         )
         if anchored is not None:
             own_rows = anchored

time: 380 us -> 375 us (0.987)
  starting transfers between devices: 76.7 us -> 69.2 us
  blocking collectives: 27.6 us -> 33.7 us
    all_to_all x2, waiting for transfers between devices: 166 us -> 157 us  [aggregate(): lax.all_to_all(payload, 'dom', split_axis=0, concat_axis=0, tiled=True)]
    all_to_all x2, starting transfers between devices: 15.5 us -> 7.41 us  [feat_to_rows(): lax.all_to_all(pieces, 'feat', split_axis=0, concat_axis=0, tiled=True)]
    all_to_all x1, blocking collectives: 9.85 us -> 16 us  [feat_to_rows(): lax.all_to_all(pieces, 'feat', split_axis=0, concat_axis=0, tiled=True)]
    all_to_all x2, waiting for transfers between devices: 5.4 us -> 9.37 us  [feat_to_rows(): lax.all_to_all(pieces, 'feat', split_axis=0, concat_axis=0, tiled=True)]
    unnamed x39 -> x29, local copies, waits for them, and re-layouts: 13.2 us -> 12.5 us
  transfers between devices with their start and end apart: 11 -> 11, of which waited for: 8 -> 9; matrix products, arithmetic and copies ran while one was open for 5% -> 6% of each run, Pallas kernels for 2% -> 0%
where the time goes in v13:
time: 375 us; the launch traced here: 374 us
  waiting for transfers between devices  214 us (57%)
  starting transfers between devices  69.2 us (18%)
  blocking collectives  33.7 us (9%)
  local copies, waits for them, and re-layouts  25.4 us (7%)
  matrix products  15 us (4%)
  Pallas kernels  13.7 us (4%)
    all_to_all x2, waiting for transfers between devices, aggregate(): lax.all_to_all(payload, 'dom', split_axis=0, concat_axis=0, tiled=True)  157 us
    ppermute x7, waiting for transfers between devices, gather_weights(): pieces.append(lax.ppermute(stacked, 'feat', pairs))  47.3 us
    ppermute x7, starting transfers between devices, gather_weights(): pieces.append(lax.ppermute(stacked, 'feat', pairs))  36.3 us
    all_to_all x2, starting transfers between devices, aggregate(): lax.all_to_all(payload, 'dom', split_axis=0, concat_axis=0, tiled=True)  25.5 us
    all_to_all x2, blocking collectives, rows_to_feat(): lax.all_to_all(pieces, 'feat', split_axis=0, concat_axis=0, tiled=True)  17.7 us
    all_to_all x1, blocking collectives, feat_to_rows(): lax.all_to_all(pieces, 'feat', split_axis=0, concat_axis=0, tiled=True)  16 us
    pallas_call x2, Pallas kernels, build_payload(): pl.pallas_call(payload_kernel, out_shape=jax.ShapeDtypeStruct((node_count...  13.7 us
    unnamed x29, local copies, waits for them, and re-layouts  12.5 us
  transfers between devices with their start and end apart: 11, of which 9 were waited for; matrix products, arithmetic and copies ran while one was open for 6% of the time, Pallas kernels for 0%

profile of v13, /device:TPU:40, one launch (start us, length us, event | category | flops | bytes accessed | tf_op | source)
XLA Modules:
  0.0 374.0 jit_solution(13812372841456043788)
XLA Ops:
  0.0 6.9 %shard_map.136 = bf16[64,264,128]{2,1,0:T(8,128)(2,1)} custom-call(s32[64]{0:T(128)} %bitcast.153, s32[64]{0:T(128)} %src_ref.3, s32[2]{0:T(128)} %hub_ref.3, bf16[64,128,128]{2,1,0:T(8,128)(2,1)} %tiles_ref.3, bf16[4,128,128]{2,1,0:T(8,128)(2,1)} %bitcast.9.blocks_ref), custom_call_target="tpu_custom_call" | custom-call | tf_op jit(solution)/shard_map/pallas_call | solution.py:69
  6.9 16.4 %all-to-all-start.1 = ((bf16[64,264,128]{2,1,0:T(8,128)(2,1)}), bf16[64,264,128]{2,1,0:T(8,128)(2,1)}, u32[]{:S(2)}, u32[]{:S(2)}) async-start(bf16[64,264,128]{2,1,0:T(8,128)(2,1)} %shard_map.136), calls=%async_computation.1 | async-start | bytes 8650752 | tf_op jit(solution)/shard_map/all_to_all | solution.py:114
  23.4 1.4 fusion.26
  24.8 3.4 collective-permute-start.1
  28.2 4.0 %collective-permute-start.2 = (bf16[2,2056,128]{2,1,0:T(8,128)(2,1)S(1)}, bf16[2,2056,128]{2,1,0:T(8,128)(2,1)}, u32[]{:S(2)}, u32[]{:S(2)}) collective-permute-start(bf16[2,2056,128]{2,1,0:T(8,128)(2,1)S(1)} %get-tuple-element.20), channel_id=1, source_target_pairs={{0,3},{1,4},{2,5},{3,6},{4,7},{5,0},{6,1},{7,2},{8,11},{9,12},{10,... | collective-permute-start | bytes 3158024 | tf_op jit(solution)/shard_map/ppermute | solution.py:166
  32.3 3.9 %collective-permute-start.3 = (bf16[2,2056,128]{2,1,0:T(8,128)(2,1)S(1)}, bf16[2,2056,128]{2,1,0:T(8,128)(2,1)}, u32[]{:S(2)}, u32[]{:S(2)}) collective-permute-start(bf16[2,2056,128]{2,1,0:T(8,128)(2,1)S(1)} %get-tuple-element.20), channel_id=1, source_target_pairs={{0,4},{1,5},{2,6},{3,7},{4,0},{5,1},{6,2},{7,3},{8,12},{9,13},{10,... | collective-permute-start | bytes 3158024 | tf_op jit(solution)/shard_map/ppermute | solution.py:166
  36.2 3.5 collective-permute-start.4
  39.7 1.5 gather_fusion
  41.2 0.3 convolution_bitcast_fusion.1
  41.6 0.2 copy.41
  41.8 0.1 copy.38
  41.9 0.1 eq.17
  42.1 0.4 fusion.41
  42.5 6.7 %collective-permute-done = bf16[2,2056,128]{2,1,0:T(8,128)(2,1)} collective-permute-done((bf16[2,2056,128]{2,1,0:T(8,128)(2,1)S(1)}, bf16[2,2056,128]{2,1,0:T(8,128)(2,1)}, u32[]{:S(2)}, u32[]{:S(2)}) %collective-permute-start) | collective-permute-done | bytes 1052704 | tf_op jit(solution)/shard_map/ppermute | solution.py:166
  49.1 3.4 collective-permute-start.5
  52.6 2.4 constant_dynamic-update-slice_fusion.6
  55.0 18.0 %collective-permute-start.6 = (bf16[2,2056,128]{2,1,0:T(8,128)(2,1)S(1)}, bf16[2,2056,128]{2,1,0:T(8,128)(2,1)S(1)}, u32[]{:S(2)}, u32[]{:S(2)}) collective-permute-start(bf16[2,2056,128]{2,1,0:T(8,128)(2,1)S(1)} %get-tuple-element.20), channel_id=1, source_target_pairs={{0,7},{1,0},{2,1},{3,2},{4,3},{5,4},{6,5},{7,6},{8,15},{9,8},{10,9... | collective-permute-start | bytes 3158024 | tf_op jit(solution)/shard_map/ppermute | solution.py:166
  73.0 2.4 constant_dynamic-update-slice_fusion.5
  75.4 19.9 %collective-permute-done.2 = bf16[2,2056,128]{2,1,0:T(8,128)(2,1)} collective-permute-done((bf16[2,2056,128]{2,1,0:T(8,128)(2,1)S(1)}, bf16[2,2056,128]{2,1,0:T(8,128)(2,1)}, u32[]{:S(2)}, u32[]{:S(2)}) %collective-permute-start.2) | collective-permute-done | bytes 1052704 | tf_op jit(solution)/shard_map/ppermute | solution.py:166
  95.2 2.3 constant_dynamic-update-slice_fusion.4
  97.6 2.7 collective-permute-done.3
  100.3 2.3 constant_dynamic-update-slice_fusion.3
  102.6 14.4 %collective-permute-done.4 = bf16[2,2056,128]{2,1,0:T(8,128)(2,1)S(1)} collective-permute-done((bf16[2,2056,128]{2,1,0:T(8,128)(2,1)S(1)}, bf16[2,2056,128]{2,1,0:T(8,128)(2,1)S(1)}, u32[]{:S(2)}, u32[]{:S(2)}) %collective-permute-start.4) | collective-permute-done | bytes 1052704 | tf_op jit(solution)/shard_map/ppermute | solution.py:166
  117.0 1.2 constant_dynamic-update-slice_fusion.2
  118.2 1.1 constant_dynamic-update-slice_fusion.1
  119.3 3.6 collective-permute-done.6
  122.9 1.1 constant_dynamic-update-slice_fusion
  124.0 31.0 %all-to-all-done.1 = bf16[64,264,128]{2,1,0:T(8,128)(2,1)} async-done(((bf16[64,264,128]{2,1,0:T(8,128)(2,1)}), bf16[64,264,128]{2,1,0:T(8,128)(2,1)}, u32[]{:S(2)}, u32[]{:S(2)}) %all-to-all-start.1) | async-done | bytes 4325408 | tf_op jit(solution)/shard_map/all_to_all | solution.py:114
  155.0 2.5 slice.81
  157.4 2.3 fusion.11
  159.8 0.1 copy.43
  159.9 0.9 slice.82
  160.9 0.2 fusion.24
  161.1 0.8 copy.44
  161.9 4.0 %all-to-all-start.2 = ((bf16[8,64,128]{2,1,0:T(8,128)(2,1)}), bf16[8,64,128]{2,1,0:T(8,128)(2,1)S(1)}, u32[]{:S(2)}, u32[]{:S(2)}) async-start(bf16[8,64,128]{2,1,0:T(8,128)(2,1)} %bitcast.16), calls=%async_computation.2 | async-start | bytes 262144 | tf_op jit(solution)/shard_map/all_to_all | solution.py:136
  165.9 0.7 slice_convert_fusion.1
  166.6 5.4 %all-to-all-done.2 = bf16[8,64,128]{2,1,0:T(8,128)(2,1)S(1)} async-done(((bf16[8,64,128]{2,1,0:T(8,128)(2,1)}), bf16[8,64,128]{2,1,0:T(8,128)(2,1)S(1)}, u32[]{:S(2)}, u32[]{:S(2)}) %all-to-all-start.2) | async-done | bytes 131104 | tf_op jit(solution)/shard_map/all_to_all | solution.py:136
  172.0 3.4 all-to-all-start
  175.4 2.1 fusion.7
  177.5 4.0 %all-to-all-done = bf16[8,64,128]{2,1,0:T(8,128)(2,1)S(1)} async-done(((bf16[8,64,128]{2,1,0:T(8,128)(2,1)}), bf16[8,64,128]{2,1,0:T(8,128)(2,1)S(1)}, u32[]{:S(2)}, u32[]{:S(2)}) %all-to-all-start) | async-done | bytes 131104 | tf_op jit(solution)/shard_map/all_to_all | solution.py:136
  181.5 2.2 multiply_reduce_fusion.1
  183.7 0.1 copy_bitcast_fusion.1
  183.8 0.6 gather_fusion.2
  184.4 9.2 %all_to_all.35 = bf16[8,64,128]{2,1,0:T(8,128)(2,1)} all-to-all(bf16[8,64,128]{2,1,0:T(8,128)(2,1)S(1)} %broadcast_select_fusion), channel_id=1, replica_groups=mesh['dom'=64,'feat'=8] {'feat'}, dimensions={0} | all-to-all | bytes 262144 | tf_op jit(solution)/shard_map/all_to_all | solution.py:144
  193.6 6.8 %shard_map.137 = bf16[64,264,128]{2,1,0:T(8,128)(2,1)} custom-call(s32[64]{0:T(128)} %bitcast.154, s32[64]{0:T(128)} %src_ref.3, s32[2]{0:T(128)} %hub_ref.3, bf16[64,128,128]{2,1,0:T(8,128)(2,1)} %tiles_ref.3, bf16[4,128,128]{2,1,0:T(8,128)(2,1)} %bitcast.143), custom_call_target="tpu_custom_call" | custom-call | tf_op jit(solution)/shard_map/pallas_call | solution.py:69
  200.4 9.1 %all-to-all-start.4 = ((bf16[64,264,128]{2,1,0:T(8,128)(2,1)}), bf16[64,264,128]{2,1,0:T(8,128)(2,1)}, u32[]{:S(2)}, u32[]{:S(2)}) async-start(bf16[64,264,128]{2,1,0:T(8,128)(2,1)} %shard_map.137), calls=%async_computation.4 | async-start | bytes 8650752 | tf_op jit(solution)/shard_map/all_to_all | solution.py:114
  209.5 0.6 gather_fusion.1
  210.1 0.3 convolution_bitcast_fusion
  210.5 0.2 copy.50
  210.7 0.4 fusion.39
  211.1 126.5 %all-to-all-done.4 = bf16[64,264,128]{2,1,0:T(8,128)(2,1)} async-done(((bf16[64,264,128]{2,1,0:T(8,128)(2,1)}), bf16[64,264,128]{2,1,0:T(8,128)(2,1)}, u32[]{:S(2)}, u32[]{:S(2)}) %all-to-all-start.4) | async-done | bytes 4325408 | tf_op jit(solution)/shard_map/all_to_all | solution.py:114
  337.5 2.5 slice.85
  340.0 2.3 fusion.14
  342.3 0.2 copy.51
  342.5 0.9 slice.86
  343.4 0.2 fusion.25
  343.6 0.1 copy.52
  343.8 16.0 %all_to_all.36 = bf16[8,64,128]{2,1,0:T(8,128)(2,1)S(1)} all-to-all(bf16[8,64,128]{2,1,0:T(8,128)(2,1)S(1)} %bitcast.146), channel_id=1, replica_groups=mesh['dom'=64,'feat'=8] {'feat'}, dimensions={0} | all-to-all | bytes 262144 | tf_op jit(solution)/shard_map/all_to_all | solution.py:136
  359.8 2.1 fusion.5
  361.8 2.2 multiply_reduce_fusion
  364.1 0.1 copy_bitcast_fusion
  364.2 0.6 gather_fusion.3
  364.9 8.5 %all_to_all.37 = bf16[8,64,128]{2,1,0:T(8,128)(2,1)S(1)} all-to-all(bf16[8,64,128]{2,1,0:T(8,128)(2,1)S(1)} %broadcast_select_fusion.1), channel_id=1, replica_groups=mesh['dom'=64,'feat'=8] {'feat'}, dimensions={0} | all-to-all | bytes 262144 | tf_op jit(solution)/shard_map/all_to_all | solution.py:144
  373.4 0.7 copy.104
  (34 shorter events, 0.3 us)
Async XLA Ops:
  0.0 41.2 %copy-start = (bf16[8,128,128]{2,1,0:T(8,128)(2,1)S(1)}, bf16[8,128,128]{2,1,0:T(8,128)(2,1)}, u32[]{:S(2)}) copy-start(bf16[8,128,128]{2,1,0:T(8,128)(2,1)} %param.24) | copy-start | bytes 786436
  6.9 16.5 %copy-start.8 = (bf16[2,128]{1,0:T(2,128)(2,1)S(1)}, bf16[2,128]{1,0:T(2,128)(2,1)}, u32[]{:S(2)}) copy-start(bf16[2,128]{1,0:T(2,128)(2,1)} %param.31) | copy-start | bytes 1540
  6.9 16.5 %copy-start.2 = (bf16[2,1024,128]{2,1,0:T(8,128)(2,1)S(1)}, bf16[2,1024,128]{2,1,0:T(8,128)(2,1)}, u32[]{:S(2)}) copy-start(bf16[2,1024,128]{2,1,0:T(8,128)(2,1)} %param.30) | copy-start | bytes 1572868
  6.9 16.5 %copy-start.3 = (bf16[2,1024,128]{2,1,0:T(8,128)(2,1)S(1)}, bf16[2,1024,128]{2,1,0:T(8,128)(2,1)}, u32[]{:S(2)}) copy-start(bf16[2,1024,128]{2,1,0:T(8,128)(2,1)} %param.29) | copy-start | bytes 1572868
  6.9 32.8 %copy-start.9 = (s32[8]{0:T(128)S(1)}, s32[8]{0:T(128)}, u32[]{:S(2)}) copy-start(s32[8]{0:T(128)} %param.23) | copy-start | bytes 100
  6.9 148.1 %all-to-all-start.1 = ((bf16[64,264,128]{2,1,0:T(8,128)(2,1)}), bf16[64,264,128]{2,1,0:T(8,128)(2,1)}, u32[]{:S(2)}, u32[]{:S(2)}) async-start(bf16[64,264,128]{2,1,0:T(8,128)(2,1)} %shard_map.136), calls=%async_computation.1 | async-start | bytes 8650752 | tf_op jit(solution)/shard_map/all_to_all | solution.py:114
  23.4 18.4 %copy-start.6 = (s32[1,64,2]{1,2,0:T(2,128)S(1)}, s32[1,64,2]{1,2,0:T(2,128)}, u32[]{:S(2)}) copy-start(s32[1,64,2]{1,2,0:T(2,128)} %param.28) | copy-start | bytes 1540
  23.4 18.7 %copy-start.4 = (s32[512]{0:T(512)S(1)}, s32[512]{0:T(512)}, u32[]{:S(2)}) copy-start(s32[512]{0:T(512)} %param.19) | copy-start | bytes 6148
  23.4 18.7 %copy-start.5 = (s32[8]{0:T(128)S(1)}, s32[8]{0:T(128)}, u32[]{:S(2)}) copy-start(s32[8]{0:T(128)} %param.22) | copy-start | bytes 100
  24.8 24.3 %collective-permute-start = (bf16[2,2056,128]{2,1,0:T(8,128)(2,1)S(1)}, bf16[2,2056,128]{2,1,0:T(8,128)(2,1)}, u32[]{:S(2)}, u32[]{:S(2)}) collective-permute-start(bf16[2,2056,128]{2,1,0:T(8,128)(2,1)S(1)} %get-tuple-element.20), channel_id=1, source_target_pairs={{0,1},{1,2},{2,3},{3,4},{4,5},{5,6},{6,7},{7,0},{8,9},{9,10},{10,1... | collective-permute-start | bytes 3158024 | tf_op jit(solution)/shard_map/ppermute | solution.py:166
  24.8 30.2 %collective-permute-start.1 = (bf16[2,2056,128]{2,1,0:T(8,128)(2,1)S(1)}, bf16[2,2056,128]{2,1,0:T(8,128)(2,1)}, u32[]{:S(2)}, u32[]{:S(2)}) collective-permute-start(bf16[2,2056,128]{2,1,0:T(8,128)(2,1)S(1)} %get-tuple-element.20), channel_id=1, source_target_pairs={{0,2},{1,3},{2,4},{3,5},{4,6},{5,7},{6,0},{7,1},{8,10},{9,11},{10,... | collective-permute-start | bytes 3158024 | tf_op jit(solution)/shard_map/ppermute | solution.py:166
  28.2 67.0 %collective-permute-start.2 = (bf16[2,2056,128]{2,1,0:T(8,128)(2,1)S(1)}, bf16[2,2056,128]{2,1,0:T(8,128)(2,1)}, u32[]{:S(2)}, u32[]{:S(2)}) collective-permute-start(bf16[2,2056,128]{2,1,0:T(8,128)(2,1)S(1)} %get-tuple-element.20), channel_id=1, source_target_pairs={{0,3},{1,4},{2,5},{3,6},{4,7},{5,0},{6,1},{7,2},{8,11},{9,12},{10,... | collective-permute-start | bytes 3158024 | tf_op jit(solution)/shard_map/ppermute | solution.py:166
  32.3 68.0 %collective-permute-start.3 = (bf16[2,2056,128]{2,1,0:T(8,128)(2,1)S(1)}, bf16[2,2056,128]{2,1,0:T(8,128)(2,1)}, u32[]{:S(2)}, u32[]{:S(2)}) collective-permute-start(bf16[2,2056,128]{2,1,0:T(8,128)(2,1)S(1)} %get-tuple-element.20), channel_id=1, source_target_pairs={{0,4},{1,5},{2,6},{3,7},{4,0},{5,1},{6,2},{7,3},{8,12},{9,13},{10,... | collective-permute-start | bytes 3158024 | tf_op jit(solution)/shard_map/ppermute | solution.py:166
  36.2 80.9 %collective-permute-start.4 = (bf16[2,2056,128]{2,1,0:T(8,128)(2,1)S(1)}, bf16[2,2056,128]{2,1,0:T(8,128)(2,1)S(1)}, u32[]{:S(2)}, u32[]{:S(2)}) collective-permute-start(bf16[2,2056,128]{2,1,0:T(8,128)(2,1)S(1)} %get-tuple-element.20), channel_id=1, source_target_pairs={{0,5},{1,6},{2,7},{3,0},{4,1},{5,2},{6,3},{7,4},{8,13},{9,14},{10,... | collective-permute-start | bytes 3158024 | tf_op jit(solution)/shard_map/ppermute | solution.py:166
  49.1 69.1 %collective-permute-start.5 = (bf16[2,2056,128]{2,1,0:T(8,128)(2,1)S(1)}, bf16[2,2056,128]{2,1,0:T(8,128)(2,1)S(1)}, u32[]{:S(2)}, u32[]{:S(2)}) collective-permute-start(bf16[2,2056,128]{2,1,0:T(8,128)(2,1)S(1)} %get-tuple-element.20), channel_id=1, source_target_pairs={{0,6},{1,7},{2,0},{3,1},{4,2},{5,3},{6,4},{7,5},{8,14},{9,15},{10,... | collective-permute-start | bytes 3158024 | tf_op jit(solution)/shard_map/ppermute | solution.py:166
  55.0 67.9 %collective-permute-start.6 = (bf16[2,2056,128]{2,1,0:T(8,128)(2,1)S(1)}, bf16[2,2056,128]{2,1,0:T(8,128)(2,1)S(1)}, u32[]{:S(2)}, u32[]{:S(2)}) collective-permute-start(bf16[2,2056,128]{2,1,0:T(8,128)(2,1)S(1)} %get-tuple-element.20), channel_id=1, source_target_pairs={{0,7},{1,0},{2,1},{3,2},{4,3},{5,4},{6,5},{7,6},{8,15},{9,8},{10,9... | collective-permute-start | bytes 3158024 | tf_op jit(solution)/shard_map/ppermute | solution.py:166
  157.4 3.4 copy-start.7
  161.9 10.2 %all-to-all-start.2 = ((bf16[8,64,128]{2,1,0:T(8,128)(2,1)}), bf16[8,64,128]{2,1,0:T(8,128)(2,1)S(1)}, u32[]{:S(2)}, u32[]{:S(2)}) async-start(bf16[8,64,128]{2,1,0:T(8,128)(2,1)} %bitcast.16), calls=%async_computation.2 | async-start | bytes 262144 | tf_op jit(solution)/shard_map/all_to_all | solution.py:136
  172.0 9.4 %all-to-all-start = ((bf16[8,64,128]{2,1,0:T(8,128)(2,1)}), bf16[8,64,128]{2,1,0:T(8,128)(2,1)S(1)}, u32[]{:S(2)}, u32[]{:S(2)}) async-start(bf16[8,64,128]{2,1,0:T(8,128)(2,1)} %bitcast.4), calls=%async_computation | async-start | bytes 262144 | tf_op jit(solution)/shard_map/all_to_all | solution.py:136
  200.4 9.1 %copy-start.1 = (bf16[8,64,128]{2,1,0:T(8,128)(2,1)S(1)}, bf16[8,64,128]{2,1,0:T(8,128)(2,1)}, u32[]{:S(2)}) copy-start(bf16[8,64,128]{2,1,0:T(8,128)(2,1)} %all_to_all.35) | copy-start | bytes 393220
  200.4 137.1 %all-to-all-start.4 = ((bf16[64,264,128]{2,1,0:T(8,128)(2,1)}), bf16[64,264,128]{2,1,0:T(8,128)(2,1)}, u32[]{:S(2)}, u32[]{:S(2)}) async-start(bf16[64,264,128]{2,1,0:T(8,128)(2,1)} %shard_map.137), calls=%async_computation.4 | async-start | bytes 8650752 | tf_op jit(solution)/shard_map/all_to_all | solution.py:114
